TPU v7x, 512 devices: a whole 4x8x8 slice. The times are simulated.
512 devices in a mesh: ind: 16 (over z, core), blk: 32 (over x, y).
Axes of the slice: x: 4, y: 8, z: 8, core: 2. Of those that a mesh axis runs over, the one named last changes fastest.
Arguments:
- genotypes: int32 [1024, 65536], P('ind', 'blk'), may hold values from 0 to 2, as said below
- block_units: int32 [64], replicated, may hold values from 4 to 32, as said below
- sketch_seed: int32 [1], replicated, may hold values from 0 to 999999
Outputs:
- basis: float32 [65536, 256], P(('blk', 'ind'))
Inputs may be any that keep to these rules, and one draw needn't show every extreme that they name: `block_units`: every block holds between 4 and 32 units; the units of all blocks sum to 512; one block holds exactly 32 and some hold exactly 4. `genotypes`: dosages are 0, 1 or 2.
All inputs are finite; a program needn't handle non-finite values.
Results may differ from a plain program's by a relative error of at most 0.0041.
Values sent between devices are 32-bit elements; how exact they have to be, the bound alone decides.
No kernel may reach another device: no remote copies, remote signals or barrier semaphores. Data moves between devices by JAX's collectives and lax.ppermute only.
A program may use at most 64 MiB of HBM per device.

v0:
```python
import math

import jax
import jax.numpy as jnp
from jax import lax
from jax.sharding import PartitionSpec as P

K = 256
UNIT = 128


SHRINKAGE = 0.25


def prefix(part, axis, combine, identity, reverse):
    count = lax.axis_size(axis)
    place = lax.axis_index(axis)
    ahead = count - 1 - place if reverse else place
    gathered = jax.tree.map(lambda a: lax.all_gather(a, axis), part)
    state = jax.tree.map(lambda a, e: jnp.zeros_like(a) + jnp.asarray(e, a.dtype), part, identity)

    def one(lap, state):
        source = count - 1 - lap if reverse else lap
        return combine(
            state, jax.tree.map(lambda a: lax.dynamic_index_in_dim(a, source, 0, False), gathered)
        )

    return lax.fori_loop(0, ahead, one, state)


def sketch_signs(columns, seed_value, lane_count):
    lane_ids = jnp.arange(lane_count, dtype=jnp.int32)
    hashed = columns[:, None] * lane_count + lane_ids[None, :]
    hashed = jnp.bitwise_xor(hashed, seed_value)
    hashed = hashed * 73244475
    hashed = jnp.bitwise_xor(hashed, jnp.right_shift(hashed, 16))
    hashed = hashed * 73244475
    hashed = jnp.bitwise_xor(hashed, jnp.right_shift(hashed, 16))
    parity = jnp.bitwise_and(jnp.right_shift(hashed, 5), 1)
    return (1 - 2 * parity).astype(jnp.float32)


def join_parts(earlier, later):
    return (later[0] + (1.0 - later[1]) * earlier[0], jnp.maximum(earlier[1], later[1]))


def link_blocks(stacked, first_block, last_block, col_base, col_span, block_starts, block_ends):
    offset = last_block - first_block
    head_part = stacked[0]
    tail_part = lax.dynamic_index_in_dim(stacked, offset, 0, keepdims=False)
    opens_tail = (block_starts[last_block] >= col_base).astype(jnp.float32)
    closes_head = (block_ends[first_block] <= col_base + col_span).astype(jnp.float32)
    blank_pair = (jnp.zeros_like(head_part), jnp.zeros((), jnp.float32))
    from_lower = prefix((tail_part, opens_tail), "blk", join_parts, blank_pair, False)
    from_upper = prefix((head_part, closes_head), "blk", join_parts, blank_pair, True)
    head_open = block_starts[first_block] < col_base
    tail_open = block_ends[last_block] > col_base + col_span
    slot_ids = jnp.arange(stacked.shape[0], dtype=jnp.int32)
    extra_shape = (stacked.shape[0],) + (1,) * (stacked.ndim - 1)
    head_mask = jnp.logical_and(slot_ids == 0, head_open).reshape(extra_shape)
    tail_mask = jnp.logical_and(slot_ids == offset, tail_open).reshape(extra_shape)
    stacked = stacked + jnp.where(head_mask, from_lower[0][None], 0.0)
    stacked = stacked + jnp.where(tail_mask, from_upper[0][None], 0.0)
    return stacked


def slot_grams(rows_now, slots_now, slot_total):
    row_count, lane_count = rows_now.shape
    tile_size = math.gcd(row_count, UNIT)
    row_tiles = rows_now.reshape(row_count // tile_size, tile_size, lane_count)
    tile_slot = slots_now[::tile_size]
    outer_sums = jnp.einsum(
        "tgk,tgl->tkl",
        row_tiles,
        row_tiles,
        precision=lax.Precision.HIGHEST,
        preferred_element_type=jnp.float32,
    )
    selector = (tile_slot[None, :] == jnp.arange(slot_total, dtype=jnp.int32)[:, None]).astype(
        jnp.float32
    )
    return jnp.einsum(
        "st,tkl->skl",
        selector,
        outer_sums,
        precision=lax.Precision.HIGHEST,
        preferred_element_type=jnp.float32,
    )


def solve_rows(rows_now, slots_now, factor):
    row_count, lane_count = rows_now.shape
    tile_size = math.gcd(row_count, UNIT)
    row_tiles = rows_now.reshape(row_count // tile_size, tile_size, lane_count)
    tile_factor = jnp.take(factor, slots_now[::tile_size], axis=0)

    def solve_one(lower_factor, block_rows):
        return jax.scipy.linalg.solve_triangular(lower_factor, block_rows.T, lower=True).T

    return jax.vmap(solve_one)(tile_factor, row_tiles).reshape(row_count, lane_count)


def on_device(genotypes, block_units, sketch_seed):
    ind_count = lax.axis_size("ind")
    people, col_span = genotypes.shape
    row_slice = col_span // ind_count
    blk_index = lax.axis_index("blk")
    ind_index = lax.axis_index("ind")
    dosage = genotypes.astype(jnp.float32)
    col_sums, col_squares = lax.psum((jnp.sum(dosage, 0), jnp.sum(dosage * dosage, 0)), "ind")
    everyone = people * ind_count
    average = col_sums / everyone
    spread_sq = col_squares / everyone - average * average
    standard = ((dosage - average) * lax.rsqrt(spread_sq + 1e-05)).astype(jnp.bfloat16)
    widths = block_units * UNIT
    block_ends = jnp.cumsum(widths, dtype=jnp.int32)
    block_starts = block_ends - widths
    col_base = blk_index * col_span
    columns = col_base + jnp.arange(col_span, dtype=jnp.int32)
    block_of = jnp.sum((columns[:, None] >= block_starts[None, :]).astype(jnp.int32), axis=1) - 1
    first_block = block_of[0]
    last_block = block_of[col_span - 1]
    slot_of = block_of - first_block
    slot_total = (col_span // UNIT - 1) // 4 + 2
    sign_rows = sketch_signs(columns, sketch_seed[0], K).astype(jnp.bfloat16)
    tile_total = col_span // UNIT
    tile_slot = slot_of[::UNIT]

    def add_tile(tile_id, running):
        pieces = lax.dynamic_slice_in_dim(standard, tile_id * UNIT, UNIT, 1)
        sign_piece = lax.dynamic_slice_in_dim(sign_rows, tile_id * UNIT, UNIT, 0)
        return running.at[tile_slot[tile_id]].add(
            jnp.dot(pieces, sign_piece, preferred_element_type=jnp.float32)
        )

    sketch_parts = lax.fori_loop(
        0, tile_total, add_tile, jnp.zeros((slot_total, people, K), jnp.float32)
    )
    sketch_parts = link_blocks(
        sketch_parts, first_block, last_block, col_base, col_span, block_starts, block_ends
    )
    sketch = sketch_parts.astype(jnp.bfloat16)
    row_scale = (1.0 - SHRINKAGE) / everyone
    row_start = ind_index * row_slice
    my_slots = lax.dynamic_slice_in_dim(slot_of, row_start, row_slice, 0)
    tile_size = math.gcd(row_slice * lax.axis_size("ind"), UNIT)
    tile_count = row_slice * lax.axis_size("ind") // tile_size
    pieces = standard.reshape(people, tile_count, tile_size)
    starts = jnp.arange(tile_count, dtype=jnp.int32) * tile_size
    chosen = jnp.take(sketch, jnp.take(slot_of, starts), axis=0)
    product = jnp.einsum("ntg,tnk->tgk", pieces, chosen, preferred_element_type=jnp.float32)
    projected = lax.psum_scatter(
        product.reshape(row_slice * lax.axis_size("ind"), K) * row_scale,
        "ind",
        scatter_dimension=0,
        tiled=True,
    )
    my_signs = lax.dynamic_slice_in_dim(sign_rows, row_start, row_slice, 0).astype(jnp.float32)
    projected = projected + SHRINKAGE * my_signs
    gram_parts = lax.psum(slot_grams(projected, my_slots, slot_total), "ind")
    gram_parts = link_blocks(
        gram_parts, first_block, last_block, col_base, col_span, block_starts, block_ends
    )
    slot_ids = jnp.arange(slot_total, dtype=jnp.int32)
    block_ids = jnp.minimum(first_block + slot_ids, block_units.shape[0] - 1)
    slot_widths = (jnp.take(block_units, block_ids) * UNIT).astype(jnp.float32)
    slot_valid = slot_ids <= last_block - first_block
    identity_mat = jnp.eye(K, dtype=jnp.float32)
    gram_blocks = gram_parts / slot_widths[:, None, None]
    gram_blocks = jnp.where(slot_valid[:, None, None], gram_blocks, identity_mat[None])
    factor = jnp.linalg.cholesky(gram_blocks)
    return solve_rows(projected, my_slots, factor)


def solution(mesh):
    return jax.shard_map(
        on_device,
        mesh=mesh,
        in_specs=(P("ind", "blk"), P(), P()),
        out_specs=P(("blk", "ind"), None),
        check_vma=False,
    )
```

profile of v0, /device:TPU:6, one launch (start us, length us, event | category | flops | bytes accessed | tf_op | source)
XLA Modules:
  0.0 1021.4 jit_solution(7402001263264046166)
XLA Ops:
  9.7 1.2 convert_reduce_fusion
  12.7 54.0 %all-reduce.4 = (f32[2048]{0:T(1024)S(1)}, f32[2048]{0:T(1024)S(1)}) all-reduce(f32[2048]{0:T(1024)S(1)} %get-tuple-element.458, f32[2048]{0:T(1024)S(1)} %get-tuple-element.457), channel_id=1, replica_groups=mesh['ind'=16,'blk'=32] {'ind'}, use_global_device_ids=true, to_apply=%region_5.6 | all-reduce | flops 4096 | bytes 32768 | tf_op jit(solution)/shard_map/psum | solution.py:110
  66.7 1.1 multiply_convert_fusion
  68.9 64.9 %while.68 = (s32[]{:T(128)}, f32[5,64,256]{2,1,0:T(8,128)S(1)}, s32[16]{0:T(128)S(1)}, bf16[64,2048]{1,0:T(8,128)(2,1)S(1)}, bf16[2048,256]{0,1:T(8,128)(2,1)S(1...) while((s32[]{:T(128)}, f32[5,64,256]{2,1,0:T(8,128)S(1)}, ...), condition=%wide.region_8.9_spmd, body=%wide.region_6.8_spmd.sunk | while | flops 4227098 | bytes 214259 | solution.py:136
  143.3 1.3 dynamic-slice.28
  146.1 63.8 %all-reduce.3 = (f32[32]{0:T(128)S(1)}, f32[32]{0:T(128)S(1)}) all-reduce(f32[32]{0:T(128)S(1)} %dynamic-update-slice.20, f32[32]{0:T(128)S(1)} %dynamic-update-slice.19), channel_id=1, replica_groups=mesh['ind'=16,'blk'=32] {'blk'}, use_global_device_ids=true, to_apply=%add.2 | all-reduce | flops 64 | bytes 512
  210.5 1.9 all-gather.7.cloned.1.call-done
  212.5 15.5 %while.70 = (s32[]{:T(128)}, f32[64,256]{1,0:T(8,128)S(1)}, s32[]{:T(128)}, f32[32,64,256]{2,1,0:T(8,128)}, f32[32]{0:T(128)S(1)}, /*index=5*/s32[]{:T(128)}, s32[]{:T(128)}, s32[]{:T(128)}, s32[]{:T(128)}, f32[1]{0:T(128)}) while((s32[]{:T(128)}, f32[64,256]{1,0:T(8,128)S(1)}, s32[]{:T(128)}, f32[32,64,256]{2,1,0:T(8,128)}, ...), condition=%wide.region_12.13_spmd, body=%wide.region_11.12_spmd.sunk | while | flops 32775 | bytes 196795 | solution.py:28
  228.0 68.4 %all-gather.5.cloned.1.call-done = f32[32,64,256]{2,1,0:T(8,128)} async-done(((f32[1,64,256]{2,1,0:T(8,128)}), f32[32,64,256]{2,1,0:T(8,128)}) %all-gather.5.cloned.1.call-update) | async-done | bytes 2097168 | tf_op jit(solution)/shard_map/all_gather | solution.py:19
  296.4 50.9 %while.69 = (s32[]{:T(128)}, f32[64,256]{1,0:T(8,128)S(1)}, s32[]{:T(128)}, f32[32,64,256]{2,1,0:T(8,128)}, f32[32]{0:T(128)S(1)}, /*index=5*/s32[]{:T(128)}, s32[]{:T(128)}, s32[]{:T(128)}, f32[1]{0:T(128)}) while((s32[]{:T(128)}, f32[64,256]{1,0:T(8,128)S(1)}, s32[]{:T(128)}, f32[32,64,256]{2,1,0:T(8,128)}, f32[32]{0:T(128)S(1)}, ...), condition=%wide.region_10.11_spmd, body=%wide.region_9.10_spmd.sunk | while | flops 32774 | bytes 196775 | solution.py:28
  348.6 1.2 convolution_multiply_fusion
  349.8 1.9 copy.58
  351.8 75.8 %reduce-scatter.2.cloned.1.call-done = f32[128,256]{0,1:T(8,128)} async-done(((f32[2048,256]{0,1:T(8,128)}), f32[128,256]{0,1:T(8,128)}) %reduce-scatter.2.cloned.1.call-update) | async-done | bytes 131088 | tf_op jit(solution)/shard_map/reduce_scatter | solution.py:152
  427.7 1.4 fusion.29
  429.1 1.3 broadcast_multiply_fusion
  430.4 117.3 %all-reduce.7.cloned.1.call-done = f32[5,256,256]{1,2,0:T(8,128)} async-done(((f32[5,256,256]{1,2,0:T(8,128)}), f32[5,256,256]{1,2,0:T(8,128)}) %all-reduce.7.cloned.1.call-update) | async-done | bytes 1310736 | tf_op jit(solution)/shard_map/psum | solution.py:160
  547.7 1.1 constant_dynamic-slice_fusion.2
  554.4 1.2 multiply_convert_fusion.1
  556.5 95.0 %all-gather.11.cloned.1.call-done = f32[32,256,256]{2,1,0:T(8,128)} async-done(((f32[1,256,256]{2,1,0:T(8,128)}), f32[32,256,256]{2,1,0:T(8,128)}) %all-gather.11.cloned.1.call-update) | async-done | bytes 8388624 | tf_op jit(solution)/shard_map/all_gather | solution.py:19
  651.6 16.2 %while.72 = (s32[]{:T(128)}, f32[256,256]{1,0:T(8,128)S(1)}, s32[]{:T(128)}, f32[32,256,256]{2,1,0:T(8,128)}, f32[32]{0:T(128)S(1)}, /*index=5*/s32[]{:T(128)}, s32[]{:T(128)}, s32[]{:T(128)}, s32[]{:T(128)}, f32[1]{0:T(128)}) while((s32[]{:T(128)}, f32[256,256]{1,0:T(8,128)S(1)}, s32[]{:T(128)}, f32[32,256,256]{2,1,0:T(8,128)}, ...), condition=%wide.region_18.19_spmd, body=%wide.region_17.18_spmd.sunk | while | flops 131079 | bytes 786619 | solution.py:28
  652.8 1.0 bitcast_add_fusion.12
  655.2 1.0 bitcast_add_fusion.12
  657.5 1.0 bitcast_add_fusion.12
  659.8 1.0 bitcast_add_fusion.12
  662.1 1.0 bitcast_add_fusion.12
  664.4 1.0 bitcast_add_fusion.12
  666.7 1.0 bitcast_add_fusion.12
  667.9 87.1 %all-gather.9.cloned.1.call-done = f32[32,256,256]{2,1,0:T(8,128)} async-done(((f32[1,256,256]{2,1,0:T(8,128)}), f32[32,256,256]{2,1,0:T(8,128)}) %all-gather.9.cloned.1.call-update) | async-done | bytes 8388624 | tf_op jit(solution)/shard_map/all_gather | solution.py:19
  755.1 55.6 %while.71 = (s32[]{:T(128)}, f32[256,256]{1,0:T(8,128)S(1)}, s32[]{:T(128)}, f32[32,256,256]{2,1,0:T(8,128)}, f32[32]{0:T(128)S(1)}, /*index=5*/s32[]{:T(128)}, s32[]{:T(128)}, s32[]{:T(128)}, f32[1]{0:T(128)}) while((s32[]{:T(128)}, f32[256,256]{1,0:T(8,128)S(1)}, s32[]{:T(128)}, f32[32,256,256]{2,1,0:T(8,128)}, f32[32]{0:T(128)S(1)}, ...), condition=%wide.region_16.17_spmd, body=%wide.region_15.16_spmd.sunk | while | flops 131078 | bytes 786599 | solution.py:28
  756.4 1.0 bitcast_add_fusion.11
  758.7 1.0 bitcast_add_fusion.11
  761.0 1.0 bitcast_add_fusion.11
  763.3 1.0 bitcast_add_fusion.11
  765.6 1.0 bitcast_add_fusion.11
  767.9 1.0 bitcast_add_fusion.11
  770.3 1.0 bitcast_add_fusion.11
  772.6 1.0 bitcast_add_fusion.11
  774.9 1.0 bitcast_add_fusion.11
  777.2 1.0 bitcast_add_fusion.11
  779.5 1.0 bitcast_add_fusion.11
  781.8 1.0 bitcast_add_fusion.11
  784.2 1.0 bitcast_add_fusion.11
  786.5 1.0 bitcast_add_fusion.11
  788.8 1.0 bitcast_add_fusion.11
  791.1 1.0 bitcast_add_fusion.11
  793.4 1.0 bitcast_add_fusion.11
  795.7 1.0 bitcast_add_fusion.11
  798.1 1.0 bitcast_add_fusion.11
  800.4 1.0 bitcast_add_fusion.11
  802.7 1.0 bitcast_add_fusion.11
  805.0 1.0 bitcast_add_fusion.11
  807.3 1.0 bitcast_add_fusion.11
  809.6 1.0 bitcast_add_fusion.11
  810.8 1.0 divide_select_fusion
  811.8 1.5 copy.64
  813.3 1.7 fusion.13
  815.1 58.8 %custom-call.17 = f32[5,128,128]{2,1,0:T(8,128)S(1)} custom-call(f32[5,128,128]{2,1,0:T(8,128)S(1)} %cholesky.119), custom_call_target="Cholesky" | custom-call | tf_op jit(solution)/shard_map/jit(cholesky)/cholesky | solution.py:171
  874.1 49.1 %custom-call.18 = f32[5,1,128,128]{2,3,1,0:T(8,128)S(1)} custom-call(f32[5,1,128,128]{3,2,1,0:T(8,128)S(1)} %select_bitcast_fusion), custom_call_target="InvertDiagBlocksLowerTriangular" | custom-call | tf_op jit(solution)/shard_map/jit(cholesky)/cholesky | solution.py:171
  923.9 1.5 convolution_subtract_fusion
  925.4 59.4 %custom-call.19 = f32[5,128,128]{2,1,0:T(8,128)S(1)} custom-call(f32[5,128,128]{2,1,0:T(8,128)} %convolution_subtract_fusion), custom_call_target="Cholesky" | custom-call | tf_op jit(solution)/shard_map/jit(cholesky)/cholesky | solution.py:171
  987.0 5.4 while.73
  987.7 1.3 constant_dynamic-slice_fusion.9
  990.4 1.3 constant_dynamic-slice_fusion.9
  992.4 20.5 %custom-call.20 = f32[1,2,128,128]{2,3,1,0:T(8,128)S(1)} custom-call(f32[1,2,128,128]{3,2,1,0:T(8,128)} %bitcast.142), custom_call_target="InvertDiagBlocksLowerTriangular" | custom-call | tf_op jit(solution)/shard_map/vmap(jit(_solve_triangular))/triangular_solve | solution.py:98
  (266 shorter events, 123.4 us)
Async XLA Ops:
  6.5 205.9 %all-gather.7.cloned.1.call-start = ((), (), s32[]{:S(2)}) async-start(), calls=%async_computation.2 | async-start | bytes 2162688 | tf_op jit(solution)/shard_map/all_gather | solution.py:19
  9.6 59.2 %copy-start.8 = (s32[3]{0:T(128)S(1)}, s32[3]{0:T(128)}, u32[]{:S(2)}) copy-start(s32[3]{0:T(128)} %constant.349.clone.1) | copy-start | bytes 40
  66.7 1.1 copy-start.6
  133.8 78.7 %copy-start.3 = (bf16[2048,256]{0,1:T(8,128)(2,1)}, bf16[2048,256]{0,1:T(8,128)(2,1)S(1)}, u32[]{:S(2)}) copy-start(bf16[2048,256]{0,1:T(8,128)(2,1)S(1)} %get-tuple-element.903) | copy-start | bytes 3145732
  134.5 161.9 %all-gather.5.cloned.1.call-start = ((), (), s32[]{:S(2)}) async-start(), calls=%async_computation.1 | async-start | bytes 2162688 | tf_op jit(solution)/shard_map/all_gather | solution.py:19
  135.3 292.4 %reduce-scatter.2.cloned.1.call-start = ((), (), s32[]{:S(2)}) async-start(), calls=%async_computation.3 | async-start | bytes 2228224 | tf_op jit(solution)/shard_map/reduce_scatter | solution.py:152
  209.9 137.5 %copy-start.9 = (pred[5]{0:T(512)(128)(4,1)}, pred[5]{0:T(512)(128)(4,1)S(1)}, u32[]{:S(2)}) copy-start(pred[5]{0:T(512)(128)(4,1)S(1)} %compare_and_fusion) | copy-start | bytes 19
  209.9 137.5 %copy-start.10 = (pred[5]{0:T(512)(128)(4,1)}, pred[5]{0:T(512)(128)(4,1)S(1)}, u32[]{:S(2)}) copy-start(pred[5]{0:T(512)(128)(4,1)S(1)} %compare_and_fusion.1) | copy-start | bytes 19
  228.0 119.5 %copy-start.13 = (f32[32]{0:T(128)}, f32[32]{0:T(128)S(1)}, u32[]{:S(2)}) copy-start(f32[32]{0:T(128)S(1)} %get-tuple-element.919) | copy-start | bytes 388
  296.4 52.1 %copy-start.2 = (s32[64,2048]{1,0:T(8,128)S(1)}, s32[64,2048]{1,0:T(8,128)}, u32[]{:S(2)}) copy-start(s32[64,2048]{1,0:T(8,128)} %param.15) | copy-start | bytes 1572868
  347.4 0.6 copy-start.11
  351.7 196.0 %all-reduce.7.cloned.1.call-start = ((), (), s32[]{:S(2)}) async-start(), calls=%async_computation.4 | async-start | bytes 2621440 | tf_op jit(solution)/shard_map/psum | solution.py:160
  430.4 120.9 %copy-start = (s32[64]{0:T(128)S(1)}, s32[64]{0:T(128)}, u32[]{:S(2)}) copy-start(s32[64]{0:T(128)} %param.16) | copy-start | bytes 772
  430.4 221.1 %all-gather.11.cloned.1.call-start = ((), (), s32[]{:S(2)}) async-start(), calls=%async_computation.6 | async-start | bytes 8650752 | tf_op jit(solution)/shard_map/all_gather | solution.py:19
  548.8 6.9 copy-start.4
  549.6 101.9 %copy-start.14 = (f32[32]{0:T(128)S(1)}, f32[32]{0:T(128)}, u32[]{:S(2)}) copy-start(f32[32]{0:T(128)} %copy-done.13) | copy-start | bytes 388
  549.7 205.4 %all-gather.9.cloned.1.call-start = ((), (), s32[]{:S(2)}) async-start(), calls=%async_computation.5 | async-start | bytes 8650752 | tf_op jit(solution)/shard_map/all_gather | solution.py:19
  651.6 103.5 %copy-start.12 = (f32[32]{0:T(128)S(1)}, f32[32]{0:T(128)}, u32[]{:S(2)}) copy-start(f32[32]{0:T(128)} %copy-done.11) | copy-start | bytes 388
  755.1 55.8 %copy-start.1 = (f32[5,256,256]{1,2,0:T(8,128)S(1)}, f32[5,256,256]{1,2,0:T(8,128)}, u32[]{:S(2)}) copy-start(f32[5,256,256]{1,2,0:T(8,128)} %all-reduce.7.cloned.1.call-done) | copy-start | bytes 3932164
  815.1 59.0 %copy-start.7 = (pred[128,128]{1,0:T(8,128)(4,1)S(1)}, pred[128,128]{1,0:T(8,128)(4,1)}, u32[]{:S(2)}) copy-start(pred[128,128]{1,0:T(8,128)(4,1)} %iota_compare_fusion.3) | copy-start | bytes 49156
  985.3 0.9 copy-start.5
  985.5 1.5 copy-start.15
Sparse Core Ops, SparseCore 0:
  134.6 77.7 all-gather.6
  215.6 80.7 all-gather.4
  351.8 75.8 reduce-scatter.1
  430.5 117.1 all-reduce.6
  550.7 100.7 all-gather.10
  654.6 100.4 all-gather.8
where the time goes:
time: 1040 us; the launch traced here: 1020 us
  waiting for transfers between devices  446 us (43%)
  other arithmetic  275 us (26%)
  blocking collectives  118 us (11%)
  loops' own time  72.2 us (7%)
  local copies, waits for them, and re-layouts  69.4 us (7%)
  between operations  22.1 us (2%)
  matrix products  18 us (2%)
    all_gather x4, waiting for transfers between devices, prefix(): gathered = jax.tree.map(lambda a: lax.all_gather(a, axis), part)  252 us
    another operation x10, other arithmetic, on_device(): factor = jnp.linalg.cholesky(gram_blocks)  168 us
    psum x1, waiting for transfers between devices, on_device(): gram_parts = lax.psum(slot_grams(projected, my_slots, slot_total), 'ind')  117 us
    reduce_scatter x1, waiting for transfers between devices, on_device(): lax.psum_scatter(product.reshape(row_slice * lax.axis_size('ind'), K) * r...  75.8 us
    unnamed x1, blocking collectives  63.8 us
    add x62, other arithmetic, join_parts(): later[0] + (1.0 - later[1]) * earlier[0]  59.2 us
    psum x1, blocking collectives, on_device(): lax.psum((jnp.sum(dosage, 0), jnp.sum(dosage * dosage, 0)), 'ind')  54 us
    another operation x4, loops' own time, prefix(): return lax.fori_loop(0, ahead, one, state)  41.6 us
  transfers between devices with their start and end apart: 6, of which 6 were waited for; matrix products, arithmetic and copies ran while one was open for 3% of the time, Pallas kernels for 0%

commit v1 on v0

v1 whole, which is shorter than its diff:
```python
import math

import jax
import jax.numpy as jnp
from jax import lax
from jax.sharding import PartitionSpec as P

K = 256
UNIT = 128
MAX_UNITS = 32
MIN_UNITS = 4

SHRINKAGE = 0.25


def sketch_signs(columns, seed_value, lane_count):
    lane_ids = jnp.arange(lane_count, dtype=jnp.int32)
    hashed = columns[:, None] * lane_count + lane_ids[None, :]
    hashed = jnp.bitwise_xor(hashed, seed_value)
    hashed = hashed * 73244475
    hashed = jnp.bitwise_xor(hashed, jnp.right_shift(hashed, 16))
    hashed = hashed * 73244475
    hashed = jnp.bitwise_xor(hashed, jnp.right_shift(hashed, 16))
    parity = jnp.bitwise_and(jnp.right_shift(hashed, 5), 1)
    return (1 - 2 * parity).astype(jnp.float32)


def xor_allreduce(x, axis, count):
    mask = 1
    while mask < count:
        x = x + lax.ppermute(x, axis, [(j, j ^ mask) for j in range(count)])
        mask *= 2
    return x


def halving_allreduce(x, axis, count):
    place = lax.axis_index(axis)
    masks = []
    mask = 1
    while mask < count:
        masks.append(mask)
        mask *= 2
    for mask in masks:
        half = x.shape[0] // 2
        lower, upper = x[:half], x[half:]
        high = (place & mask) != 0
        send = jnp.where(high, lower, upper)
        keep = jnp.where(high, upper, lower)
        x = keep + lax.ppermute(send, axis, [(j, j ^ mask) for j in range(count)])
    for mask in reversed(masks):
        got = lax.ppermute(x, axis, [(j, j ^ mask) for j in range(count)])
        high = (place & mask) != 0
        x = jnp.where(high, jnp.concatenate([got, x], 0), jnp.concatenate([x, got], 0))
    return x


def shift(x, axis, count, step):
    pairs = [(j, j + step) for j in range(count) if 0 <= j + step < count]
    return lax.ppermute(x, axis, pairs)


def block_of(col, block_starts):
    return jnp.sum((col[..., None] >= block_starts).astype(jnp.int32), axis=-1) - 1


def halo(head_part, tail_part, blk_index, blk_count, reach, edge_blocks, first_block, last_block):
    from_lower = []
    from_upper = []
    for step in range(1, reach + 1):
        got_tail = shift(tail_part, "blk", blk_count, step)
        got_head = shift(head_part, "blk", blk_count, -step)
        lower = blk_index - step
        upper = blk_index + step
        lower_ok = jnp.logical_and(
            lower >= 0, edge_blocks[jnp.clip(lower, 0, blk_count - 1), 1] == first_block
        )
        upper_ok = jnp.logical_and(
            upper < blk_count, edge_blocks[jnp.clip(upper, 0, blk_count - 1), 0] == last_block
        )
        from_lower.append(jnp.where(lower_ok, got_tail, 0.0))
        from_upper.append(jnp.where(upper_ok, got_head, 0.0))
    return sum(from_lower[1:], from_lower[0]), sum(from_upper[1:], from_upper[0])


def on_device(genotypes, block_units, sketch_seed):
    ind_count = lax.axis_size("ind")
    blk_count = lax.axis_size("blk")
    people, col_span = genotypes.shape
    everyone = people * ind_count
    row_slice = col_span // ind_count
    unit_count = col_span // UNIT
    slot_total = (unit_count - 1) // MIN_UNITS + 2
    reach = min(-(-(MAX_UNITS - 1) // unit_count), blk_count - 1)
    blk_index = lax.axis_index("blk")
    ind_index = lax.axis_index("ind")

    dosage = genotypes.astype(jnp.float32)
    stats = xor_allreduce(jnp.stack([jnp.sum(dosage, 0), jnp.sum(dosage * dosage, 0)]), "ind", ind_count)
    average = stats[0] / everyone
    spread_sq = stats[1] / everyone - average * average
    standard = ((dosage - average) * lax.rsqrt(spread_sq + 1e-05)).astype(jnp.bfloat16)

    widths = block_units * UNIT
    block_ends = jnp.cumsum(widths, dtype=jnp.int32)
    block_starts = block_ends - widths
    col_base = blk_index * col_span
    unit_cols = col_base + jnp.arange(unit_count, dtype=jnp.int32) * UNIT
    unit_block = block_of(unit_cols, block_starts)
    first_block = unit_block[0]
    last_block = unit_block[unit_count - 1]
    unit_slot = unit_block - first_block
    group_bases = jnp.arange(blk_count, dtype=jnp.int32) * col_span
    edge_blocks = jnp.stack(
        [block_of(group_bases, block_starts), block_of(group_bases + col_span - 1, block_starts)], 1
    )
    last_slot = last_block - first_block

    columns = col_base + jnp.arange(col_span, dtype=jnp.int32)
    signs = sketch_signs(columns, sketch_seed[0], K)
    slot_ids = jnp.arange(slot_total, dtype=jnp.int32)
    col_slot = jnp.repeat(unit_slot, UNIT)
    col_mask = col_slot[None, :] == slot_ids[:, None]
    masked_std = jnp.where(col_mask[:, None, :], standard[None], jnp.zeros((), jnp.bfloat16))

    parts = jnp.einsum(
        "snc,ck->snk", masked_std, signs.astype(jnp.bfloat16), preferred_element_type=jnp.float32
    )
    head_in, tail_in = halo(
        parts[0], parts[last_slot], blk_index, blk_count, reach, edge_blocks, first_block, last_block
    )
    parts = parts.at[0].add(head_in)
    parts = parts.at[last_slot].add(tail_in)
    sketch = parts.astype(jnp.bfloat16)

    product = jnp.einsum("snc,snk->ck", masked_std, sketch, preferred_element_type=jnp.float32)
    product = halving_allreduce(product, "ind", ind_count)
    projected = product * ((1.0 - SHRINKAGE) / everyone) + SHRINKAGE * signs

    row_start = ind_index * row_slice
    my_rows = lax.dynamic_slice_in_dim(projected, row_start, row_slice, 0)
    my_slot = unit_slot[row_start // UNIT]
    pick = jnp.stack([col_slot == 0, col_slot == last_slot, col_slot == my_slot]).astype(jnp.float32)
    grams = jnp.einsum(
        "mc,ck,cl->mkl",
        pick,
        projected,
        projected,
        precision=lax.Precision.HIGHEST,
        preferred_element_type=jnp.float32,
    )
    head_in, tail_in = halo(
        grams[0], grams[1], blk_index, blk_count, reach, edge_blocks, first_block, last_block
    )
    gram = grams[2]
    gram = gram + jnp.where(my_slot == 0, head_in, 0.0)
    gram = gram + jnp.where(my_slot == last_slot, tail_in, 0.0)
    my_block = first_block + my_slot
    gram = gram / (block_units[my_block] * UNIT).astype(jnp.float32)
    factor = jnp.linalg.cholesky(gram)
    return jax.scipy.linalg.solve_triangular(factor, my_rows.T, lower=True).T


def solution(mesh):
    return jax.shard_map(
        on_device,
        mesh=mesh,
        in_specs=(P("ind", "blk"), P(), P()),
        out_specs=P(("blk", "ind"), None),
        check_vma=False,
    )
```

time: 1040 us -> 263 us (0.25); the launches traced: 1020 us -> 260 us
  waiting for transfers between devices: 446 us -> 76.8 us
  other arithmetic: 275 us -> 67.3 us
  blocking collectives: 118 us -> 0 us
  starting transfers between devices: 0.21 us -> 79.8 us
  loops' own time: 72.2 us -> 0.25 us
  local copies, waits for them, and re-layouts: 69.4 us -> 13.2 us
    all_gather x4 -> x0, waiting for transfers between devices: 252 us -> none  [prefix(): gathered = jax.tree.map(lambda a: lax.all_gather(a, axis), part)]
    another operation x33 -> x17, other arithmetic: 203 us -> 56.8 us  [the longest x7 34.7 us: on_device(): factor = jnp.linalg.cholesky(gram)]
    psum x1 -> x0, waiting for transfers between devices: 117 us -> none  [on_device(): gram_parts = lax.psum(slot_grams(projected, my_slots, slot_total), 'ind')]
    ppermute x0 -> x20, starting transfers between devices: none -> 79.8 us  [the longest x8 29.8 us: shift(): return lax.ppermute(x, axis, pairs)]
    ppermute x0 -> x20, waiting for transfers between devices: none -> 76.8 us  [the longest x4 32.4 us: halving_allreduce(): x = keep + lax.ppermute(send, axis, [(j, j ^ mask) for j in range(count)])]
    reduce_scatter x1 -> x0, waiting for transfers between devices: 75.8 us -> none  [on_device(): lax.psum_scatter(product.reshape(row_slice * lax.axis_size('ind'), K) * r...]
    another operation x6 -> x1, loops' own time: 72.2 us -> 0.25 us  [on_device(): return jax.scipy.linalg.solve_triangular(factor, my_rows.T, lower=True).T]
    unnamed x1 -> x0, blocking collectives: 63.8 us -> none
  transfers between devices with their start and end apart: 6 -> 20, of which waited for: 6 -> 14; matrix products, arithmetic and copies ran while one was open for 3% -> 3% of each run, Pallas kernels for 0% -> 0%
where the time goes in v1:
time: 263 us; the launch traced here: 260 us
  starting transfers between devices  79.8 us (30%)
  waiting for transfers between devices  76.8 us (29%)
  other arithmetic  67.3 us (26%)
  local copies, waits for them, and re-layouts  13.2 us (5%)
  between operations  11.9 us (5%)
  matrix products  10.9 us (4%)
    another operation x7, other arithmetic, on_device(): factor = jnp.linalg.cholesky(gram)  34.7 us
    ppermute x4, waiting for transfers between devices, halving_allreduce(): x = keep + lax.ppermute(send, axis, [(j, j ^ mask) for j in range(count)])  32.4 us
    ppermute x8, starting transfers between devices, shift(): return lax.ppermute(x, axis, pairs)  29.8 us
    ppermute x4, waiting for transfers between devices, halving_allreduce(): got = lax.ppermute(x, axis, [(j, j ^ mask) for j in range(count)])  26.2 us
    ppermute x4, starting transfers between devices, xor_allreduce(): x = x + lax.ppermute(x, axis, [(j, j ^ mask) for j in range(count)])  21.6 us
    another operation x3, other arithmetic, on_device(): return jax.scipy.linalg.solve_triangular(factor, my_rows.T, lower=True).T  20.5 us
    ppermute x4, starting transfers between devices, halving_allreduce(): x = keep + lax.ppermute(send, axis, [(j, j ^ mask) for j in range(count)])  17.2 us
    ppermute x8, waiting for transfers between devices, shift(): return lax.ppermute(x, axis, pairs)  15 us
  transfers between devices with their start and end apart: 20, of which 14 were waited for; matrix products, arithmetic and copies ran while one was open for 3% of the time, Pallas kernels for 0%

profile of v1, /device:TPU:6, one launch (start us, length us, event | category | flops | bytes accessed | tf_op | source)
XLA Modules:
  0.0 260.1 jit_solution(11081295295029203043)
XLA Ops:
  0.0 1.1 convert_reduce_fusion
  1.2 1.9 collective-permute-start
  3.1 0.7 multiply_bitcast_fusion
  4.1 0.7 multiply_subtract_fusion
  6.2 4.3 %collective-permute-start.1 = (f32[2,2048]{1,0:T(2,128)S(1)}, f32[2,2048]{1,0:T(2,128)S(1)}, u32[]{:S(2)}, u32[]{:S(2)}) collective-permute-start(f32[2,2048]{1,0:T(2,128)S(1)} %fusion.60), channel_id=1, source_target_pairs={{0,64},{32,96},{64,0},{96,32},{128,192},{160,224},{192,128},{224,1... | collective-permute-start | bytes 49160 | tf_op jit(solution)/shard_map/ppermute | solution.py:31
  10.7 1.5 collective-permute-done.1
  12.3 6.1 %collective-permute-start.2 = (f32[2,2048]{1,0:T(2,128)S(1)}, f32[2,2048]{1,0:T(2,128)S(1)}, u32[]{:S(2)}, u32[]{:S(2)}) collective-permute-start(f32[2,2048]{1,0:T(2,128)S(1)} %fusion.66), channel_id=1, source_target_pairs={{0,128},{32,160},{64,192},{96,224},{128,0},{160,32},{192,64},{224,... | collective-permute-start | bytes 49160 | tf_op jit(solution)/shard_map/ppermute | solution.py:31
  18.4 1.7 collective-permute-done.2
  20.1 9.3 %collective-permute-start.3 = (f32[2,2048]{1,0:T(2,128)S(1)}, f32[2,2048]{1,0:T(2,128)S(1)}, u32[]{:S(2)}, u32[]{:S(2)}) collective-permute-start(f32[2,2048]{1,0:T(2,128)S(1)} %add.189), channel_id=1, source_target_pairs={{0,256},{32,288},{64,320},{96,352},{128,384},{160,416},{192,448},{... | collective-permute-start | bytes 49160 | tf_op jit(solution)/shard_map/ppermute | solution.py:31
  31.3 1.1 multiply_convert_fusion
  32.4 1.3 fusion.14
  33.8 3.5 %collective-permute-start.4 = (f32[64,256]{1,0:T(8,128)S(1)}, f32[64,256]{1,0:T(8,128)S(1)}, u32[]{:S(2)}, u32[]{:S(2)}) collective-permute-start(f32[64,256]{1,0:T(8,128)S(1)} %dynamic-slice_bitcast_fusion.1), channel_id=1, source_target_pairs={{0,1},{1,2},{2,3},{3,4},{4,5},{5,6},{6,7},{7,8},{8,9},{9,10},{10,1... | collective-permute-start | bytes 196616 | tf_op jit(solution)/shard_map/ppermute | solution.py:59
  37.3 4.5 %collective-permute-start.5 = (f32[64,256]{1,0:T(8,128)S(1)}, f32[64,256]{1,0:T(8,128)S(1)}, u32[]{:S(2)}, u32[]{:S(2)}) collective-permute-start(f32[64,256]{1,0:T(8,128)S(1)} %dynamic-slice_bitcast_fusion.1), channel_id=1, source_target_pairs={{0,2},{1,3},{2,4},{3,5},{4,6},{5,7},{6,8},{7,9},{8,10},{9,11},{10,... | collective-permute-start | bytes 196616 | tf_op jit(solution)/shard_map/ppermute | solution.py:59
  41.8 0.7 constant_dynamic-slice_fusion.2
  47.5 4.5 %collective-permute-start.6 = (f32[64,256]{1,0:T(8,128)S(1)}, f32[64,256]{1,0:T(8,128)S(1)}, u32[]{:S(2)}, u32[]{:S(2)}) collective-permute-start(f32[64,256]{1,0:T(8,128)S(1)} %get-tuple-element.67), channel_id=1, source_target_pairs={{1,0},{2,1},{3,2},{4,3},{5,4},{6,5},{7,6},{8,7},{9,8},{10,9},{11,1... | collective-permute-start | bytes 196616 | tf_op jit(solution)/shard_map/ppermute | solution.py:59
  51.9 2.5 collective-permute-start.7
  54.4 0.7 and_reduce_fusion
  55.1 4.3 %collective-permute-done.7 = f32[64,256]{1,0:T(8,128)S(1)} collective-permute-done((f32[64,256]{1,0:T(8,128)S(1)}, f32[64,256]{1,0:T(8,128)S(1)}, u32[]{:S(2)}, u32[]{:S(2)}) %collective-permute-start.7) | collective-permute-done | bytes 65568 | tf_op jit(solution)/shard_map/ppermute | solution.py:59
  59.4 0.7 fusion.42
  60.1 0.8 convolution_bitcast_fusion
  61.0 1.9 collective-permute-start.8
  62.9 2.8 %collective-permute-done.8 = f32[1024,256]{1,0:T(8,128)} collective-permute-done((f32[1024,256]{1,0:T(8,128)S(1)}, f32[1024,256]{1,0:T(8,128)}, u32[]{:S(2)}, u32[]{:S(2)}) %collective-permute-start.8) | collective-permute-done | bytes 1048608 | tf_op jit(solution)/shard_map/ppermute | solution.py:49
  65.6 1.4 select_add_fusion
  67.2 3.4 %collective-permute-start.9 = (f32[512,256]{1,0:T(8,128)S(1)}, f32[512,256]{1,0:T(8,128)S(1)}, u32[]{:S(2)}, u32[]{:S(2)}) collective-permute-start(f32[512,256]{1,0:T(8,128)S(1)} %slice_select_fusion.1), channel_id=1, source_target_pairs={{0,64},{32,96},{64,0},{96,32},{128,192},{160,224},{192,128},{224,1... | collective-permute-start | bytes 1572872 | tf_op jit(solution)/shard_map/ppermute | solution.py:49
  70.5 12.5 %collective-permute-done.9 = f32[512,256]{1,0:T(8,128)S(1)} collective-permute-done((f32[512,256]{1,0:T(8,128)S(1)}, f32[512,256]{1,0:T(8,128)S(1)}, u32[]{:S(2)}, u32[]{:S(2)}) %collective-permute-start.9) | collective-permute-done | bytes 524320 | tf_op jit(solution)/shard_map/ppermute | solution.py:49
  83.2 4.3 %collective-permute-start.10 = (f32[256,256]{1,0:T(8,128)S(1)}, f32[256,256]{1,0:T(8,128)S(1)}, u32[]{:S(2)}, u32[]{:S(2)}) collective-permute-start(f32[256,256]{1,0:T(8,128)S(1)} %slice_select_fusion.2), channel_id=1, source_target_pairs={{0,128},{32,160},{64,192},{96,224},{128,0},{160,32},{192,64},{224,... | collective-permute-start | bytes 786440 | tf_op jit(solution)/shard_map/ppermute | solution.py:49
  87.5 11.6 %collective-permute-done.10 = f32[256,256]{1,0:T(8,128)S(1)} collective-permute-done((f32[256,256]{1,0:T(8,128)S(1)}, f32[256,256]{1,0:T(8,128)S(1)}, u32[]{:S(2)}, u32[]{:S(2)}) %collective-permute-start.10) | collective-permute-done | bytes 262176 | tf_op jit(solution)/shard_map/ppermute | solution.py:49
  99.1 7.6 %collective-permute-start.11 = (f32[128,256]{1,0:T(8,128)S(1)}, f32[128,256]{1,0:T(8,128)S(1)}, u32[]{:S(2)}, u32[]{:S(2)}) collective-permute-start(f32[128,256]{1,0:T(8,128)S(1)} %slice_select_fusion.3), channel_id=1, source_target_pairs={{0,256},{32,288},{64,320},{96,352},{128,384},{160,416},{192,448},{... | collective-permute-start | bytes 393224 | tf_op jit(solution)/shard_map/ppermute | solution.py:49
  106.8 5.6 %collective-permute-done.11 = f32[128,256]{1,0:T(8,128)S(1)} collective-permute-done((f32[128,256]{1,0:T(8,128)S(1)}, f32[128,256]{1,0:T(8,128)S(1)}, u32[]{:S(2)}, u32[]{:S(2)}) %collective-permute-start.11) | collective-permute-done | bytes 131104 | tf_op jit(solution)/shard_map/ppermute | solution.py:49
  112.4 5.2 %collective-permute-start.12 = (f32[128,256]{1,0:T(8,128)S(1)}, f32[128,256]{1,0:T(8,128)S(1)}, u32[]{:S(2)}, u32[]{:S(2)}) collective-permute-start(f32[128,256]{1,0:T(8,128)S(1)} %select_add_fusion.3), channel_id=1, source_target_pairs={{0,256},{32,288},{64,320},{96,352},{128,384},{160,416},{192,448},{... | collective-permute-start | bytes 393224 | tf_op jit(solution)/shard_map/ppermute | solution.py:51
  117.7 5.5 %collective-permute-done.12 = f32[128,256]{1,0:T(8,128)S(1)} collective-permute-done((f32[128,256]{1,0:T(8,128)S(1)}, f32[128,256]{1,0:T(8,128)S(1)}, u32[]{:S(2)}, u32[]{:S(2)}) %collective-permute-start.12) | collective-permute-done | bytes 131104 | tf_op jit(solution)/shard_map/ppermute | solution.py:51
  123.2 1.9 collective-permute-start.13
  125.1 10.6 %collective-permute-done.13 = f32[256,256]{1,0:T(8,128)S(1)} collective-permute-done((f32[256,256]{1,0:T(8,128)S(1)}, f32[256,256]{1,0:T(8,128)S(1)}, u32[]{:S(2)}, u32[]{:S(2)}) %collective-permute-start.13) | collective-permute-done | bytes 262176 | tf_op jit(solution)/shard_map/ppermute | solution.py:51
  135.7 1.9 collective-permute-start.14
  137.7 9.2 %collective-permute-done.14 = f32[512,256]{1,0:T(8,128)S(1)} collective-permute-done((f32[512,256]{1,0:T(8,128)S(1)}, f32[512,256]{1,0:T(8,128)S(1)}, u32[]{:S(2)}, u32[]{:S(2)}) %collective-permute-start.14) | collective-permute-done | bytes 524320 | tf_op jit(solution)/shard_map/ppermute | solution.py:51
  147.0 2.1 collective-permute-start.15
  149.7 0.6 broadcast_compare_fusion.1
  150.6 0.9 collective-permute-done.15
  151.5 1.0 copy-done
  152.5 3.0 %fusion.11 = f32[2048,256]{1,0:T(8,128)S(1)} fusion(f32[1024,256]{1,0:T(8,128)S(1)} %maximum_select_fusion.1, f32[1024,256]{1,0:T(8,128)} %copy-done, s32[]{:T(128)} %bitcast.109, s32[2048]{0:T(1024)S(1)} %add_multiply_fusion, pred[]{:T(512)S(6)} %ne.24), kind=kLoop, calls=%fused_computation.17 | loop fusion | flops 9961472 | bytes 4202501 | tf_op jit(solution)/shard_map/add | solution.py:137
  155.5 1.9 copy.23
  157.4 7.4 %fusion.19 = f32[3,256,256]{1,2,0:T(8,128)S(1)} fusion(f32[2048,256]{1,0:T(8,128)S(1)} %fusion.11, f32[2048,3]{0,1:T(4,128)S(1)} %convert_bitcast_fusion, f32[2048,256]{0,1:T(8,128)} %copy.23), kind=kOutput, calls=%fused_computation.25 | convolution fusion | flops 4833411072 | bytes 5005312 | tf_op jit(solution)/shard_map/mc,ck,cl->mkl/dot_general | solution.py:143
  164.8 0.8 slice_bitcast_fusion.1
  165.7 3.0 %collective-permute-start.16 = (f32[256,256]{0,1:T(8,128)}, f32[256,256]{0,1:T(8,128)S(1)}, u32[]{:S(2)}, u32[]{:S(2)}) collective-permute-start(f32[256,256]{0,1:T(8,128)} %get-tuple-element.65), channel_id=1, source_target_pairs={{0,1},{1,2},{2,3},{3,4},{4,5},{5,6},{6,7},{7,8},{8,9},{9,10},{10,1... | collective-permute-start | bytes 786440 | tf_op jit(solution)/shard_map/ppermute | solution.py:59
  168.6 4.8 %collective-permute-start.17 = (f32[256,256]{0,1:T(8,128)}, f32[256,256]{0,1:T(8,128)S(1)}, u32[]{:S(2)}, u32[]{:S(2)}) collective-permute-start(f32[256,256]{0,1:T(8,128)} %get-tuple-element.65), channel_id=1, source_target_pairs={{0,2},{1,3},{2,4},{3,5},{4,6},{5,7},{6,8},{7,9},{8,10},{9,11},{10,... | collective-permute-start | bytes 786440 | tf_op jit(solution)/shard_map/ppermute | solution.py:59
  173.4 4.9 %collective-permute-start.18 = (f32[256,256]{0,1:T(8,128)}, f32[256,256]{0,1:T(8,128)}, u32[]{:S(2)}, u32[]{:S(2)}) collective-permute-start(f32[256,256]{0,1:T(8,128)} %get-tuple-element.66), channel_id=1, source_target_pairs={{1,0},{2,1},{3,2},{4,3},{5,4},{6,5},{7,6},{8,7},{9,8},{10,9},{11,1... | collective-permute-start | bytes 786440 | tf_op jit(solution)/shard_map/ppermute | solution.py:59
  178.3 2.3 collective-permute-start.19
  183.1 0.6 dynamic_slice.34
  184.7 6.0 %collective-permute-done.18 = f32[256,256]{0,1:T(8,128)} collective-permute-done((f32[256,256]{0,1:T(8,128)}, f32[256,256]{0,1:T(8,128)}, u32[]{:S(2)}, u32[]{:S(2)}) %collective-permute-start.18) | collective-permute-done | bytes 262176 | tf_op jit(solution)/shard_map/ppermute | solution.py:59
  190.7 4.4 %collective-permute-done.19 = f32[256,256]{0,1:T(8,128)} collective-permute-done((f32[256,256]{0,1:T(8,128)}, f32[256,256]{0,1:T(8,128)}, u32[]{:S(2)}, u32[]{:S(2)}) %collective-permute-start.19) | collective-permute-done | bytes 262176 | tf_op jit(solution)/shard_map/ppermute | solution.py:59
  195.4 11.7 %cholesky.49 = f32[128,128]{1,0:T(8,128)S(1)} custom-call(f32[128,128]{1,0:T(8,128)S(1)} %cholesky.115), custom_call_target="Cholesky" | custom-call | tf_op jit(solution)/shard_map/jit(cholesky)/cholesky | solution.py:159
  207.2 9.8 %custom-call.15 = f32[1,128,128]{1,2,0:T(8,128)S(1)} custom-call(f32[1,128,128]{2,1,0:T(8,128)S(1)} %get-tuple-element.70), custom_call_target="InvertDiagBlocksLowerTriangular" | custom-call | tf_op jit(solution)/shard_map/jit(cholesky)/cholesky | solution.py:159
  217.5 11.7 %cholesky.103 = f32[128,128]{1,0:T(8,128)S(1)} custom-call(f32[128,128]{1,0:T(8,128)S(1)} %convolution_subtract_fusion), custom_call_target="Cholesky" | custom-call | tf_op jit(solution)/shard_map/jit(cholesky)/cholesky | solution.py:159
  229.5 0.7 compare_reduce_fusion
  230.2 0.7 compare_reduce_fusion.1
  232.3 5.7 %while.3 = (s32[]{:T(128)}, f32[256,256]{0,1:T(8,128)S(1)}, s32[2,2]{1,0:T(2,128)S(1)}, f32[2,128,128]{2,1,0:T(8,128)}, s32[]{:T(128)}) while((s32[]{:T(128)}, f32[256,256]{0,1:T(8,128)S(1)}, s32[2,2]{1,0:T(2,128)S(1)}, f32[2,128,128]{2,1,0:T(8,128)}, s32[]{:T(128)}) %tuple.44), condition=%wide.while_cond.2, body=%wide.while_body.2.sunk | while | flops 2 | bytes 393829 | solution.py:160
  232.5 0.6 fusion.68
  233.2 1.4 dynamic-slice.27
  234.6 0.6 bitcast_dynamic-update-slice_fusion.2
  235.3 0.6 fusion.68
  235.9 1.4 dynamic-slice.27
  237.3 0.6 bitcast_dynamic-update-slice_fusion.2
  238.0 20.5 %custom-call.16 = f32[2,128,128]{1,2,0:T(8,128)S(1)} custom-call(f32[2,128,128]{2,1,0:T(8,128)} %get-tuple-element.36), custom_call_target="InvertDiagBlocksLowerTriangular" | custom-call | tf_op jit(solution)/shard_map/jit(_solve_triangular)/triangular_solve | solution.py:160
  259.4 0.8 copy.31
  (80 shorter events, 6.1 us)
Async XLA Ops:
  1.2 5.0 %collective-permute-start = (f32[2,2048]{1,0:T(2,128)S(1)}, f32[2,2048]{1,0:T(2,128)S(1)}, u32[]{:S(2)}, u32[]{:S(2)}) collective-permute-start(f32[2,2048]{1,0:T(2,128)S(1)} %pad_maximum_fusion), channel_id=1, source_target_pairs={{0,32},{32,0},{64,96},{96,64},{128,160},{160,128},{192,224},{224,1... | collective-permute-start | bytes 49160 | tf_op jit(solution)/shard_map/ppermute | solution.py:31
  6.2 6.0 %collective-permute-start.1 = (f32[2,2048]{1,0:T(2,128)S(1)}, f32[2,2048]{1,0:T(2,128)S(1)}, u32[]{:S(2)}, u32[]{:S(2)}) collective-permute-start(f32[2,2048]{1,0:T(2,128)S(1)} %fusion.60), channel_id=1, source_target_pairs={{0,64},{32,96},{64,0},{96,32},{128,192},{160,224},{192,128},{224,1... | collective-permute-start | bytes 49160 | tf_op jit(solution)/shard_map/ppermute | solution.py:31
  12.3 7.8 %collective-permute-start.2 = (f32[2,2048]{1,0:T(2,128)S(1)}, f32[2,2048]{1,0:T(2,128)S(1)}, u32[]{:S(2)}, u32[]{:S(2)}) collective-permute-start(f32[2,2048]{1,0:T(2,128)S(1)} %fusion.66), channel_id=1, source_target_pairs={{0,128},{32,160},{64,192},{96,224},{128,0},{160,32},{192,64},{224,... | collective-permute-start | bytes 49160 | tf_op jit(solution)/shard_map/ppermute | solution.py:31
  20.1 11.2 %collective-permute-start.3 = (f32[2,2048]{1,0:T(2,128)S(1)}, f32[2,2048]{1,0:T(2,128)S(1)}, u32[]{:S(2)}, u32[]{:S(2)}) collective-permute-start(f32[2,2048]{1,0:T(2,128)S(1)} %add.189), channel_id=1, source_target_pairs={{0,256},{32,288},{64,320},{96,352},{128,384},{160,416},{192,448},{... | collective-permute-start | bytes 49160 | tf_op jit(solution)/shard_map/ppermute | solution.py:31
  32.4 22.0 %copy-start.1 = (s32[3]{0:T(128)S(1)}, s32[3]{0:T(128)}, u32[]{:S(2)}) copy-start(s32[3]{0:T(128)} %constant.206.clone.1) | copy-start | bytes 40
  33.8 13.6 %collective-permute-start.4 = (f32[64,256]{1,0:T(8,128)S(1)}, f32[64,256]{1,0:T(8,128)S(1)}, u32[]{:S(2)}, u32[]{:S(2)}) collective-permute-start(f32[64,256]{1,0:T(8,128)S(1)} %dynamic-slice_bitcast_fusion.1), channel_id=1, source_target_pairs={{0,1},{1,2},{2,3},{3,4},{4,5},{5,6},{6,7},{7,8},{8,9},{9,10},{10,1... | collective-permute-start | bytes 196616 | tf_op jit(solution)/shard_map/ppermute | solution.py:59
  37.3 10.1 %collective-permute-start.5 = (f32[64,256]{1,0:T(8,128)S(1)}, f32[64,256]{1,0:T(8,128)S(1)}, u32[]{:S(2)}, u32[]{:S(2)}) collective-permute-start(f32[64,256]{1,0:T(8,128)S(1)} %dynamic-slice_bitcast_fusion.1), channel_id=1, source_target_pairs={{0,2},{1,3},{2,4},{3,5},{4,6},{5,7},{6,8},{7,9},{8,10},{9,11},{10,... | collective-permute-start | bytes 196616 | tf_op jit(solution)/shard_map/ppermute | solution.py:59
  47.5 7.7 %collective-permute-start.6 = (f32[64,256]{1,0:T(8,128)S(1)}, f32[64,256]{1,0:T(8,128)S(1)}, u32[]{:S(2)}, u32[]{:S(2)}) collective-permute-start(f32[64,256]{1,0:T(8,128)S(1)} %get-tuple-element.67), channel_id=1, source_target_pairs={{1,0},{2,1},{3,2},{4,3},{5,4},{6,5},{7,6},{8,7},{9,8},{10,9},{11,1... | collective-permute-start | bytes 196616 | tf_op jit(solution)/shard_map/ppermute | solution.py:59
  51.9 7.5 %collective-permute-start.7 = (f32[64,256]{1,0:T(8,128)S(1)}, f32[64,256]{1,0:T(8,128)S(1)}, u32[]{:S(2)}, u32[]{:S(2)}) collective-permute-start(f32[64,256]{1,0:T(8,128)S(1)} %get-tuple-element.67), channel_id=1, source_target_pairs={{2,0},{3,1},{4,2},{5,3},{6,4},{7,5},{8,6},{9,7},{10,8},{11,9},{12,... | collective-permute-start | bytes 196616 | tf_op jit(solution)/shard_map/ppermute | solution.py:59
  61.0 4.7 %collective-permute-start.8 = (f32[1024,256]{1,0:T(8,128)S(1)}, f32[1024,256]{1,0:T(8,128)}, u32[]{:S(2)}, u32[]{:S(2)}) collective-permute-start(f32[1024,256]{1,0:T(8,128)S(1)} %slice_select_fusion), channel_id=1, source_target_pairs={{0,32},{32,0},{64,96},{96,64},{128,160},{160,128},{192,224},{224,1... | collective-permute-start | bytes 3145736 | tf_op jit(solution)/shard_map/ppermute | solution.py:49
  67.2 15.9 %collective-permute-start.9 = (f32[512,256]{1,0:T(8,128)S(1)}, f32[512,256]{1,0:T(8,128)S(1)}, u32[]{:S(2)}, u32[]{:S(2)}) collective-permute-start(f32[512,256]{1,0:T(8,128)S(1)} %slice_select_fusion.1), channel_id=1, source_target_pairs={{0,64},{32,96},{64,0},{96,32},{128,192},{160,224},{192,128},{224,1... | collective-permute-start | bytes 1572872 | tf_op jit(solution)/shard_map/ppermute | solution.py:49
  83.2 15.9 %collective-permute-start.10 = (f32[256,256]{1,0:T(8,128)S(1)}, f32[256,256]{1,0:T(8,128)S(1)}, u32[]{:S(2)}, u32[]{:S(2)}) collective-permute-start(f32[256,256]{1,0:T(8,128)S(1)} %slice_select_fusion.2), channel_id=1, source_target_pairs={{0,128},{32,160},{64,192},{96,224},{128,0},{160,32},{192,64},{224,... | collective-permute-start | bytes 786440 | tf_op jit(solution)/shard_map/ppermute | solution.py:49
  99.1 13.2 %collective-permute-start.11 = (f32[128,256]{1,0:T(8,128)S(1)}, f32[128,256]{1,0:T(8,128)S(1)}, u32[]{:S(2)}, u32[]{:S(2)}) collective-permute-start(f32[128,256]{1,0:T(8,128)S(1)} %slice_select_fusion.3), channel_id=1, source_target_pairs={{0,256},{32,288},{64,320},{96,352},{128,384},{160,416},{192,448},{... | collective-permute-start | bytes 393224 | tf_op jit(solution)/shard_map/ppermute | solution.py:49
  112.4 10.8 %collective-permute-start.12 = (f32[128,256]{1,0:T(8,128)S(1)}, f32[128,256]{1,0:T(8,128)S(1)}, u32[]{:S(2)}, u32[]{:S(2)}) collective-permute-start(f32[128,256]{1,0:T(8,128)S(1)} %select_add_fusion.3), channel_id=1, source_target_pairs={{0,256},{32,288},{64,320},{96,352},{128,384},{160,416},{192,448},{... | collective-permute-start | bytes 393224 | tf_op jit(solution)/shard_map/ppermute | solution.py:51
  123.2 12.5 %collective-permute-start.13 = (f32[256,256]{1,0:T(8,128)S(1)}, f32[256,256]{1,0:T(8,128)S(1)}, u32[]{:S(2)}, u32[]{:S(2)}) collective-permute-start(f32[256,256]{1,0:T(8,128)S(1)} %maximum_select_fusion.3), channel_id=1, source_target_pairs={{0,128},{32,160},{64,192},{96,224},{128,0},{160,32},{192,64},{224,... | collective-permute-start | bytes 786440 | tf_op jit(solution)/shard_map/ppermute | solution.py:51
  135.7 11.1 %collective-permute-start.14 = (f32[512,256]{1,0:T(8,128)S(1)}, f32[512,256]{1,0:T(8,128)S(1)}, u32[]{:S(2)}, u32[]{:S(2)}) collective-permute-start(f32[512,256]{1,0:T(8,128)S(1)} %maximum_select_fusion.2), channel_id=1, source_target_pairs={{0,64},{32,96},{64,0},{96,32},{128,192},{160,224},{192,128},{224,1... | collective-permute-start | bytes 1572872 | tf_op jit(solution)/shard_map/ppermute | solution.py:51
  147.0 4.6 %collective-permute-start.15 = (f32[1024,256]{1,0:T(8,128)S(1)}, f32[1024,256]{1,0:T(8,128)S(1)}, u32[]{:S(2)}, u32[]{:S(2)}) collective-permute-start(f32[1024,256]{1,0:T(8,128)S(1)} %maximum_select_fusion.1), channel_id=1, source_target_pairs={{0,32},{32,0},{64,96},{96,64},{128,160},{160,128},{192,224},{224,1... | collective-permute-start | bytes 3145736 | tf_op jit(solution)/shard_map/ppermute | solution.py:51
  151.5 1.0 copy-start
  157.4 25.7 %copy-start.2 = (s32[64]{0:T(128)S(1)}, s32[64]{0:T(128)}, u32[]{:S(2)}) copy-start(s32[64]{0:T(128)} %param.8) | copy-start | bytes 772
  165.7 19.0 %collective-permute-start.16 = (f32[256,256]{0,1:T(8,128)}, f32[256,256]{0,1:T(8,128)S(1)}, u32[]{:S(2)}, u32[]{:S(2)}) collective-permute-start(f32[256,256]{0,1:T(8,128)} %get-tuple-element.65), channel_id=1, source_target_pairs={{0,1},{1,2},{2,3},{3,4},{4,5},{5,6},{6,7},{7,8},{8,9},{9,10},{10,1... | collective-permute-start | bytes 786440 | tf_op jit(solution)/shard_map/ppermute | solution.py:59
  168.6 16.0 %collective-permute-start.17 = (f32[256,256]{0,1:T(8,128)}, f32[256,256]{0,1:T(8,128)S(1)}, u32[]{:S(2)}, u32[]{:S(2)}) collective-permute-start(f32[256,256]{0,1:T(8,128)} %get-tuple-element.65), channel_id=1, source_target_pairs={{0,2},{1,3},{2,4},{3,5},{4,6},{5,7},{6,8},{7,9},{8,10},{9,11},{10,... | collective-permute-start | bytes 786440 | tf_op jit(solution)/shard_map/ppermute | solution.py:59
  173.4 17.3 %collective-permute-start.18 = (f32[256,256]{0,1:T(8,128)}, f32[256,256]{0,1:T(8,128)}, u32[]{:S(2)}, u32[]{:S(2)}) collective-permute-start(f32[256,256]{0,1:T(8,128)} %get-tuple-element.66), channel_id=1, source_target_pairs={{1,0},{2,1},{3,2},{4,3},{5,4},{6,5},{7,6},{8,7},{9,8},{10,9},{11,1... | collective-permute-start | bytes 786440 | tf_op jit(solution)/shard_map/ppermute | solution.py:59
  178.3 16.8 %collective-permute-start.19 = (f32[256,256]{0,1:T(8,128)}, f32[256,256]{0,1:T(8,128)}, u32[]{:S(2)}, u32[]{:S(2)}) collective-permute-start(f32[256,256]{0,1:T(8,128)} %get-tuple-element.66), channel_id=1, source_target_pairs={{2,0},{3,1},{4,2},{5,3},{6,4},{7,5},{8,6},{9,7},{10,8},{11,9},{12,... | collective-permute-start | bytes 786440 | tf_op jit(solution)/shard_map/ppermute | solution.py:59

commit v2 on v1

--- a/solution.py
+++ b/solution.py
@@ -25,33 +25,76 @@
     return (1 - 2 * parity).astype(jnp.float32)
 
 
-def xor_allreduce(x, axis, count):
-    mask = 1
-    while mask < count:
-        x = x + lax.ppermute(x, axis, [(j, j ^ mask) for j in range(count)])
-        mask *= 2
+def digit_rounds(count):
+    rounds = []
+    bit = 0
+    while (1 << bit) < count:
+        radix = 4 if (4 << bit) <= count else 2
+        rounds.append((bit, radix))
+        bit += 2 if radix == 4 else 1
+    return rounds
+
+
+def exact_allreduce(x, axis, count):
+    for bit, radix in digit_rounds(count):
+        got = [
+            lax.ppermute(x, axis, [(j, j ^ (o << bit)) for j in range(count)])
+            for o in range(1, radix)
+        ]
+        x = x + sum(got[1:], got[0])
     return x
 
 
-def halving_allreduce(x, axis, count):
+def chunked_allreduce(x, axis, count):
     place = lax.axis_index(axis)
-    masks = []
-    mask = 1
-    while mask < count:
-        masks.append(mask)
-        mask *= 2
-    for mask in masks:
-        half = x.shape[0] // 2
-        lower, upper = x[:half], x[half:]
-        high = (place & mask) != 0
-        send = jnp.where(high, lower, upper)
-        keep = jnp.where(high, upper, lower)
-        x = keep + lax.ppermute(send, axis, [(j, j ^ mask) for j in range(count)])
-    for mask in reversed(masks):
-        got = lax.ppermute(x, axis, [(j, j ^ mask) for j in range(count)])
-        high = (place & mask) != 0
-        x = jnp.where(high, jnp.concatenate([got, x], 0), jnp.concatenate([x, got], 0))
+    rounds = digit_rounds(count)
+    for bit, radix in rounds:
+        digit = (place >> bit) & (radix - 1)
+        piece = x.shape[0] // radix
+        parts = [lax.dynamic_slice_in_dim(x, (digit ^ o) * piece, piece, 0) for o in range(radix)]
+        total = parts[0]
+        for o in range(1, radix):
+            total = total + lax.ppermute(
+                parts[o], axis, [(j, j ^ (o << bit)) for j in range(count)]
+            )
+        x = total
+    for bit, radix in reversed(rounds):
+        digit = (place >> bit) & (radix - 1)
+        got = [x] + [
+            lax.ppermute(x, axis, [(j, j ^ (o << bit)) for j in range(count)])
+            for o in range(1, radix)
+        ]
+        pieces = []
+        for t in range(radix):
+            offset = t ^ digit
+            pick = got[radix - 1]
+            for o in range(radix - 2, -1, -1):
+                pick = jnp.where(offset == o, got[o], pick)
+            pieces.append(pick)
+        x = jnp.concatenate(pieces, 0)
     return x
+
+
+def dot_hi(a, b):
+    return jnp.dot(a, b, precision=lax.Precision.HIGHEST, preferred_element_type=jnp.float32)
+
+
+def lower_inverse(lower):
+    eye = jnp.eye(lower.shape[0], dtype=lower.dtype)
+    return jax.scipy.linalg.solve_triangular(lower, eye, lower=True)
+
+
+def basis_rows(gram, rows):
+    half = gram.shape[0] // 2
+    l11 = jnp.linalg.cholesky(gram[:half, :half])
+    m11 = lower_inverse(l11)
+    l21 = dot_hi(gram[half:, :half], m11.T)
+    l22 = jnp.linalg.cholesky(gram[half:, half:] - dot_hi(l21, l21.T))
+    m22 = lower_inverse(l22)
+    m21 = -dot_hi(m22, dot_hi(l21, m11))
+    left = dot_hi(rows[:, :half], m11.T)
+    right = dot_hi(rows[:, :half], m21.T) + dot_hi(rows[:, half:], m22.T)
+    return jnp.concatenate([left, right], 1)
 
 
 def shift(x, axis, count, step):
@@ -95,7 +138,7 @@
     ind_index = lax.axis_index("ind")
 
     dosage = genotypes.astype(jnp.float32)
-    stats = xor_allreduce(jnp.stack([jnp.sum(dosage, 0), jnp.sum(dosage * dosage, 0)]), "ind", ind_count)
+    stats = exact_allreduce(jnp.stack([jnp.sum(dosage, 0), jnp.sum(dosage * dosage, 0)]), "ind", ind_count)
     average = stats[0] / everyone
     spread_sq = stats[1] / everyone - average * average
     standard = ((dosage - average) * lax.rsqrt(spread_sq + 1e-05)).astype(jnp.bfloat16)
@@ -133,7 +176,7 @@
     sketch = parts.astype(jnp.bfloat16)
 
     product = jnp.einsum("snc,snk->ck", masked_std, sketch, preferred_element_type=jnp.float32)
-    product = halving_allreduce(product, "ind", ind_count)
+    product = chunked_allreduce(product, "ind", ind_count)
     projected = product * ((1.0 - SHRINKAGE) / everyone) + SHRINKAGE * signs
 
     row_start = ind_index * row_slice
@@ -156,8 +199,7 @@
     gram = gram + jnp.where(my_slot == last_slot, tail_in, 0.0)
     my_block = first_block + my_slot
     gram = gram / (block_units[my_block] * UNIT).astype(jnp.float32)
-    factor = jnp.linalg.cholesky(gram)
-    return jax.scipy.linalg.solve_triangular(factor, my_rows.T, lower=True).T
+    return basis_rows(gram, my_rows)
 
 
 def solution(mesh):

time: 263 us -> 258 us (0.981)
  starting transfers between devices: 79.8 us -> 94.4 us
  other arithmetic: 67.3 us -> 57.6 us
  local copies, waits for them, and re-layouts: 13.2 us -> 7.42 us
    ppermute x12 -> x18, starting transfers between devices: 50 us -> 64.8 us  [the longest x6 24.7 us: exact_allreduce(): lax.ppermute(x, axis, [(j, j ^ o << bit) for j in range(count)])]
    another operation x15, other arithmetic: 56.8 us -> 47.3 us  [the longest x4 20.9 us: lower_inverse(): return jax.scipy.linalg.solve_triangular(lower, eye, lower=True)]
    another operation x19 -> x1, local copies, waits for them, and re-layouts: 5.89 us -> 0.1 us
    ppermute x12 -> x18, waiting for transfers between devices: 61.8 us -> 59.9 us  [the longest x6 30.4 us: chunked_allreduce(): lax.ppermute(parts[o], axis, [(j, j ^ o << bit) for j in range(count)])]
  transfers between devices with their start and end apart: 20 -> 26, of which waited for: 14 -> 13; matrix products, arithmetic and copies ran while one was open for 3% -> 3% of each run, Pallas kernels for 0% -> 0%
where the time goes in v2:
time: 258 us; the launch traced here: 257 us
  starting transfers between devices  94.4 us (37%)
  waiting for transfers between devices  74.5 us (29%)
  other arithmetic  57.6 us (22%)
  matrix products  11.9 us (5%)
  between operations  10.9 us (4%)
  local copies, waits for them, and re-layouts  7.42 us (3%)
    ppermute x6, waiting for transfers between devices, chunked_allreduce(): lax.ppermute(parts[o], axis, [(j, j ^ o << bit) for j in range(count)])  30.4 us
    ppermute x8, starting transfers between devices, shift(): return lax.ppermute(x, axis, pairs)  29.6 us
    ppermute x6, waiting for transfers between devices, chunked_allreduce(): lax.ppermute(x, axis, [(j, j ^ o << bit) for j in range(count)])  28.2 us
    ppermute x6, starting transfers between devices, exact_allreduce(): lax.ppermute(x, axis, [(j, j ^ o << bit) for j in range(count)])  24.7 us
    another operation x4, other arithmetic, lower_inverse(): return jax.scipy.linalg.solve_triangular(lower, eye, lower=True)  20.9 us
    ppermute x6, starting transfers between devices, chunked_allreduce(): lax.ppermute(parts[o], axis, [(j, j ^ o << bit) for j in range(count)])  20.1 us
    ppermute x6, starting transfers between devices, chunked_allreduce(): lax.ppermute(x, axis, [(j, j ^ o << bit) for j in range(count)])  20 us
    ppermute x8, waiting for transfers between devices, shift(): return lax.ppermute(x, axis, pairs)  14.6 us
  transfers between devices with their start and end apart: 26, of which 13 were waited for; matrix products, arithmetic and copies ran while one was open for 3% of the time, Pallas kernels for 0%

profile of v2, /device:TPU:6, one launch (start us, length us, event | category | flops | bytes accessed | tf_op | source)
XLA Modules:
  0.0 256.7 jit_solution(15060370430778592040)
XLA Ops:
  0.0 1.1 convert_reduce_fusion
  1.2 3.7 %collective-permute-start.2 = (f32[2,2048]{1,0:T(2,128)S(1)}, f32[2,2048]{1,0:T(2,128)S(1)}, u32[]{:S(2)}, u32[]{:S(2)}) collective-permute-start(f32[2,2048]{1,0:T(2,128)S(1)} %pad_maximum_fusion.2), channel_id=1, source_target_pairs={{0,96},{32,64},{64,32},{96,0},{128,224},{160,192},{192,160},{224,1... | collective-permute-start | bytes 49160 | tf_op jit(solution)/shard_map/ppermute | solution.py:41
  4.9 2.5 collective-permute-start.1
  7.4 2.0 collective-permute-start
  9.4 0.7 multiply_bitcast_fusion
  10.4 0.7 multiply_subtract_fusion
  12.8 10.3 %collective-permute-start.5 = (f32[2,2048]{1,0:T(2,128)S(1)}, f32[2,2048]{1,0:T(2,128)S(1)}, u32[]{:S(2)}, u32[]{:S(2)}) collective-permute-start(f32[2,2048]{1,0:T(2,128)S(1)} %add_add_fusion.3), channel_id=1, source_target_pairs={{0,384},{32,416},{64,448},{96,480},{128,256},{160,288},{192,320},{... | collective-permute-start | bytes 49160 | tf_op jit(solution)/shard_map/ppermute | solution.py:41
  23.2 1.9 collective-permute-start.4
  25.1 4.3 %collective-permute-start.3 = (f32[2,2048]{1,0:T(2,128)S(1)}, f32[2,2048]{1,0:T(2,128)S(1)}, u32[]{:S(2)}, u32[]{:S(2)}) collective-permute-start(f32[2,2048]{1,0:T(2,128)S(1)} %add_add_fusion.3), channel_id=1, source_target_pairs={{0,128},{32,160},{64,192},{96,224},{128,0},{160,32},{192,64},{224,... | collective-permute-start | bytes 49160 | tf_op jit(solution)/shard_map/ppermute | solution.py:41
  31.3 1.3 collective-permute-done.4
  32.8 1.1 multiply_convert_fusion
  33.9 1.3 fusion.13
  35.2 4.5 %collective-permute-start.7 = (f32[64,256]{1,0:T(8,128)S(1)}, f32[64,256]{1,0:T(8,128)S(1)}, u32[]{:S(2)}, u32[]{:S(2)}) collective-permute-start(f32[64,256]{1,0:T(8,128)S(1)} %dynamic-slice_bitcast_fusion), channel_id=1, source_target_pairs={{0,2},{1,3},{2,4},{3,5},{4,6},{5,7},{6,8},{7,9},{8,10},{9,11},{10,... | collective-permute-start | bytes 196616 | tf_op jit(solution)/shard_map/ppermute | solution.py:102
  39.7 3.5 %collective-permute-start.6 = (f32[64,256]{1,0:T(8,128)S(1)}, f32[64,256]{1,0:T(8,128)S(1)}, u32[]{:S(2)}, u32[]{:S(2)}) collective-permute-start(f32[64,256]{1,0:T(8,128)S(1)} %dynamic-slice_bitcast_fusion), channel_id=1, source_target_pairs={{0,1},{1,2},{2,3},{3,4},{4,5},{5,6},{6,7},{7,8},{8,9},{9,10},{10,1... | collective-permute-start | bytes 196616 | tf_op jit(solution)/shard_map/ppermute | solution.py:102
  43.3 0.7 constant_dynamic-slice_fusion.7
  49.0 4.4 %collective-permute-start.9 = (f32[64,256]{1,0:T(8,128)S(1)}, f32[64,256]{1,0:T(8,128)S(1)}, u32[]{:S(2)}, u32[]{:S(2)}) collective-permute-start(f32[64,256]{1,0:T(8,128)S(1)} %get-tuple-element.53), channel_id=1, source_target_pairs={{2,0},{3,1},{4,2},{5,3},{6,4},{7,5},{8,6},{9,7},{10,8},{11,9},{12,... | collective-permute-start | bytes 196616 | tf_op jit(solution)/shard_map/ppermute | solution.py:102
  53.4 2.4 collective-permute-start.8
  55.7 0.7 and_reduce_fusion
  56.4 3.1 %collective-permute-done.8 = f32[64,256]{1,0:T(8,128)S(1)} collective-permute-done((f32[64,256]{1,0:T(8,128)S(1)}, f32[64,256]{1,0:T(8,128)S(1)}, u32[]{:S(2)}, u32[]{:S(2)}) %collective-permute-start.8) | collective-permute-done | bytes 65568 | tf_op jit(solution)/shard_map/ppermute | solution.py:102
  59.5 0.7 fusion.46
  60.2 0.8 convolution_bitcast_fusion
  60.9 0.9 constant_dynamic-slice_fusion.5
  61.9 1.9 collective-permute-start.10
  63.8 3.6 %collective-permute-start.12 = (f32[512,256]{1,0:T(8,128)S(1)}, f32[512,256]{1,0:T(8,128)}, u32[]{:S(2)}, u32[]{:S(2)}) collective-permute-start(f32[512,256]{1,0:T(8,128)S(1)} %get-tuple-element.42), channel_id=1, source_target_pairs={{0,96},{32,64},{64,32},{96,0},{128,224},{160,192},{192,160},{224,1... | collective-permute-start | bytes 1572872 | tf_op jit(solution)/shard_map/ppermute | solution.py:57
  67.4 2.3 collective-permute-start.11
  69.8 9.9 %collective-permute-done.12 = f32[512,256]{1,0:T(8,128)} collective-permute-done((f32[512,256]{1,0:T(8,128)S(1)}, f32[512,256]{1,0:T(8,128)}, u32[]{:S(2)}, u32[]{:S(2)}) %collective-permute-start.12) | collective-permute-done | bytes 524320 | tf_op jit(solution)/shard_map/ppermute | solution.py:57
  79.7 11.5 %collective-permute-done.11 = f32[512,256]{1,0:T(8,128)} collective-permute-done((f32[512,256]{1,0:T(8,128)S(1)}, f32[512,256]{1,0:T(8,128)}, u32[]{:S(2)}, u32[]{:S(2)}) %collective-permute-start.11) | collective-permute-done | bytes 524320 | tf_op jit(solution)/shard_map/ppermute | solution.py:57
  91.3 1.5 add_add_fusion
  92.8 3.2 %collective-permute-start.13 = (f32[128,256]{1,0:T(8,128)S(1)}, f32[128,256]{1,0:T(8,128)S(1)}, u32[]{:S(2)}, u32[]{:S(2)}) collective-permute-start(f32[128,256]{1,0:T(8,128)S(1)} %get-tuple-element.50), channel_id=1, source_target_pairs={{0,128},{32,160},{64,192},{96,224},{128,0},{160,32},{192,64},{224,... | collective-permute-start | bytes 393224 | tf_op jit(solution)/shard_map/ppermute | solution.py:57
  96.0 6.0 %collective-permute-start.15 = (f32[128,256]{1,0:T(8,128)S(1)}, f32[128,256]{1,0:T(8,128)S(1)}, u32[]{:S(2)}, u32[]{:S(2)}) collective-permute-start(f32[128,256]{1,0:T(8,128)S(1)} %get-tuple-element.51), channel_id=1, source_target_pairs={{0,384},{32,416},{64,448},{96,480},{128,256},{160,288},{192,320},{... | collective-permute-start | bytes 393224 | tf_op jit(solution)/shard_map/ppermute | solution.py:57
  102.0 3.0 %collective-permute-start.14 = (f32[128,256]{1,0:T(8,128)S(1)}, f32[128,256]{1,0:T(8,128)S(1)}, u32[]{:S(2)}, u32[]{:S(2)}) collective-permute-start(f32[128,256]{1,0:T(8,128)S(1)} %get-tuple-element.52), channel_id=1, source_target_pairs={{0,256},{32,288},{64,320},{96,352},{128,384},{160,416},{192,448},{... | collective-permute-start | bytes 393224 | tf_op jit(solution)/shard_map/ppermute | solution.py:57
  105.7 6.8 %collective-permute-done.15 = f32[128,256]{1,0:T(8,128)S(1)} collective-permute-done((f32[128,256]{1,0:T(8,128)S(1)}, f32[128,256]{1,0:T(8,128)S(1)}, u32[]{:S(2)}, u32[]{:S(2)}) %collective-permute-start.15) | collective-permute-done | bytes 131104 | tf_op jit(solution)/shard_map/ppermute | solution.py:57
  112.5 2.1 collective-permute-done.14
  114.6 4.4 %collective-permute-start.18 = (f32[128,256]{1,0:T(8,128)S(1)}, f32[128,256]{1,0:T(8,128)S(1)}, u32[]{:S(2)}, u32[]{:S(2)}) collective-permute-start(f32[128,256]{1,0:T(8,128)S(1)} %add_add_fusion.1), channel_id=1, source_target_pairs={{0,384},{32,416},{64,448},{96,480},{128,256},{160,288},{192,320},{... | collective-permute-start | bytes 393224 | tf_op jit(solution)/shard_map/ppermute | solution.py:64
  119.1 3.9 %collective-permute-start.17 = (f32[128,256]{1,0:T(8,128)S(1)}, f32[128,256]{1,0:T(8,128)S(1)}, u32[]{:S(2)}, u32[]{:S(2)}) collective-permute-start(f32[128,256]{1,0:T(8,128)S(1)} %add_add_fusion.1), channel_id=1, source_target_pairs={{0,256},{32,288},{64,320},{96,352},{128,384},{160,416},{192,448},{... | collective-permute-start | bytes 393224 | tf_op jit(solution)/shard_map/ppermute | solution.py:64
  123.0 3.9 %collective-permute-start.16 = (f32[128,256]{1,0:T(8,128)S(1)}, f32[128,256]{1,0:T(8,128)S(1)}, u32[]{:S(2)}, u32[]{:S(2)}) collective-permute-start(f32[128,256]{1,0:T(8,128)S(1)} %add_add_fusion.1), channel_id=1, source_target_pairs={{0,128},{32,160},{64,192},{96,224},{128,0},{160,32},{192,64},{224,... | collective-permute-start | bytes 393224 | tf_op jit(solution)/shard_map/ppermute | solution.py:64
  126.9 0.7 broadcast_compare_fusion.1
  127.5 5.4 %collective-permute-done.17 = f32[128,256]{1,0:T(8,128)S(1)} collective-permute-done((f32[128,256]{1,0:T(8,128)S(1)}, f32[128,256]{1,0:T(8,128)S(1)}, u32[]{:S(2)}, u32[]{:S(2)}) %collective-permute-start.17) | collective-permute-done | bytes 131104 | tf_op jit(solution)/shard_map/ppermute | solution.py:64
  132.9 3.5 %collective-permute-done.16 = f32[128,256]{1,0:T(8,128)S(1)} collective-permute-done((f32[128,256]{1,0:T(8,128)S(1)}, f32[128,256]{1,0:T(8,128)S(1)}, u32[]{:S(2)}, u32[]{:S(2)}) %collective-permute-start.16) | collective-permute-done | bytes 131104 | tf_op jit(solution)/shard_map/ppermute | solution.py:64
  136.5 1.9 collective-permute-start.21
  138.4 3.5 %collective-permute-start.20 = (f32[512,256]{1,0:T(8,128)S(1)}, f32[512,256]{1,0:T(8,128)S(1)}, u32[]{:S(2)}, u32[]{:S(2)}) collective-permute-start(f32[512,256]{1,0:T(8,128)S(1)} %pad_maximum_fusion), channel_id=1, source_target_pairs={{0,64},{32,96},{64,0},{96,32},{128,192},{160,224},{192,128},{224,1... | collective-permute-start | bytes 1572872 | tf_op jit(solution)/shard_map/ppermute | solution.py:64
  142.0 2.3 collective-permute-start.19
  144.6 7.9 %collective-permute-done.21 = f32[512,256]{1,0:T(8,128)S(1)} collective-permute-done((f32[512,256]{1,0:T(8,128)S(1)}, f32[512,256]{1,0:T(8,128)S(1)}, u32[]{:S(2)}, u32[]{:S(2)}) %collective-permute-start.21) | collective-permute-done | bytes 524320 | tf_op jit(solution)/shard_map/ppermute | solution.py:64
  152.5 11.4 %collective-permute-done.20 = f32[512,256]{1,0:T(8,128)S(1)} collective-permute-done((f32[512,256]{1,0:T(8,128)S(1)}, f32[512,256]{1,0:T(8,128)S(1)}, u32[]{:S(2)}, u32[]{:S(2)}) %collective-permute-start.20) | collective-permute-done | bytes 524320 | tf_op jit(solution)/shard_map/ppermute | solution.py:64
  164.2 1.8 fusion.10
  165.9 1.9 copy.19
  167.8 7.5 %fusion.18 = f32[3,256,256]{1,2,0:T(8,128)S(1)} fusion(f32[2048,256]{1,0:T(8,128)S(1)} %fusion.10, f32[2048,3]{0,1:T(4,128)S(1)} %convert_bitcast_fusion, f32[2048,256]{0,1:T(8,128)} %copy.19), kind=kOutput, calls=%fused_computation.22 | convolution fusion | flops 4833411072 | bytes 5005312 | tf_op jit(solution)/shard_map/mc,ck,cl->mkl/dot_general | solution.py:186
  175.3 0.8 slice_bitcast_fusion.1
  176.1 3.9 %collective-permute-start.23 = (f32[256,256]{0,1:T(8,128)}, f32[256,256]{0,1:T(8,128)S(1)}, u32[]{:S(2)}, u32[]{:S(2)}) collective-permute-start(f32[256,256]{0,1:T(8,128)} %get-tuple-element.44), channel_id=1, source_target_pairs={{0,2},{1,3},{2,4},{3,5},{4,6},{5,7},{6,8},{7,9},{8,10},{9,11},{10,... | collective-permute-start | bytes 786440 | tf_op jit(solution)/shard_map/ppermute | solution.py:102
  180.0 4.4 %collective-permute-start.22 = (f32[256,256]{0,1:T(8,128)}, f32[256,256]{0,1:T(8,128)S(1)}, u32[]{:S(2)}, u32[]{:S(2)}) collective-permute-start(f32[256,256]{0,1:T(8,128)} %get-tuple-element.44), channel_id=1, source_target_pairs={{0,1},{1,2},{2,3},{3,4},{4,5},{5,6},{6,7},{7,8},{8,9},{9,10},{10,1... | collective-permute-start | bytes 786440 | tf_op jit(solution)/shard_map/ppermute | solution.py:102
  184.4 4.0 %collective-permute-start.25 = (f32[256,256]{0,1:T(8,128)}, f32[256,256]{0,1:T(8,128)}, u32[]{:S(2)}, u32[]{:S(2)}) collective-permute-start(f32[256,256]{0,1:T(8,128)} %get-tuple-element.45), channel_id=1, source_target_pairs={{2,0},{3,1},{4,2},{5,3},{6,4},{7,5},{8,6},{9,7},{10,8},{11,9},{12,... | collective-permute-start | bytes 786440 | tf_op jit(solution)/shard_map/ppermute | solution.py:102
  188.4 2.6 %collective-permute-start.24 = (f32[256,256]{0,1:T(8,128)}, f32[256,256]{0,1:T(8,128)}, u32[]{:S(2)}, u32[]{:S(2)}) collective-permute-start(f32[256,256]{0,1:T(8,128)} %get-tuple-element.45), channel_id=1, source_target_pairs={{1,0},{2,1},{3,2},{4,3},{5,4},{6,5},{7,6},{8,7},{9,8},{10,9},{11,1... | collective-permute-start | bytes 786440 | tf_op jit(solution)/shard_map/ppermute | solution.py:102
  194.8 1.1 collective-permute-done.23
  195.9 4.7 %collective-permute-done.22 = f32[256,256]{0,1:T(8,128)S(1)} collective-permute-done((f32[256,256]{0,1:T(8,128)}, f32[256,256]{0,1:T(8,128)S(1)}, u32[]{:S(2)}, u32[]{:S(2)}) %collective-permute-start.22) | collective-permute-done | bytes 262176 | tf_op jit(solution)/shard_map/ppermute | solution.py:102
  200.6 5.8 %collective-permute-done.24 = f32[256,256]{0,1:T(8,128)} collective-permute-done((f32[256,256]{0,1:T(8,128)}, f32[256,256]{0,1:T(8,128)}, u32[]{:S(2)}, u32[]{:S(2)}) %collective-permute-start.24) | collective-permute-done | bytes 262176 | tf_op jit(solution)/shard_map/ppermute | solution.py:102
  206.4 1.1 fusion.38
  207.7 11.7 %cholesky.44 = f32[128,128]{1,0:T(8,128)S(1)} custom-call(f32[128,128]{1,0:T(8,128)S(1)} %fusion.54), custom_call_target="Cholesky" | custom-call | tf_op jit(solution)/shard_map/jit(cholesky)/cholesky | solution.py:89
  219.4 0.6 compare_reduce_fusion.1
  220.1 0.7 fusion.44
  220.7 9.8 %custom-call.6 = f32[1,128,128]{1,2,0:T(8,128)S(1)} custom-call(f32[1,128,128]{2,1,0:T(8,128)S(1)} %fusion.44), custom_call_target="InvertDiagBlocksLowerTriangular" | custom-call | tf_op jit(solution)/shard_map/jit(_solve_triangular)/triangular_solve | solution.py:84
  232.0 11.7 %cholesky.55 = f32[128,128]{1,0:T(8,128)S(1)} custom-call(f32[128,128]{1,0:T(8,128)S(1)} %fusion.52), custom_call_target="Cholesky" | custom-call | tf_op jit(solution)/shard_map/jit(cholesky)/cholesky | solution.py:92
  244.4 0.7 fusion.45
  245.1 9.8 %custom-call.7 = f32[1,128,128]{1,2,0:T(8,128)S(1)} custom-call(f32[1,128,128]{2,1,0:T(8,128)S(1)} %fusion.45), custom_call_target="InvertDiagBlocksLowerTriangular" | custom-call | tf_op jit(solution)/shard_map/jit(_solve_triangular)/triangular_solve | solution.py:84
  255.9 0.8 copy.24
  (73 shorter events, 7.3 us)
Async XLA Ops:
  1.2 11.6 %collective-permute-start.2 = (f32[2,2048]{1,0:T(2,128)S(1)}, f32[2,2048]{1,0:T(2,128)S(1)}, u32[]{:S(2)}, u32[]{:S(2)}) collective-permute-start(f32[2,2048]{1,0:T(2,128)S(1)} %pad_maximum_fusion.2), channel_id=1, source_target_pairs={{0,96},{32,64},{64,32},{96,0},{128,224},{160,192},{192,160},{224,1... | collective-permute-start | bytes 49160 | tf_op jit(solution)/shard_map/ppermute | solution.py:41
  4.9 7.9 %collective-permute-start.1 = (f32[2,2048]{1,0:T(2,128)S(1)}, f32[2,2048]{1,0:T(2,128)S(1)}, u32[]{:S(2)}, u32[]{:S(2)}) collective-permute-start(f32[2,2048]{1,0:T(2,128)S(1)} %pad_maximum_fusion.2), channel_id=1, source_target_pairs={{0,64},{32,96},{64,0},{96,32},{128,192},{160,224},{192,128},{224,1... | collective-permute-start | bytes 49160 | tf_op jit(solution)/shard_map/ppermute | solution.py:41
  7.4 5.4 %collective-permute-start = (f32[2,2048]{1,0:T(2,128)S(1)}, f32[2,2048]{1,0:T(2,128)S(1)}, u32[]{:S(2)}, u32[]{:S(2)}) collective-permute-start(f32[2,2048]{1,0:T(2,128)S(1)} %pad_maximum_fusion.2), channel_id=1, source_target_pairs={{0,32},{32,0},{64,96},{96,64},{128,160},{160,128},{192,224},{224,1... | collective-permute-start | bytes 49160 | tf_op jit(solution)/shard_map/ppermute | solution.py:41
  12.8 18.5 %collective-permute-start.5 = (f32[2,2048]{1,0:T(2,128)S(1)}, f32[2,2048]{1,0:T(2,128)S(1)}, u32[]{:S(2)}, u32[]{:S(2)}) collective-permute-start(f32[2,2048]{1,0:T(2,128)S(1)} %add_add_fusion.3), channel_id=1, source_target_pairs={{0,384},{32,416},{64,448},{96,480},{128,256},{160,288},{192,320},{... | collective-permute-start | bytes 49160 | tf_op jit(solution)/shard_map/ppermute | solution.py:41
  23.2 9.5 %collective-permute-start.4 = (f32[2,2048]{1,0:T(2,128)S(1)}, f32[2,2048]{1,0:T(2,128)S(1)}, u32[]{:S(2)}, u32[]{:S(2)}) collective-permute-start(f32[2,2048]{1,0:T(2,128)S(1)} %add_add_fusion.3), channel_id=1, source_target_pairs={{0,256},{32,288},{64,320},{96,352},{128,384},{160,416},{192,448},{... | collective-permute-start | bytes 49160 | tf_op jit(solution)/shard_map/ppermute | solution.py:41
  25.1 7.6 %collective-permute-start.3 = (f32[2,2048]{1,0:T(2,128)S(1)}, f32[2,2048]{1,0:T(2,128)S(1)}, u32[]{:S(2)}, u32[]{:S(2)}) collective-permute-start(f32[2,2048]{1,0:T(2,128)S(1)} %add_add_fusion.3), channel_id=1, source_target_pairs={{0,128},{32,160},{64,192},{96,224},{128,0},{160,32},{192,64},{224,... | collective-permute-start | bytes 49160 | tf_op jit(solution)/shard_map/ppermute | solution.py:41
  33.9 21.9 %copy-start.1 = (s32[3]{0:T(128)S(1)}, s32[3]{0:T(128)}, u32[]{:S(2)}) copy-start(s32[3]{0:T(128)} %constant.162.clone.1) | copy-start | bytes 40
  35.2 13.7 %collective-permute-start.7 = (f32[64,256]{1,0:T(8,128)S(1)}, f32[64,256]{1,0:T(8,128)S(1)}, u32[]{:S(2)}, u32[]{:S(2)}) collective-permute-start(f32[64,256]{1,0:T(8,128)S(1)} %dynamic-slice_bitcast_fusion), channel_id=1, source_target_pairs={{0,2},{1,3},{2,4},{3,5},{4,6},{5,7},{6,8},{7,9},{8,10},{9,11},{10,... | collective-permute-start | bytes 196616 | tf_op jit(solution)/shard_map/ppermute | solution.py:102
  39.7 9.2 %collective-permute-start.6 = (f32[64,256]{1,0:T(8,128)S(1)}, f32[64,256]{1,0:T(8,128)S(1)}, u32[]{:S(2)}, u32[]{:S(2)}) collective-permute-start(f32[64,256]{1,0:T(8,128)S(1)} %dynamic-slice_bitcast_fusion), channel_id=1, source_target_pairs={{0,1},{1,2},{2,3},{3,4},{4,5},{5,6},{6,7},{7,8},{8,9},{9,10},{10,1... | collective-permute-start | bytes 196616 | tf_op jit(solution)/shard_map/ppermute | solution.py:102
  49.0 7.5 %collective-permute-start.9 = (f32[64,256]{1,0:T(8,128)S(1)}, f32[64,256]{1,0:T(8,128)S(1)}, u32[]{:S(2)}, u32[]{:S(2)}) collective-permute-start(f32[64,256]{1,0:T(8,128)S(1)} %get-tuple-element.53), channel_id=1, source_target_pairs={{2,0},{3,1},{4,2},{5,3},{6,4},{7,5},{8,6},{9,7},{10,8},{11,9},{12,... | collective-permute-start | bytes 196616 | tf_op jit(solution)/shard_map/ppermute | solution.py:102
  53.4 6.2 %collective-permute-start.8 = (f32[64,256]{1,0:T(8,128)S(1)}, f32[64,256]{1,0:T(8,128)S(1)}, u32[]{:S(2)}, u32[]{:S(2)}) collective-permute-start(f32[64,256]{1,0:T(8,128)S(1)} %get-tuple-element.53), channel_id=1, source_target_pairs={{1,0},{2,1},{3,2},{4,3},{5,4},{6,5},{7,6},{8,7},{9,8},{10,9},{11,1... | collective-permute-start | bytes 196616 | tf_op jit(solution)/shard_map/ppermute | solution.py:102
  61.9 7.9 %collective-permute-start.10 = (f32[512,256]{1,0:T(8,128)}, f32[512,256]{1,0:T(8,128)}, u32[]{:S(2)}, u32[]{:S(2)}) collective-permute-start(f32[512,256]{1,0:T(8,128)} %get-tuple-element.41), channel_id=1, source_target_pairs={{0,32},{32,0},{64,96},{96,64},{128,160},{160,128},{192,224},{224,1... | collective-permute-start | bytes 1572872 | tf_op jit(solution)/shard_map/ppermute | solution.py:57
  63.8 15.9 %collective-permute-start.12 = (f32[512,256]{1,0:T(8,128)S(1)}, f32[512,256]{1,0:T(8,128)}, u32[]{:S(2)}, u32[]{:S(2)}) collective-permute-start(f32[512,256]{1,0:T(8,128)S(1)} %get-tuple-element.42), channel_id=1, source_target_pairs={{0,96},{32,64},{64,32},{96,0},{128,224},{160,192},{192,160},{224,1... | collective-permute-start | bytes 1572872 | tf_op jit(solution)/shard_map/ppermute | solution.py:57
  67.4 23.8 %collective-permute-start.11 = (f32[512,256]{1,0:T(8,128)S(1)}, f32[512,256]{1,0:T(8,128)}, u32[]{:S(2)}, u32[]{:S(2)}) collective-permute-start(f32[512,256]{1,0:T(8,128)S(1)} %get-tuple-element.43), channel_id=1, source_target_pairs={{0,64},{32,96},{64,0},{96,32},{128,192},{160,224},{192,128},{224,1... | collective-permute-start | bytes 1572872 | tf_op jit(solution)/shard_map/ppermute | solution.py:57
  92.8 12.9 %collective-permute-start.13 = (f32[128,256]{1,0:T(8,128)S(1)}, f32[128,256]{1,0:T(8,128)S(1)}, u32[]{:S(2)}, u32[]{:S(2)}) collective-permute-start(f32[128,256]{1,0:T(8,128)S(1)} %get-tuple-element.50), channel_id=1, source_target_pairs={{0,128},{32,160},{64,192},{96,224},{128,0},{160,32},{192,64},{224,... | collective-permute-start | bytes 393224 | tf_op jit(solution)/shard_map/ppermute | solution.py:57
  96.0 16.5 %collective-permute-start.15 = (f32[128,256]{1,0:T(8,128)S(1)}, f32[128,256]{1,0:T(8,128)S(1)}, u32[]{:S(2)}, u32[]{:S(2)}) collective-permute-start(f32[128,256]{1,0:T(8,128)S(1)} %get-tuple-element.51), channel_id=1, source_target_pairs={{0,384},{32,416},{64,448},{96,480},{128,256},{160,288},{192,320},{... | collective-permute-start | bytes 393224 | tf_op jit(solution)/shard_map/ppermute | solution.py:57
  102.0 12.6 %collective-permute-start.14 = (f32[128,256]{1,0:T(8,128)S(1)}, f32[128,256]{1,0:T(8,128)S(1)}, u32[]{:S(2)}, u32[]{:S(2)}) collective-permute-start(f32[128,256]{1,0:T(8,128)S(1)} %get-tuple-element.52), channel_id=1, source_target_pairs={{0,256},{32,288},{64,320},{96,352},{128,384},{160,416},{192,448},{... | collective-permute-start | bytes 393224 | tf_op jit(solution)/shard_map/ppermute | solution.py:57
  114.6 12.9 %collective-permute-start.18 = (f32[128,256]{1,0:T(8,128)S(1)}, f32[128,256]{1,0:T(8,128)S(1)}, u32[]{:S(2)}, u32[]{:S(2)}) collective-permute-start(f32[128,256]{1,0:T(8,128)S(1)} %add_add_fusion.1), channel_id=1, source_target_pairs={{0,384},{32,416},{64,448},{96,480},{128,256},{160,288},{192,320},{... | collective-permute-start | bytes 393224 | tf_op jit(solution)/shard_map/ppermute | solution.py:64
  119.1 13.9 %collective-permute-start.17 = (f32[128,256]{1,0:T(8,128)S(1)}, f32[128,256]{1,0:T(8,128)S(1)}, u32[]{:S(2)}, u32[]{:S(2)}) collective-permute-start(f32[128,256]{1,0:T(8,128)S(1)} %add_add_fusion.1), channel_id=1, source_target_pairs={{0,256},{32,288},{64,320},{96,352},{128,384},{160,416},{192,448},{... | collective-permute-start | bytes 393224 | tf_op jit(solution)/shard_map/ppermute | solution.py:64
  123.0 13.4 %collective-permute-start.16 = (f32[128,256]{1,0:T(8,128)S(1)}, f32[128,256]{1,0:T(8,128)S(1)}, u32[]{:S(2)}, u32[]{:S(2)}) collective-permute-start(f32[128,256]{1,0:T(8,128)S(1)} %add_add_fusion.1), channel_id=1, source_target_pairs={{0,128},{32,160},{64,192},{96,224},{128,0},{160,32},{192,64},{224,... | collective-permute-start | bytes 393224 | tf_op jit(solution)/shard_map/ppermute | solution.py:64
  136.5 16.0 %collective-permute-start.21 = (f32[512,256]{1,0:T(8,128)S(1)}, f32[512,256]{1,0:T(8,128)S(1)}, u32[]{:S(2)}, u32[]{:S(2)}) collective-permute-start(f32[512,256]{1,0:T(8,128)S(1)} %pad_maximum_fusion), channel_id=1, source_target_pairs={{0,96},{32,64},{64,32},{96,0},{128,224},{160,192},{192,160},{224,1... | collective-permute-start | bytes 1572872 | tf_op jit(solution)/shard_map/ppermute | solution.py:64
  138.4 25.4 %collective-permute-start.20 = (f32[512,256]{1,0:T(8,128)S(1)}, f32[512,256]{1,0:T(8,128)S(1)}, u32[]{:S(2)}, u32[]{:S(2)}) collective-permute-start(f32[512,256]{1,0:T(8,128)S(1)} %pad_maximum_fusion), channel_id=1, source_target_pairs={{0,64},{32,96},{64,0},{96,32},{128,192},{160,224},{192,128},{224,1... | collective-permute-start | bytes 1572872 | tf_op jit(solution)/shard_map/ppermute | solution.py:64
  142.0 21.9 %collective-permute-start.19 = (f32[512,256]{1,0:T(8,128)S(1)}, f32[512,256]{1,0:T(8,128)S(1)}, u32[]{:S(2)}, u32[]{:S(2)}) collective-permute-start(f32[512,256]{1,0:T(8,128)S(1)} %pad_maximum_fusion), channel_id=1, source_target_pairs={{0,32},{32,0},{64,96},{96,64},{128,160},{160,128},{192,224},{224,1... | collective-permute-start | bytes 1572872 | tf_op jit(solution)/shard_map/ppermute | solution.py:64
  167.8 25.8 %copy-start.2 = (s32[64]{0:T(128)S(1)}, s32[64]{0:T(128)}, u32[]{:S(2)}) copy-start(s32[64]{0:T(128)} %param.11) | copy-start | bytes 772
  176.1 19.8 %collective-permute-start.23 = (f32[256,256]{0,1:T(8,128)}, f32[256,256]{0,1:T(8,128)S(1)}, u32[]{:S(2)}, u32[]{:S(2)}) collective-permute-start(f32[256,256]{0,1:T(8,128)} %get-tuple-element.44), channel_id=1, source_target_pairs={{0,2},{1,3},{2,4},{3,5},{4,6},{5,7},{6,8},{7,9},{8,10},{9,11},{10,... | collective-permute-start | bytes 786440 | tf_op jit(solution)/shard_map/ppermute | solution.py:102
  180.0 20.6 %collective-permute-start.22 = (f32[256,256]{0,1:T(8,128)}, f32[256,256]{0,1:T(8,128)S(1)}, u32[]{:S(2)}, u32[]{:S(2)}) collective-permute-start(f32[256,256]{0,1:T(8,128)} %get-tuple-element.44), channel_id=1, source_target_pairs={{0,1},{1,2},{2,3},{3,4},{4,5},{5,6},{6,7},{7,8},{8,9},{9,10},{10,1... | collective-permute-start | bytes 786440 | tf_op jit(solution)/shard_map/ppermute | solution.py:102
  184.4 16.2 %collective-permute-start.25 = (f32[256,256]{0,1:T(8,128)}, f32[256,256]{0,1:T(8,128)}, u32[]{:S(2)}, u32[]{:S(2)}) collective-permute-start(f32[256,256]{0,1:T(8,128)} %get-tuple-element.45), channel_id=1, source_target_pairs={{2,0},{3,1},{4,2},{5,3},{6,4},{7,5},{8,6},{9,7},{10,8},{11,9},{12,... | collective-permute-start | bytes 786440 | tf_op jit(solution)/shard_map/ppermute | solution.py:102
  188.4 18.0 %collective-permute-start.24 = (f32[256,256]{0,1:T(8,128)}, f32[256,256]{0,1:T(8,128)}, u32[]{:S(2)}, u32[]{:S(2)}) collective-permute-start(f32[256,256]{0,1:T(8,128)} %get-tuple-element.45), channel_id=1, source_target_pairs={{1,0},{2,1},{3,2},{4,3},{5,4},{6,5},{7,6},{8,7},{9,8},{10,9},{11,1... | collective-permute-start | bytes 786440 | tf_op jit(solution)/shard_map/ppermute | solution.py:102
  200.6 5.8 %copy-start = (f32[256,256]{0,1:T(8,128)}, f32[256,256]{0,1:T(8,128)S(1)}, u32[]{:S(2)}) copy-start(f32[256,256]{0,1:T(8,128)S(1)} %collective-permute-done.22) | copy-start | bytes 786436

commit v3 on v1

--- a/solution.py
+++ b/solution.py
@@ -52,6 +52,28 @@
         high = (place & mask) != 0
         x = jnp.where(high, jnp.concatenate([got, x], 0), jnp.concatenate([x, got], 0))
     return x
+
+
+def dot_hi(a, b):
+    return jnp.dot(a, b, precision=lax.Precision.HIGHEST, preferred_element_type=jnp.float32)
+
+
+def lower_inverse(lower):
+    eye = jnp.eye(lower.shape[0], dtype=lower.dtype)
+    return jax.scipy.linalg.solve_triangular(lower, eye, lower=True)
+
+
+def basis_rows(gram, rows):
+    half = gram.shape[0] // 2
+    l11 = jnp.linalg.cholesky(gram[:half, :half])
+    m11 = lower_inverse(l11)
+    l21 = dot_hi(gram[half:, :half], m11.T)
+    l22 = jnp.linalg.cholesky(gram[half:, half:] - dot_hi(l21, l21.T))
+    m22 = lower_inverse(l22)
+    m21 = -dot_hi(m22, dot_hi(l21, m11))
+    left = dot_hi(rows[:, :half], m11.T)
+    right = dot_hi(rows[:, :half], m21.T) + dot_hi(rows[:, half:], m22.T)
+    return jnp.concatenate([left, right], 1)
 
 
 def shift(x, axis, count, step):
@@ -156,8 +178,7 @@
     gram = gram + jnp.where(my_slot == last_slot, tail_in, 0.0)
     my_block = first_block + my_slot
     gram = gram / (block_units[my_block] * UNIT).astype(jnp.float32)
-    factor = jnp.linalg.cholesky(gram)
-    return jax.scipy.linalg.solve_triangular(factor, my_rows.T, lower=True).T
+    return basis_rows(gram, my_rows)
 
 
 def solution(mesh):

time: 263 us -> 246 us (0.935)
  other arithmetic: 67.3 us -> 58.9 us
  local copies, waits for them, and re-layouts: 13.2 us -> 7.48 us
    another operation x15, other arithmetic: 56.8 us -> 47.3 us  [the longest x4 20.9 us: lower_inverse(): return jax.scipy.linalg.solve_triangular(lower, eye, lower=True)]
    another operation x19 -> x1, local copies, waits for them, and re-layouts: 5.89 us -> 0.1 us
where the time goes in v3:
time: 246 us; the launch traced here: 245 us
  starting transfers between devices  79.4 us (32%)
  waiting for transfers between devices  76.5 us (31%)
  other arithmetic  58.9 us (24%)
  matrix products  11.9 us (5%)
  between operations  10.9 us (4%)
  local copies, waits for them, and re-layouts  7.48 us (3%)
    ppermute x4, waiting for transfers between devices, halving_allreduce(): x = keep + lax.ppermute(send, axis, [(j, j ^ mask) for j in range(count)])  32.5 us
    ppermute x8, starting transfers between devices, shift(): return lax.ppermute(x, axis, pairs)  29.6 us
    ppermute x4, waiting for transfers between devices, halving_allreduce(): got = lax.ppermute(x, axis, [(j, j ^ mask) for j in range(count)])  26.3 us
    ppermute x4, starting transfers between devices, xor_allreduce(): x = x + lax.ppermute(x, axis, [(j, j ^ mask) for j in range(count)])  21.6 us
    another operation x4, other arithmetic, lower_inverse(): return jax.scipy.linalg.solve_triangular(lower, eye, lower=True)  20.9 us
    ppermute x4, starting transfers between devices, halving_allreduce(): x = keep + lax.ppermute(send, axis, [(j, j ^ mask) for j in range(count)])  17.2 us
    ppermute x8, waiting for transfers between devices, shift(): return lax.ppermute(x, axis, pairs)  14.5 us
    another operation x3, other arithmetic, basis_rows(): l11 = jnp.linalg.cholesky(gram[:half, :half])  12.4 us
  transfers between devices with their start and end apart: 20, of which 14 were waited for; matrix products, arithmetic and copies ran while one was open for 3% of the time, Pallas kernels for 0%

profile of v3, /device:TPU:6, one launch (start us, length us, event | category | flops | bytes accessed | tf_op | source)
XLA Modules:
  0.0 245.1 jit_solution(11009699234954965859)
XLA Ops:
  0.0 1.1 convert_reduce_fusion
  1.2 1.9 collective-permute-start
  3.1 0.7 multiply_bitcast_fusion
  4.1 0.7 multiply_subtract_fusion
  4.9 0.6 fusion.71
  5.5 0.6 broadcast_compare_fusion.2
  6.3 4.3 %collective-permute-start.1 = (f32[2,2048]{1,0:T(2,128)S(1)}, f32[2,2048]{1,0:T(2,128)S(1)}, u32[]{:S(2)}, u32[]{:S(2)}) collective-permute-start(f32[2,2048]{1,0:T(2,128)S(1)} %fusion.70), channel_id=1, source_target_pairs={{0,64},{32,96},{64,0},{96,32},{128,192},{160,224},{192,128},{224,1... | collective-permute-start | bytes 49160 | tf_op jit(solution)/shard_map/ppermute | solution.py:31
  10.8 1.5 collective-permute-done.1
  12.3 6.1 %collective-permute-start.2 = (f32[2,2048]{1,0:T(2,128)S(1)}, f32[2,2048]{1,0:T(2,128)S(1)}, u32[]{:S(2)}, u32[]{:S(2)}) collective-permute-start(f32[2,2048]{1,0:T(2,128)S(1)} %fusion.83), channel_id=1, source_target_pairs={{0,128},{32,160},{64,192},{96,224},{128,0},{160,32},{192,64},{224,... | collective-permute-start | bytes 49160 | tf_op jit(solution)/shard_map/ppermute | solution.py:31
  18.4 1.7 collective-permute-done.2
  20.1 9.3 %collective-permute-start.3 = (f32[2,2048]{1,0:T(2,128)S(1)}, f32[2,2048]{1,0:T(2,128)S(1)}, u32[]{:S(2)}, u32[]{:S(2)}) collective-permute-start(f32[2,2048]{1,0:T(2,128)S(1)} %add.178), channel_id=1, source_target_pairs={{0,256},{32,288},{64,320},{96,352},{128,384},{160,416},{192,448},{... | collective-permute-start | bytes 49160 | tf_op jit(solution)/shard_map/ppermute | solution.py:31
  31.5 1.1 multiply_convert_fusion
  32.6 1.3 fusion.14
  33.9 4.5 %collective-permute-start.5 = (f32[64,256]{1,0:T(8,128)S(1)}, f32[64,256]{1,0:T(8,128)S(1)}, u32[]{:S(2)}, u32[]{:S(2)}) collective-permute-start(f32[64,256]{1,0:T(8,128)S(1)} %dynamic-slice_bitcast_fusion), channel_id=1, source_target_pairs={{0,2},{1,3},{2,4},{3,5},{4,6},{5,7},{6,8},{7,9},{8,10},{9,11},{10,... | collective-permute-start | bytes 196616 | tf_op jit(solution)/shard_map/ppermute | solution.py:81
  38.5 3.5 %collective-permute-start.4 = (f32[64,256]{1,0:T(8,128)S(1)}, f32[64,256]{1,0:T(8,128)S(1)}, u32[]{:S(2)}, u32[]{:S(2)}) collective-permute-start(f32[64,256]{1,0:T(8,128)S(1)} %dynamic-slice_bitcast_fusion), channel_id=1, source_target_pairs={{0,1},{1,2},{2,3},{3,4},{4,5},{5,6},{6,7},{7,8},{8,9},{9,10},{10,1... | collective-permute-start | bytes 196616 | tf_op jit(solution)/shard_map/ppermute | solution.py:81
  42.0 0.7 constant_dynamic-slice_fusion.1
  47.7 4.4 %collective-permute-start.7 = (f32[64,256]{1,0:T(8,128)S(1)}, f32[64,256]{1,0:T(8,128)S(1)}, u32[]{:S(2)}, u32[]{:S(2)}) collective-permute-start(f32[64,256]{1,0:T(8,128)S(1)} %get-tuple-element.39), channel_id=1, source_target_pairs={{2,0},{3,1},{4,2},{5,3},{6,4},{7,5},{8,6},{9,7},{10,8},{11,9},{12,... | collective-permute-start | bytes 196616 | tf_op jit(solution)/shard_map/ppermute | solution.py:81
  52.1 2.4 collective-permute-start.6
  54.5 0.7 and_reduce_fusion
  55.2 3.1 %collective-permute-done.6 = f32[64,256]{1,0:T(8,128)S(1)} collective-permute-done((f32[64,256]{1,0:T(8,128)S(1)}, f32[64,256]{1,0:T(8,128)S(1)}, u32[]{:S(2)}, u32[]{:S(2)}) %collective-permute-start.6) | collective-permute-done | bytes 65568 | tf_op jit(solution)/shard_map/ppermute | solution.py:81
  58.3 0.7 fusion.47
  58.9 0.8 convolution_bitcast_fusion
  59.8 1.9 collective-permute-start.8
  61.8 2.8 %collective-permute-done.8 = f32[1024,256]{1,0:T(8,128)} collective-permute-done((f32[1024,256]{1,0:T(8,128)S(1)}, f32[1024,256]{1,0:T(8,128)}, u32[]{:S(2)}, u32[]{:S(2)}) %collective-permute-start.8) | collective-permute-done | bytes 1048608 | tf_op jit(solution)/shard_map/ppermute | solution.py:49
  64.5 1.4 select_add_fusion
  66.0 3.4 %collective-permute-start.9 = (f32[512,256]{1,0:T(8,128)S(1)}, f32[512,256]{1,0:T(8,128)S(1)}, u32[]{:S(2)}, u32[]{:S(2)}) collective-permute-start(f32[512,256]{1,0:T(8,128)S(1)} %slice_select_fusion.1), channel_id=1, source_target_pairs={{0,64},{32,96},{64,0},{96,32},{128,192},{160,224},{192,128},{224,1... | collective-permute-start | bytes 1572872 | tf_op jit(solution)/shard_map/ppermute | solution.py:49
  69.4 12.5 %collective-permute-done.9 = f32[512,256]{1,0:T(8,128)S(1)} collective-permute-done((f32[512,256]{1,0:T(8,128)S(1)}, f32[512,256]{1,0:T(8,128)S(1)}, u32[]{:S(2)}, u32[]{:S(2)}) %collective-permute-start.9) | collective-permute-done | bytes 524320 | tf_op jit(solution)/shard_map/ppermute | solution.py:49
  82.0 4.3 %collective-permute-start.10 = (f32[256,256]{1,0:T(8,128)S(1)}, f32[256,256]{1,0:T(8,128)S(1)}, u32[]{:S(2)}, u32[]{:S(2)}) collective-permute-start(f32[256,256]{1,0:T(8,128)S(1)} %slice_select_fusion.2), channel_id=1, source_target_pairs={{0,128},{32,160},{64,192},{96,224},{128,0},{160,32},{192,64},{224,... | collective-permute-start | bytes 786440 | tf_op jit(solution)/shard_map/ppermute | solution.py:49
  86.4 11.6 %collective-permute-done.10 = f32[256,256]{1,0:T(8,128)S(1)} collective-permute-done((f32[256,256]{1,0:T(8,128)S(1)}, f32[256,256]{1,0:T(8,128)S(1)}, u32[]{:S(2)}, u32[]{:S(2)}) %collective-permute-start.10) | collective-permute-done | bytes 262176 | tf_op jit(solution)/shard_map/ppermute | solution.py:49
  98.0 7.6 %collective-permute-start.11 = (f32[128,256]{1,0:T(8,128)S(1)}, f32[128,256]{1,0:T(8,128)S(1)}, u32[]{:S(2)}, u32[]{:S(2)}) collective-permute-start(f32[128,256]{1,0:T(8,128)S(1)} %slice_select_fusion.3), channel_id=1, source_target_pairs={{0,256},{32,288},{64,320},{96,352},{128,384},{160,416},{192,448},{... | collective-permute-start | bytes 393224 | tf_op jit(solution)/shard_map/ppermute | solution.py:49
  105.6 5.7 %collective-permute-done.11 = f32[128,256]{1,0:T(8,128)S(1)} collective-permute-done((f32[128,256]{1,0:T(8,128)S(1)}, f32[128,256]{1,0:T(8,128)S(1)}, u32[]{:S(2)}, u32[]{:S(2)}) %collective-permute-start.11) | collective-permute-done | bytes 131104 | tf_op jit(solution)/shard_map/ppermute | solution.py:49
  111.3 5.1 %collective-permute-start.12 = (f32[128,256]{1,0:T(8,128)S(1)}, f32[128,256]{1,0:T(8,128)S(1)}, u32[]{:S(2)}, u32[]{:S(2)}) collective-permute-start(f32[128,256]{1,0:T(8,128)S(1)} %select_add_fusion.3), channel_id=1, source_target_pairs={{0,256},{32,288},{64,320},{96,352},{128,384},{160,416},{192,448},{... | collective-permute-start | bytes 393224 | tf_op jit(solution)/shard_map/ppermute | solution.py:51
  116.4 5.6 %collective-permute-done.12 = f32[128,256]{1,0:T(8,128)S(1)} collective-permute-done((f32[128,256]{1,0:T(8,128)S(1)}, f32[128,256]{1,0:T(8,128)S(1)}, u32[]{:S(2)}, u32[]{:S(2)}) %collective-permute-start.12) | collective-permute-done | bytes 131104 | tf_op jit(solution)/shard_map/ppermute | solution.py:51
  122.1 1.9 collective-permute-start.13
  124.0 10.5 %collective-permute-done.13 = f32[256,256]{1,0:T(8,128)S(1)} collective-permute-done((f32[256,256]{1,0:T(8,128)S(1)}, f32[256,256]{1,0:T(8,128)S(1)}, u32[]{:S(2)}, u32[]{:S(2)}) %collective-permute-start.13) | collective-permute-done | bytes 262176 | tf_op jit(solution)/shard_map/ppermute | solution.py:51
  134.6 1.9 collective-permute-start.14
  136.5 9.2 %collective-permute-done.14 = f32[512,256]{1,0:T(8,128)S(1)} collective-permute-done((f32[512,256]{1,0:T(8,128)S(1)}, f32[512,256]{1,0:T(8,128)S(1)}, u32[]{:S(2)}, u32[]{:S(2)}) %collective-permute-start.14) | collective-permute-done | bytes 524320 | tf_op jit(solution)/shard_map/ppermute | solution.py:51
  145.8 2.1 collective-permute-start.15
  147.9 0.6 dynamic_slice.34
  148.5 0.6 broadcast_compare_fusion.1
  149.4 0.9 collective-permute-done.15
  150.3 1.0 copy-done
  151.3 3.0 %fusion.11 = f32[2048,256]{1,0:T(8,128)S(1)} fusion(f32[1024,256]{1,0:T(8,128)S(1)} %maximum_select_fusion.1, f32[1024,256]{1,0:T(8,128)} %copy-done, s32[]{:T(128)} %bitcast.105, s32[2048]{0:T(1024)S(1)} %add_multiply_fusion, pred[]{:T(512)S(6)} %ne.24), kind=kLoop, calls=%fused_computation.15 | loop fusion | flops 9961472 | bytes 4202501 | tf_op jit(solution)/shard_map/add | solution.py:159
  154.4 1.9 copy.19
  156.2 7.5 %fusion.19 = f32[3,256,256]{1,2,0:T(8,128)S(1)} fusion(f32[2048,256]{1,0:T(8,128)S(1)} %fusion.11, f32[2048,3]{0,1:T(4,128)S(1)} %convert_bitcast_fusion, f32[2048,256]{0,1:T(8,128)} %copy.19), kind=kOutput, calls=%fused_computation.23 | convolution fusion | flops 4833411072 | bytes 5005312 | tf_op jit(solution)/shard_map/mc,ck,cl->mkl/dot_general | solution.py:165
  163.7 0.9 slice_bitcast_fusion.1
  164.6 3.5 %collective-permute-start.17 = (f32[256,256]{0,1:T(8,128)}, f32[256,256]{0,1:T(8,128)S(1)}, u32[]{:S(2)}, u32[]{:S(2)}) collective-permute-start(f32[256,256]{0,1:T(8,128)} %get-tuple-element.37), channel_id=1, source_target_pairs={{0,2},{1,3},{2,4},{3,5},{4,6},{5,7},{6,8},{7,9},{8,10},{9,11},{10,... | collective-permute-start | bytes 786440 | tf_op jit(solution)/shard_map/ppermute | solution.py:81
  168.1 4.8 %collective-permute-start.16 = (f32[256,256]{0,1:T(8,128)}, f32[256,256]{0,1:T(8,128)S(1)}, u32[]{:S(2)}, u32[]{:S(2)}) collective-permute-start(f32[256,256]{0,1:T(8,128)} %get-tuple-element.37), channel_id=1, source_target_pairs={{0,1},{1,2},{2,3},{3,4},{4,5},{5,6},{6,7},{7,8},{8,9},{9,10},{10,1... | collective-permute-start | bytes 786440 | tf_op jit(solution)/shard_map/ppermute | solution.py:81
  172.9 4.0 %collective-permute-start.19 = (f32[256,256]{0,1:T(8,128)}, f32[256,256]{0,1:T(8,128)}, u32[]{:S(2)}, u32[]{:S(2)}) collective-permute-start(f32[256,256]{0,1:T(8,128)} %get-tuple-element.38), channel_id=1, source_target_pairs={{2,0},{3,1},{4,2},{5,3},{6,4},{7,5},{8,6},{9,7},{10,8},{11,9},{12,... | collective-permute-start | bytes 786440 | tf_op jit(solution)/shard_map/ppermute | solution.py:81
  176.9 2.6 %collective-permute-start.18 = (f32[256,256]{0,1:T(8,128)}, f32[256,256]{0,1:T(8,128)}, u32[]{:S(2)}, u32[]{:S(2)}) collective-permute-start(f32[256,256]{0,1:T(8,128)} %get-tuple-element.38), channel_id=1, source_target_pairs={{1,0},{2,1},{3,2},{4,3},{5,4},{6,5},{7,6},{8,7},{9,8},{10,9},{11,1... | collective-permute-start | bytes 786440 | tf_op jit(solution)/shard_map/ppermute | solution.py:81
  182.1 0.6 dynamic_slice.35
  183.3 1.1 collective-permute-done.17
  184.4 4.9 %collective-permute-done.16 = f32[256,256]{0,1:T(8,128)S(1)} collective-permute-done((f32[256,256]{0,1:T(8,128)}, f32[256,256]{0,1:T(8,128)S(1)}, u32[]{:S(2)}, u32[]{:S(2)}) %collective-permute-start.16) | collective-permute-done | bytes 262176 | tf_op jit(solution)/shard_map/ppermute | solution.py:81
  189.3 5.5 %collective-permute-done.18 = f32[256,256]{0,1:T(8,128)} collective-permute-done((f32[256,256]{0,1:T(8,128)}, f32[256,256]{0,1:T(8,128)}, u32[]{:S(2)}, u32[]{:S(2)}) %collective-permute-start.18) | collective-permute-done | bytes 262176 | tf_op jit(solution)/shard_map/ppermute | solution.py:81
  194.8 1.1 fusion.39
  196.0 11.7 %cholesky.44 = f32[128,128]{1,0:T(8,128)S(1)} custom-call(f32[128,128]{1,0:T(8,128)S(1)} %fusion.55), custom_call_target="Cholesky" | custom-call | tf_op jit(solution)/shard_map/jit(cholesky)/cholesky | solution.py:68
  207.8 0.6 compare_reduce_fusion.1
  208.4 0.7 fusion.45
  209.1 9.8 %custom-call.6 = f32[1,128,128]{1,2,0:T(8,128)S(1)} custom-call(f32[1,128,128]{2,1,0:T(8,128)S(1)} %fusion.45), custom_call_target="InvertDiagBlocksLowerTriangular" | custom-call | tf_op jit(solution)/shard_map/jit(_solve_triangular)/triangular_solve | solution.py:63
  220.4 11.7 %cholesky.55 = f32[128,128]{1,0:T(8,128)S(1)} custom-call(f32[128,128]{1,0:T(8,128)S(1)} %fusion.53), custom_call_target="Cholesky" | custom-call | tf_op jit(solution)/shard_map/jit(cholesky)/cholesky | solution.py:71
  232.1 0.6 compare_reduce_fusion
  232.8 0.7 fusion.46
  233.4 9.8 %custom-call.7 = f32[1,128,128]{1,2,0:T(8,128)S(1)} custom-call(f32[1,128,128]{2,1,0:T(8,128)S(1)} %fusion.46), custom_call_target="InvertDiagBlocksLowerTriangular" | custom-call | tf_op jit(solution)/shard_map/jit(_solve_triangular)/triangular_solve | solution.py:63
  244.3 0.8 copy.24
  (68 shorter events, 4.4 us)
Async XLA Ops:
  1.2 5.1 %collective-permute-start = (f32[2,2048]{1,0:T(2,128)S(1)}, f32[2,2048]{1,0:T(2,128)S(1)}, u32[]{:S(2)}, u32[]{:S(2)}) collective-permute-start(f32[2,2048]{1,0:T(2,128)S(1)} %pad_maximum_fusion.1), channel_id=1, source_target_pairs={{0,32},{32,0},{64,96},{96,64},{128,160},{160,128},{192,224},{224,1... | collective-permute-start | bytes 49160 | tf_op jit(solution)/shard_map/ppermute | solution.py:31
  6.3 6.0 %collective-permute-start.1 = (f32[2,2048]{1,0:T(2,128)S(1)}, f32[2,2048]{1,0:T(2,128)S(1)}, u32[]{:S(2)}, u32[]{:S(2)}) collective-permute-start(f32[2,2048]{1,0:T(2,128)S(1)} %fusion.70), channel_id=1, source_target_pairs={{0,64},{32,96},{64,0},{96,32},{128,192},{160,224},{192,128},{224,1... | collective-permute-start | bytes 49160 | tf_op jit(solution)/shard_map/ppermute | solution.py:31
  12.3 7.8 %collective-permute-start.2 = (f32[2,2048]{1,0:T(2,128)S(1)}, f32[2,2048]{1,0:T(2,128)S(1)}, u32[]{:S(2)}, u32[]{:S(2)}) collective-permute-start(f32[2,2048]{1,0:T(2,128)S(1)} %fusion.83), channel_id=1, source_target_pairs={{0,128},{32,160},{64,192},{96,224},{128,0},{160,32},{192,64},{224,... | collective-permute-start | bytes 49160 | tf_op jit(solution)/shard_map/ppermute | solution.py:31
  20.1 11.2 %collective-permute-start.3 = (f32[2,2048]{1,0:T(2,128)S(1)}, f32[2,2048]{1,0:T(2,128)S(1)}, u32[]{:S(2)}, u32[]{:S(2)}) collective-permute-start(f32[2,2048]{1,0:T(2,128)S(1)} %add.178), channel_id=1, source_target_pairs={{0,256},{32,288},{64,320},{96,352},{128,384},{160,416},{192,448},{... | collective-permute-start | bytes 49160 | tf_op jit(solution)/shard_map/ppermute | solution.py:31
  32.6 21.9 %copy-start.2 = (s32[3]{0:T(128)S(1)}, s32[3]{0:T(128)}, u32[]{:S(2)}) copy-start(s32[3]{0:T(128)} %constant.163.clone.1) | copy-start | bytes 40
  33.9 13.7 %collective-permute-start.5 = (f32[64,256]{1,0:T(8,128)S(1)}, f32[64,256]{1,0:T(8,128)S(1)}, u32[]{:S(2)}, u32[]{:S(2)}) collective-permute-start(f32[64,256]{1,0:T(8,128)S(1)} %dynamic-slice_bitcast_fusion), channel_id=1, source_target_pairs={{0,2},{1,3},{2,4},{3,5},{4,6},{5,7},{6,8},{7,9},{8,10},{9,11},{10,... | collective-permute-start | bytes 196616 | tf_op jit(solution)/shard_map/ppermute | solution.py:81
  38.5 9.3 %collective-permute-start.4 = (f32[64,256]{1,0:T(8,128)S(1)}, f32[64,256]{1,0:T(8,128)S(1)}, u32[]{:S(2)}, u32[]{:S(2)}) collective-permute-start(f32[64,256]{1,0:T(8,128)S(1)} %dynamic-slice_bitcast_fusion), channel_id=1, source_target_pairs={{0,1},{1,2},{2,3},{3,4},{4,5},{5,6},{6,7},{7,8},{8,9},{9,10},{10,1... | collective-permute-start | bytes 196616 | tf_op jit(solution)/shard_map/ppermute | solution.py:81
  47.7 7.5 %collective-permute-start.7 = (f32[64,256]{1,0:T(8,128)S(1)}, f32[64,256]{1,0:T(8,128)S(1)}, u32[]{:S(2)}, u32[]{:S(2)}) collective-permute-start(f32[64,256]{1,0:T(8,128)S(1)} %get-tuple-element.39), channel_id=1, source_target_pairs={{2,0},{3,1},{4,2},{5,3},{6,4},{7,5},{8,6},{9,7},{10,8},{11,9},{12,... | collective-permute-start | bytes 196616 | tf_op jit(solution)/shard_map/ppermute | solution.py:81
  52.1 6.2 %collective-permute-start.6 = (f32[64,256]{1,0:T(8,128)S(1)}, f32[64,256]{1,0:T(8,128)S(1)}, u32[]{:S(2)}, u32[]{:S(2)}) collective-permute-start(f32[64,256]{1,0:T(8,128)S(1)} %get-tuple-element.39), channel_id=1, source_target_pairs={{1,0},{2,1},{3,2},{4,3},{5,4},{6,5},{7,6},{8,7},{9,8},{10,9},{11,1... | collective-permute-start | bytes 196616 | tf_op jit(solution)/shard_map/ppermute | solution.py:81
  59.8 4.7 %collective-permute-start.8 = (f32[1024,256]{1,0:T(8,128)S(1)}, f32[1024,256]{1,0:T(8,128)}, u32[]{:S(2)}, u32[]{:S(2)}) collective-permute-start(f32[1024,256]{1,0:T(8,128)S(1)} %slice_select_fusion), channel_id=1, source_target_pairs={{0,32},{32,0},{64,96},{96,64},{128,160},{160,128},{192,224},{224,1... | collective-permute-start | bytes 3145736 | tf_op jit(solution)/shard_map/ppermute | solution.py:49
  66.0 15.9 %collective-permute-start.9 = (f32[512,256]{1,0:T(8,128)S(1)}, f32[512,256]{1,0:T(8,128)S(1)}, u32[]{:S(2)}, u32[]{:S(2)}) collective-permute-start(f32[512,256]{1,0:T(8,128)S(1)} %slice_select_fusion.1), channel_id=1, source_target_pairs={{0,64},{32,96},{64,0},{96,32},{128,192},{160,224},{192,128},{224,1... | collective-permute-start | bytes 1572872 | tf_op jit(solution)/shard_map/ppermute | solution.py:49
  82.0 15.9 %collective-permute-start.10 = (f32[256,256]{1,0:T(8,128)S(1)}, f32[256,256]{1,0:T(8,128)S(1)}, u32[]{:S(2)}, u32[]{:S(2)}) collective-permute-start(f32[256,256]{1,0:T(8,128)S(1)} %slice_select_fusion.2), channel_id=1, source_target_pairs={{0,128},{32,160},{64,192},{96,224},{128,0},{160,32},{192,64},{224,... | collective-permute-start | bytes 786440 | tf_op jit(solution)/shard_map/ppermute | solution.py:49
  98.0 13.2 %collective-permute-start.11 = (f32[128,256]{1,0:T(8,128)S(1)}, f32[128,256]{1,0:T(8,128)S(1)}, u32[]{:S(2)}, u32[]{:S(2)}) collective-permute-start(f32[128,256]{1,0:T(8,128)S(1)} %slice_select_fusion.3), channel_id=1, source_target_pairs={{0,256},{32,288},{64,320},{96,352},{128,384},{160,416},{192,448},{... | collective-permute-start | bytes 393224 | tf_op jit(solution)/shard_map/ppermute | solution.py:49
  111.3 10.8 %collective-permute-start.12 = (f32[128,256]{1,0:T(8,128)S(1)}, f32[128,256]{1,0:T(8,128)S(1)}, u32[]{:S(2)}, u32[]{:S(2)}) collective-permute-start(f32[128,256]{1,0:T(8,128)S(1)} %select_add_fusion.3), channel_id=1, source_target_pairs={{0,256},{32,288},{64,320},{96,352},{128,384},{160,416},{192,448},{... | collective-permute-start | bytes 393224 | tf_op jit(solution)/shard_map/ppermute | solution.py:51
  122.1 12.4 %collective-permute-start.13 = (f32[256,256]{1,0:T(8,128)S(1)}, f32[256,256]{1,0:T(8,128)S(1)}, u32[]{:S(2)}, u32[]{:S(2)}) collective-permute-start(f32[256,256]{1,0:T(8,128)S(1)} %maximum_select_fusion.3), channel_id=1, source_target_pairs={{0,128},{32,160},{64,192},{96,224},{128,0},{160,32},{192,64},{224,... | collective-permute-start | bytes 786440 | tf_op jit(solution)/shard_map/ppermute | solution.py:51
  134.6 11.1 %collective-permute-start.14 = (f32[512,256]{1,0:T(8,128)S(1)}, f32[512,256]{1,0:T(8,128)S(1)}, u32[]{:S(2)}, u32[]{:S(2)}) collective-permute-start(f32[512,256]{1,0:T(8,128)S(1)} %maximum_select_fusion.2), channel_id=1, source_target_pairs={{0,64},{32,96},{64,0},{96,32},{128,192},{160,224},{192,128},{224,1... | collective-permute-start | bytes 1572872 | tf_op jit(solution)/shard_map/ppermute | solution.py:51
  145.8 4.6 %collective-permute-start.15 = (f32[1024,256]{1,0:T(8,128)S(1)}, f32[1024,256]{1,0:T(8,128)S(1)}, u32[]{:S(2)}, u32[]{:S(2)}) collective-permute-start(f32[1024,256]{1,0:T(8,128)S(1)} %maximum_select_fusion.1), channel_id=1, source_target_pairs={{0,32},{32,0},{64,96},{96,64},{128,160},{160,128},{192,224},{224,1... | collective-permute-start | bytes 3145736 | tf_op jit(solution)/shard_map/ppermute | solution.py:51
  150.3 1.0 copy-start
  156.2 25.8 %copy-start.3 = (s32[64]{0:T(128)S(1)}, s32[64]{0:T(128)}, u32[]{:S(2)}) copy-start(s32[64]{0:T(128)} %param.11) | copy-start | bytes 772
  164.6 19.8 %collective-permute-start.17 = (f32[256,256]{0,1:T(8,128)}, f32[256,256]{0,1:T(8,128)S(1)}, u32[]{:S(2)}, u32[]{:S(2)}) collective-permute-start(f32[256,256]{0,1:T(8,128)} %get-tuple-element.37), channel_id=1, source_target_pairs={{0,2},{1,3},{2,4},{3,5},{4,6},{5,7},{6,8},{7,9},{8,10},{9,11},{10,... | collective-permute-start | bytes 786440 | tf_op jit(solution)/shard_map/ppermute | solution.py:81
  168.1 21.2 %collective-permute-start.16 = (f32[256,256]{0,1:T(8,128)}, f32[256,256]{0,1:T(8,128)S(1)}, u32[]{:S(2)}, u32[]{:S(2)}) collective-permute-start(f32[256,256]{0,1:T(8,128)} %get-tuple-element.37), channel_id=1, source_target_pairs={{0,1},{1,2},{2,3},{3,4},{4,5},{5,6},{6,7},{7,8},{8,9},{9,10},{10,1... | collective-permute-start | bytes 786440 | tf_op jit(solution)/shard_map/ppermute | solution.py:81
  172.9 16.4 %collective-permute-start.19 = (f32[256,256]{0,1:T(8,128)}, f32[256,256]{0,1:T(8,128)}, u32[]{:S(2)}, u32[]{:S(2)}) collective-permute-start(f32[256,256]{0,1:T(8,128)} %get-tuple-element.38), channel_id=1, source_target_pairs={{2,0},{3,1},{4,2},{5,3},{6,4},{7,5},{8,6},{9,7},{10,8},{11,9},{12,... | collective-permute-start | bytes 786440 | tf_op jit(solution)/shard_map/ppermute | solution.py:81
  176.9 17.9 %collective-permute-start.18 = (f32[256,256]{0,1:T(8,128)}, f32[256,256]{0,1:T(8,128)}, u32[]{:S(2)}, u32[]{:S(2)}) collective-permute-start(f32[256,256]{0,1:T(8,128)} %get-tuple-element.38), channel_id=1, source_target_pairs={{1,0},{2,1},{3,2},{4,3},{5,4},{6,5},{7,6},{8,7},{9,8},{10,9},{11,1... | collective-permute-start | bytes 786440 | tf_op jit(solution)/shard_map/ppermute | solution.py:81
  189.3 5.5 %copy-start.1 = (f32[256,256]{0,1:T(8,128)}, f32[256,256]{0,1:T(8,128)S(1)}, u32[]{:S(2)}) copy-start(f32[256,256]{0,1:T(8,128)S(1)} %collective-permute-done.16) | copy-start | bytes 786436

commit v4 on v3

--- a/solution.py
+++ b/solution.py
@@ -33,21 +33,24 @@
     return x
 
 
-def halving_allreduce(x, axis, count):
+def halving_allreduce(x, axis, count, split_masks=2):
     place = lax.axis_index(axis)
     masks = []
     mask = 1
     while mask < count:
         masks.append(mask)
         mask *= 2
-    for mask in masks:
+    split, doubled = masks[:split_masks], masks[split_masks:]
+    for mask in split:
         half = x.shape[0] // 2
         lower, upper = x[:half], x[half:]
         high = (place & mask) != 0
         send = jnp.where(high, lower, upper)
         keep = jnp.where(high, upper, lower)
         x = keep + lax.ppermute(send, axis, [(j, j ^ mask) for j in range(count)])
-    for mask in reversed(masks):
+    for mask in doubled:
+        x = x + lax.ppermute(x, axis, [(j, j ^ mask) for j in range(count)])
+    for mask in reversed(split):
         got = lax.ppermute(x, axis, [(j, j ^ mask) for j in range(count)])
         high = (place & mask) != 0
         x = jnp.where(high, jnp.concatenate([got, x], 0), jnp.concatenate([x, got], 0))

time: 246 us -> 254 us (1.033)
  waiting for transfers between devices: 76.5 us -> 91.5 us
  starting transfers between devices: 79.4 us -> 72.4 us
    ppermute x0 -> x2, waiting for transfers between devices: none -> 45.4 us  [halving_allreduce(): x = x + lax.ppermute(x, axis, [(j, j ^ mask) for j in range(count)])]
    ppermute x4 -> x2, waiting for transfers between devices: 32.5 us -> 15.3 us  [halving_allreduce(): x = keep + lax.ppermute(send, axis, [(j, j ^ mask) for j in range(count)])]
    ppermute x4 -> x2, waiting for transfers between devices: 26.3 us -> 12.9 us  [halving_allreduce(): got = lax.ppermute(x, axis, [(j, j ^ mask) for j in range(count)])]
    ppermute x4 -> x2, starting transfers between devices: 17.2 us -> 5.29 us  [halving_allreduce(): x = keep + lax.ppermute(send, axis, [(j, j ^ mask) for j in range(count)])]
    ppermute x0 -> x2, starting transfers between devices: none -> 11.9 us  [halving_allreduce(): x = x + lax.ppermute(x, axis, [(j, j ^ mask) for j in range(count)])]
    ppermute x4 -> x2, starting transfers between devices: 11.1 us -> 4.02 us  [halving_allreduce(): got = lax.ppermute(x, axis, [(j, j ^ mask) for j in range(count)])]
  transfers between devices with their start and end apart: 20 -> 18, of which waited for: 14 -> 12; matrix products, arithmetic and copies ran while one was open for 3% -> 3% of each run, Pallas kernels for 0% -> 0%
where the time goes in v4:
time: 254 us; the launch traced here: 253 us
  waiting for transfers between devices  91.5 us (36%)
  starting transfers between devices  72.4 us (29%)
  other arithmetic  58.6 us (23%)
  matrix products  11.9 us (5%)
  between operations  10.8 us (4%)
  local copies, waits for them, and re-layouts  7.48 us (3%)
    ppermute x2, waiting for transfers between devices, halving_allreduce(): x = x + lax.ppermute(x, axis, [(j, j ^ mask) for j in range(count)])  45.4 us
    ppermute x8, starting transfers between devices, shift(): return lax.ppermute(x, axis, pairs)  29.6 us
    ppermute x4, starting transfers between devices, xor_allreduce(): x = x + lax.ppermute(x, axis, [(j, j ^ mask) for j in range(count)])  21.6 us
    another operation x4, other arithmetic, lower_inverse(): return jax.scipy.linalg.solve_triangular(lower, eye, lower=True)  20.9 us
    ppermute x2, waiting for transfers between devices, halving_allreduce(): x = keep + lax.ppermute(send, axis, [(j, j ^ mask) for j in range(count)])  15.3 us
    ppermute x8, waiting for transfers between devices, shift(): return lax.ppermute(x, axis, pairs)  14.6 us
    ppermute x2, waiting for transfers between devices, halving_allreduce(): got = lax.ppermute(x, axis, [(j, j ^ mask) for j in range(count)])  12.9 us
    another operation x3, other arithmetic, basis_rows(): l11 = jnp.linalg.cholesky(gram[:half, :half])  12.4 us
  transfers between devices with their start and end apart: 18, of which 12 were waited for; matrix products, arithmetic and copies ran while one was open for 3% of the time, Pallas kernels for 0%

profile of v4, /device:TPU:6, one launch (start us, length us, event | category | flops | bytes accessed | tf_op | source)
XLA Modules:
  0.0 252.7 jit_solution(12548334367296819063)
XLA Ops:
  0.0 1.1 convert_reduce_fusion
  1.2 1.9 collective-permute-start
  3.1 0.7 multiply_bitcast_fusion
  4.1 0.7 multiply_subtract_fusion
  4.9 0.6 fusion.71
  5.5 0.6 broadcast_compare_fusion.2
  6.3 4.3 %collective-permute-start.1 = (f32[2,2048]{1,0:T(2,128)S(1)}, f32[2,2048]{1,0:T(2,128)S(1)}, u32[]{:S(2)}, u32[]{:S(2)}) collective-permute-start(f32[2,2048]{1,0:T(2,128)S(1)} %fusion.70), channel_id=1, source_target_pairs={{0,64},{32,96},{64,0},{96,32},{128,192},{160,224},{192,128},{224,1... | collective-permute-start | bytes 49160 | tf_op jit(solution)/shard_map/ppermute | solution.py:31
  10.8 1.5 collective-permute-done.1
  12.3 6.1 %collective-permute-start.2 = (f32[2,2048]{1,0:T(2,128)S(1)}, f32[2,2048]{1,0:T(2,128)S(1)}, u32[]{:S(2)}, u32[]{:S(2)}) collective-permute-start(f32[2,2048]{1,0:T(2,128)S(1)} %fusion.83), channel_id=1, source_target_pairs={{0,128},{32,160},{64,192},{96,224},{128,0},{160,32},{192,64},{224,... | collective-permute-start | bytes 49160 | tf_op jit(solution)/shard_map/ppermute | solution.py:31
  18.4 1.7 collective-permute-done.2
  20.1 9.3 %collective-permute-start.3 = (f32[2,2048]{1,0:T(2,128)S(1)}, f32[2,2048]{1,0:T(2,128)S(1)}, u32[]{:S(2)}, u32[]{:S(2)}) collective-permute-start(f32[2,2048]{1,0:T(2,128)S(1)} %add.178), channel_id=1, source_target_pairs={{0,256},{32,288},{64,320},{96,352},{128,384},{160,416},{192,448},{... | collective-permute-start | bytes 49160 | tf_op jit(solution)/shard_map/ppermute | solution.py:31
  31.5 1.1 multiply_convert_fusion
  32.6 1.3 fusion.14
  33.9 4.5 %collective-permute-start.5 = (f32[64,256]{1,0:T(8,128)S(1)}, f32[64,256]{1,0:T(8,128)S(1)}, u32[]{:S(2)}, u32[]{:S(2)}) collective-permute-start(f32[64,256]{1,0:T(8,128)S(1)} %dynamic-slice_bitcast_fusion), channel_id=1, source_target_pairs={{0,2},{1,3},{2,4},{3,5},{4,6},{5,7},{6,8},{7,9},{8,10},{9,11},{10,... | collective-permute-start | bytes 196616 | tf_op jit(solution)/shard_map/ppermute | solution.py:84
  38.5 3.5 %collective-permute-start.4 = (f32[64,256]{1,0:T(8,128)S(1)}, f32[64,256]{1,0:T(8,128)S(1)}, u32[]{:S(2)}, u32[]{:S(2)}) collective-permute-start(f32[64,256]{1,0:T(8,128)S(1)} %dynamic-slice_bitcast_fusion), channel_id=1, source_target_pairs={{0,1},{1,2},{2,3},{3,4},{4,5},{5,6},{6,7},{7,8},{8,9},{9,10},{10,1... | collective-permute-start | bytes 196616 | tf_op jit(solution)/shard_map/ppermute | solution.py:84
  42.0 0.7 constant_dynamic-slice_fusion.1
  47.7 4.4 %collective-permute-start.7 = (f32[64,256]{1,0:T(8,128)S(1)}, f32[64,256]{1,0:T(8,128)S(1)}, u32[]{:S(2)}, u32[]{:S(2)}) collective-permute-start(f32[64,256]{1,0:T(8,128)S(1)} %get-tuple-element.39), channel_id=1, source_target_pairs={{2,0},{3,1},{4,2},{5,3},{6,4},{7,5},{8,6},{9,7},{10,8},{11,9},{12,... | collective-permute-start | bytes 196616 | tf_op jit(solution)/shard_map/ppermute | solution.py:84
  52.1 2.4 collective-permute-start.6
  54.5 0.7 and_reduce_fusion
  55.2 3.1 %collective-permute-done.6 = f32[64,256]{1,0:T(8,128)S(1)} collective-permute-done((f32[64,256]{1,0:T(8,128)S(1)}, f32[64,256]{1,0:T(8,128)S(1)}, u32[]{:S(2)}, u32[]{:S(2)}) %collective-permute-start.6) | collective-permute-done | bytes 65568 | tf_op jit(solution)/shard_map/ppermute | solution.py:84
  58.3 0.7 fusion.47
  58.9 0.8 convolution_bitcast_fusion
  59.7 1.1 slice_select_fusion
  60.8 1.9 collective-permute-start.8
  62.8 2.8 %collective-permute-done.8 = f32[1024,256]{1,0:T(8,128)S(1)} collective-permute-done((f32[1024,256]{1,0:T(8,128)}, f32[1024,256]{1,0:T(8,128)S(1)}, u32[]{:S(2)}, u32[]{:S(2)}) %collective-permute-start.8) | collective-permute-done | bytes 1048608 | tf_op jit(solution)/shard_map/ppermute | solution.py:50
  65.9 3.4 %collective-permute-start.9 = (f32[512,256]{1,0:T(8,128)S(1)}, f32[512,256]{1,0:T(8,128)S(1)}, u32[]{:S(2)}, u32[]{:S(2)}) collective-permute-start(f32[512,256]{1,0:T(8,128)S(1)} %slice_select_fusion.1), channel_id=1, source_target_pairs={{0,64},{32,96},{64,0},{96,32},{128,192},{160,224},{192,128},{224,1... | collective-permute-start | bytes 1572872 | tf_op jit(solution)/shard_map/ppermute | solution.py:50
  69.3 12.5 %collective-permute-done.9 = f32[512,256]{1,0:T(8,128)S(1)} collective-permute-done((f32[512,256]{1,0:T(8,128)S(1)}, f32[512,256]{1,0:T(8,128)S(1)}, u32[]{:S(2)}, u32[]{:S(2)}) %collective-permute-start.9) | collective-permute-done | bytes 524320 | tf_op jit(solution)/shard_map/ppermute | solution.py:50
  81.8 4.3 %collective-permute-start.10 = (f32[512,256]{1,0:T(8,128)S(1)}, f32[512,256]{1,0:T(8,128)S(1)}, u32[]{:S(2)}, u32[]{:S(2)}) collective-permute-start(f32[512,256]{1,0:T(8,128)S(1)} %select_add_fusion.1), channel_id=1, source_target_pairs={{0,128},{32,160},{64,192},{96,224},{128,0},{160,32},{192,64},{224,... | collective-permute-start | bytes 1572872 | tf_op jit(solution)/shard_map/ppermute | solution.py:52
  86.1 22.8 %collective-permute-done.10 = f32[512,256]{1,0:T(8,128)S(1)} collective-permute-done((f32[512,256]{1,0:T(8,128)S(1)}, f32[512,256]{1,0:T(8,128)S(1)}, u32[]{:S(2)}, u32[]{:S(2)}) %collective-permute-start.10) | collective-permute-done | bytes 524320 | tf_op jit(solution)/shard_map/ppermute | solution.py:52
  109.0 7.6 %collective-permute-start.11 = (f32[512,256]{1,0:T(8,128)S(1)}, f32[512,256]{1,0:T(8,128)S(1)}, u32[]{:S(2)}, u32[]{:S(2)}) collective-permute-start(f32[512,256]{1,0:T(8,128)S(1)} %add.196), channel_id=1, source_target_pairs={{0,256},{32,288},{64,320},{96,352},{128,384},{160,416},{192,448},{... | collective-permute-start | bytes 1572872 | tf_op jit(solution)/shard_map/ppermute | solution.py:52
  116.6 22.6 %collective-permute-done.11 = f32[512,256]{1,0:T(8,128)S(1)} collective-permute-done((f32[512,256]{1,0:T(8,128)S(1)}, f32[512,256]{1,0:T(8,128)S(1)}, u32[]{:S(2)}, u32[]{:S(2)}) %collective-permute-start.11) | collective-permute-done | bytes 524320 | tf_op jit(solution)/shard_map/ppermute | solution.py:52
  139.3 1.9 collective-permute-start.12
  141.2 12.0 %collective-permute-done.12 = f32[512,256]{1,0:T(8,128)S(1)} collective-permute-done((f32[512,256]{1,0:T(8,128)S(1)}, f32[512,256]{1,0:T(8,128)S(1)}, u32[]{:S(2)}, u32[]{:S(2)}) %collective-permute-start.12) | collective-permute-done | bytes 524320 | tf_op jit(solution)/shard_map/ppermute | solution.py:54
  153.3 2.1 collective-permute-start.13
  155.4 0.6 dynamic_slice.34
  156.0 0.6 broadcast_compare_fusion.1
  156.9 0.9 collective-permute-done.13
  157.8 1.0 copy-done
  158.8 3.0 %fusion.11 = f32[2048,256]{1,0:T(8,128)S(1)} fusion(f32[1024,256]{1,0:T(8,128)S(1)} %maximum_select_fusion.1, f32[1024,256]{1,0:T(8,128)} %copy-done, s32[]{:T(128)} %bitcast.105, s32[2048]{0:T(1024)S(1)} %add_multiply_fusion, pred[]{:T(512)S(6)} %ne.16), kind=kLoop, calls=%fused_computation.15 | loop fusion | flops 9961472 | bytes 4202501 | tf_op jit(solution)/shard_map/add | solution.py:162
  161.9 1.9 copy.19
  163.7 7.5 %fusion.19 = f32[3,256,256]{1,2,0:T(8,128)S(1)} fusion(f32[2048,256]{1,0:T(8,128)S(1)} %fusion.11, f32[2048,3]{0,1:T(4,128)S(1)} %convert_bitcast_fusion, f32[2048,256]{0,1:T(8,128)} %copy.19), kind=kOutput, calls=%fused_computation.23 | convolution fusion | flops 4833411072 | bytes 5005312 | tf_op jit(solution)/shard_map/mc,ck,cl->mkl/dot_general | solution.py:168
  171.2 0.9 slice_bitcast_fusion.1
  172.1 3.6 %collective-permute-start.15 = (f32[256,256]{0,1:T(8,128)}, f32[256,256]{0,1:T(8,128)S(1)}, u32[]{:S(2)}, u32[]{:S(2)}) collective-permute-start(f32[256,256]{0,1:T(8,128)} %get-tuple-element.37), channel_id=1, source_target_pairs={{0,2},{1,3},{2,4},{3,5},{4,6},{5,7},{6,8},{7,9},{8,10},{9,11},{10,... | collective-permute-start | bytes 786440 | tf_op jit(solution)/shard_map/ppermute | solution.py:84
  175.7 4.7 %collective-permute-start.14 = (f32[256,256]{0,1:T(8,128)}, f32[256,256]{0,1:T(8,128)S(1)}, u32[]{:S(2)}, u32[]{:S(2)}) collective-permute-start(f32[256,256]{0,1:T(8,128)} %get-tuple-element.37), channel_id=1, source_target_pairs={{0,1},{1,2},{2,3},{3,4},{4,5},{5,6},{6,7},{7,8},{8,9},{9,10},{10,1... | collective-permute-start | bytes 786440 | tf_op jit(solution)/shard_map/ppermute | solution.py:84
  180.4 4.0 %collective-permute-start.17 = (f32[256,256]{0,1:T(8,128)}, f32[256,256]{0,1:T(8,128)}, u32[]{:S(2)}, u32[]{:S(2)}) collective-permute-start(f32[256,256]{0,1:T(8,128)} %get-tuple-element.38), channel_id=1, source_target_pairs={{2,0},{3,1},{4,2},{5,3},{6,4},{7,5},{8,6},{9,7},{10,8},{11,9},{12,... | collective-permute-start | bytes 786440 | tf_op jit(solution)/shard_map/ppermute | solution.py:84
  184.4 2.6 %collective-permute-start.16 = (f32[256,256]{0,1:T(8,128)}, f32[256,256]{0,1:T(8,128)}, u32[]{:S(2)}, u32[]{:S(2)}) collective-permute-start(f32[256,256]{0,1:T(8,128)} %get-tuple-element.38), channel_id=1, source_target_pairs={{1,0},{2,1},{3,2},{4,3},{5,4},{6,5},{7,6},{8,7},{9,8},{10,9},{11,1... | collective-permute-start | bytes 786440 | tf_op jit(solution)/shard_map/ppermute | solution.py:84
  189.6 0.6 dynamic_slice.35
  190.8 1.1 collective-permute-done.15
  191.9 4.9 %collective-permute-done.14 = f32[256,256]{0,1:T(8,128)S(1)} collective-permute-done((f32[256,256]{0,1:T(8,128)}, f32[256,256]{0,1:T(8,128)S(1)}, u32[]{:S(2)}, u32[]{:S(2)}) %collective-permute-start.14) | collective-permute-done | bytes 262176 | tf_op jit(solution)/shard_map/ppermute | solution.py:84
  196.8 5.6 %collective-permute-done.16 = f32[256,256]{0,1:T(8,128)} collective-permute-done((f32[256,256]{0,1:T(8,128)}, f32[256,256]{0,1:T(8,128)}, u32[]{:S(2)}, u32[]{:S(2)}) %collective-permute-start.16) | collective-permute-done | bytes 262176 | tf_op jit(solution)/shard_map/ppermute | solution.py:84
  202.4 1.1 fusion.39
  203.6 11.7 %cholesky.44 = f32[128,128]{1,0:T(8,128)S(1)} custom-call(f32[128,128]{1,0:T(8,128)S(1)} %fusion.55), custom_call_target="Cholesky" | custom-call | tf_op jit(solution)/shard_map/jit(cholesky)/cholesky | solution.py:71
  215.4 0.6 compare_reduce_fusion.1
  216.0 0.7 fusion.45
  216.7 9.8 %custom-call.6 = f32[1,128,128]{1,2,0:T(8,128)S(1)} custom-call(f32[1,128,128]{2,1,0:T(8,128)S(1)} %fusion.45), custom_call_target="InvertDiagBlocksLowerTriangular" | custom-call | tf_op jit(solution)/shard_map/jit(_solve_triangular)/triangular_solve | solution.py:66
  226.5 0.3 fusion.43
  226.8 0.3 fusion.50
  228.0 11.7 %cholesky.55 = f32[128,128]{1,0:T(8,128)S(1)} custom-call(f32[128,128]{1,0:T(8,128)S(1)} %fusion.53), custom_call_target="Cholesky" | custom-call | tf_op jit(solution)/shard_map/jit(cholesky)/cholesky | solution.py:74
  239.7 0.6 compare_reduce_fusion
  240.4 0.7 fusion.46
  241.0 9.8 %custom-call.7 = f32[1,128,128]{1,2,0:T(8,128)S(1)} custom-call(f32[1,128,128]{2,1,0:T(8,128)S(1)} %fusion.46), custom_call_target="InvertDiagBlocksLowerTriangular" | custom-call | tf_op jit(solution)/shard_map/jit(_solve_triangular)/triangular_solve | solution.py:66
  250.8 0.3 fusion.41
  251.6 0.3 convolution_add_fusion
  251.9 0.8 copy.24
  (60 shorter events, 3.3 us)
Async XLA Ops:
  1.2 5.1 %collective-permute-start = (f32[2,2048]{1,0:T(2,128)S(1)}, f32[2,2048]{1,0:T(2,128)S(1)}, u32[]{:S(2)}, u32[]{:S(2)}) collective-permute-start(f32[2,2048]{1,0:T(2,128)S(1)} %pad_maximum_fusion.1), channel_id=1, source_target_pairs={{0,32},{32,0},{64,96},{96,64},{128,160},{160,128},{192,224},{224,1... | collective-permute-start | bytes 49160 | tf_op jit(solution)/shard_map/ppermute | solution.py:31
  6.3 6.0 %collective-permute-start.1 = (f32[2,2048]{1,0:T(2,128)S(1)}, f32[2,2048]{1,0:T(2,128)S(1)}, u32[]{:S(2)}, u32[]{:S(2)}) collective-permute-start(f32[2,2048]{1,0:T(2,128)S(1)} %fusion.70), channel_id=1, source_target_pairs={{0,64},{32,96},{64,0},{96,32},{128,192},{160,224},{192,128},{224,1... | collective-permute-start | bytes 49160 | tf_op jit(solution)/shard_map/ppermute | solution.py:31
  12.3 7.8 %collective-permute-start.2 = (f32[2,2048]{1,0:T(2,128)S(1)}, f32[2,2048]{1,0:T(2,128)S(1)}, u32[]{:S(2)}, u32[]{:S(2)}) collective-permute-start(f32[2,2048]{1,0:T(2,128)S(1)} %fusion.83), channel_id=1, source_target_pairs={{0,128},{32,160},{64,192},{96,224},{128,0},{160,32},{192,64},{224,... | collective-permute-start | bytes 49160 | tf_op jit(solution)/shard_map/ppermute | solution.py:31
  20.1 11.2 %collective-permute-start.3 = (f32[2,2048]{1,0:T(2,128)S(1)}, f32[2,2048]{1,0:T(2,128)S(1)}, u32[]{:S(2)}, u32[]{:S(2)}) collective-permute-start(f32[2,2048]{1,0:T(2,128)S(1)} %add.178), channel_id=1, source_target_pairs={{0,256},{32,288},{64,320},{96,352},{128,384},{160,416},{192,448},{... | collective-permute-start | bytes 49160 | tf_op jit(solution)/shard_map/ppermute | solution.py:31
  32.6 21.9 %copy-start.2 = (s32[3]{0:T(128)S(1)}, s32[3]{0:T(128)}, u32[]{:S(2)}) copy-start(s32[3]{0:T(128)} %constant.159.clone.1) | copy-start | bytes 40
  33.9 13.7 %collective-permute-start.5 = (f32[64,256]{1,0:T(8,128)S(1)}, f32[64,256]{1,0:T(8,128)S(1)}, u32[]{:S(2)}, u32[]{:S(2)}) collective-permute-start(f32[64,256]{1,0:T(8,128)S(1)} %dynamic-slice_bitcast_fusion), channel_id=1, source_target_pairs={{0,2},{1,3},{2,4},{3,5},{4,6},{5,7},{6,8},{7,9},{8,10},{9,11},{10,... | collective-permute-start | bytes 196616 | tf_op jit(solution)/shard_map/ppermute | solution.py:84
  38.5 9.3 %collective-permute-start.4 = (f32[64,256]{1,0:T(8,128)S(1)}, f32[64,256]{1,0:T(8,128)S(1)}, u32[]{:S(2)}, u32[]{:S(2)}) collective-permute-start(f32[64,256]{1,0:T(8,128)S(1)} %dynamic-slice_bitcast_fusion), channel_id=1, source_target_pairs={{0,1},{1,2},{2,3},{3,4},{4,5},{5,6},{6,7},{7,8},{8,9},{9,10},{10,1... | collective-permute-start | bytes 196616 | tf_op jit(solution)/shard_map/ppermute | solution.py:84
  47.7 7.5 %collective-permute-start.7 = (f32[64,256]{1,0:T(8,128)S(1)}, f32[64,256]{1,0:T(8,128)S(1)}, u32[]{:S(2)}, u32[]{:S(2)}) collective-permute-start(f32[64,256]{1,0:T(8,128)S(1)} %get-tuple-element.39), channel_id=1, source_target_pairs={{2,0},{3,1},{4,2},{5,3},{6,4},{7,5},{8,6},{9,7},{10,8},{11,9},{12,... | collective-permute-start | bytes 196616 | tf_op jit(solution)/shard_map/ppermute | solution.py:84
  52.1 6.2 %collective-permute-start.6 = (f32[64,256]{1,0:T(8,128)S(1)}, f32[64,256]{1,0:T(8,128)S(1)}, u32[]{:S(2)}, u32[]{:S(2)}) collective-permute-start(f32[64,256]{1,0:T(8,128)S(1)} %get-tuple-element.39), channel_id=1, source_target_pairs={{1,0},{2,1},{3,2},{4,3},{5,4},{6,5},{7,6},{8,7},{9,8},{10,9},{11,1... | collective-permute-start | bytes 196616 | tf_op jit(solution)/shard_map/ppermute | solution.py:84
  60.8 4.8 %collective-permute-start.8 = (f32[1024,256]{1,0:T(8,128)}, f32[1024,256]{1,0:T(8,128)S(1)}, u32[]{:S(2)}, u32[]{:S(2)}) collective-permute-start(f32[1024,256]{1,0:T(8,128)} %slice_select_fusion), channel_id=1, source_target_pairs={{0,32},{32,0},{64,96},{96,64},{128,160},{160,128},{192,224},{224,1... | collective-permute-start | bytes 3145736 | tf_op jit(solution)/shard_map/ppermute | solution.py:50
  65.9 15.9 %collective-permute-start.9 = (f32[512,256]{1,0:T(8,128)S(1)}, f32[512,256]{1,0:T(8,128)S(1)}, u32[]{:S(2)}, u32[]{:S(2)}) collective-permute-start(f32[512,256]{1,0:T(8,128)S(1)} %slice_select_fusion.1), channel_id=1, source_target_pairs={{0,64},{32,96},{64,0},{96,32},{128,192},{160,224},{192,128},{224,1... | collective-permute-start | bytes 1572872 | tf_op jit(solution)/shard_map/ppermute | solution.py:50
  81.8 27.1 %collective-permute-start.10 = (f32[512,256]{1,0:T(8,128)S(1)}, f32[512,256]{1,0:T(8,128)S(1)}, u32[]{:S(2)}, u32[]{:S(2)}) collective-permute-start(f32[512,256]{1,0:T(8,128)S(1)} %select_add_fusion.1), channel_id=1, source_target_pairs={{0,128},{32,160},{64,192},{96,224},{128,0},{160,32},{192,64},{224,... | collective-permute-start | bytes 1572872 | tf_op jit(solution)/shard_map/ppermute | solution.py:52
  109.0 30.2 %collective-permute-start.11 = (f32[512,256]{1,0:T(8,128)S(1)}, f32[512,256]{1,0:T(8,128)S(1)}, u32[]{:S(2)}, u32[]{:S(2)}) collective-permute-start(f32[512,256]{1,0:T(8,128)S(1)} %add.196), channel_id=1, source_target_pairs={{0,256},{32,288},{64,320},{96,352},{128,384},{160,416},{192,448},{... | collective-permute-start | bytes 1572872 | tf_op jit(solution)/shard_map/ppermute | solution.py:52
  139.3 13.9 %collective-permute-start.12 = (f32[512,256]{1,0:T(8,128)S(1)}, f32[512,256]{1,0:T(8,128)S(1)}, u32[]{:S(2)}, u32[]{:S(2)}) collective-permute-start(f32[512,256]{1,0:T(8,128)S(1)} %add.197), channel_id=1, source_target_pairs={{0,64},{32,96},{64,0},{96,32},{128,192},{160,224},{192,128},{224,1... | collective-permute-start | bytes 1572872 | tf_op jit(solution)/shard_map/ppermute | solution.py:54
  153.3 4.6 %collective-permute-start.13 = (f32[1024,256]{1,0:T(8,128)S(1)}, f32[1024,256]{1,0:T(8,128)S(1)}, u32[]{:S(2)}, u32[]{:S(2)}) collective-permute-start(f32[1024,256]{1,0:T(8,128)S(1)} %maximum_select_fusion.1), channel_id=1, source_target_pairs={{0,32},{32,0},{64,96},{96,64},{128,160},{160,128},{192,224},{224,1... | collective-permute-start | bytes 3145736 | tf_op jit(solution)/shard_map/ppermute | solution.py:54
  157.8 1.0 copy-start
  163.7 25.8 %copy-start.3 = (s32[64]{0:T(128)S(1)}, s32[64]{0:T(128)}, u32[]{:S(2)}) copy-start(s32[64]{0:T(128)} %param.11) | copy-start | bytes 772
  172.1 19.8 %collective-permute-start.15 = (f32[256,256]{0,1:T(8,128)}, f32[256,256]{0,1:T(8,128)S(1)}, u32[]{:S(2)}, u32[]{:S(2)}) collective-permute-start(f32[256,256]{0,1:T(8,128)} %get-tuple-element.37), channel_id=1, source_target_pairs={{0,2},{1,3},{2,4},{3,5},{4,6},{5,7},{6,8},{7,9},{8,10},{9,11},{10,... | collective-permute-start | bytes 786440 | tf_op jit(solution)/shard_map/ppermute | solution.py:84
  175.7 21.1 %collective-permute-start.14 = (f32[256,256]{0,1:T(8,128)}, f32[256,256]{0,1:T(8,128)S(1)}, u32[]{:S(2)}, u32[]{:S(2)}) collective-permute-start(f32[256,256]{0,1:T(8,128)} %get-tuple-element.37), channel_id=1, source_target_pairs={{0,1},{1,2},{2,3},{3,4},{4,5},{5,6},{6,7},{7,8},{8,9},{9,10},{10,1... | collective-permute-start | bytes 786440 | tf_op jit(solution)/shard_map/ppermute | solution.py:84
  180.4 16.4 %collective-permute-start.17 = (f32[256,256]{0,1:T(8,128)}, f32[256,256]{0,1:T(8,128)}, u32[]{:S(2)}, u32[]{:S(2)}) collective-permute-start(f32[256,256]{0,1:T(8,128)} %get-tuple-element.38), channel_id=1, source_target_pairs={{2,0},{3,1},{4,2},{5,3},{6,4},{7,5},{8,6},{9,7},{10,8},{11,9},{12,... | collective-permute-start | bytes 786440 | tf_op jit(solution)/shard_map/ppermute | solution.py:84
  184.4 18.0 %collective-permute-start.16 = (f32[256,256]{0,1:T(8,128)}, f32[256,256]{0,1:T(8,128)}, u32[]{:S(2)}, u32[]{:S(2)}) collective-permute-start(f32[256,256]{0,1:T(8,128)} %get-tuple-element.38), channel_id=1, source_target_pairs={{1,0},{2,1},{3,2},{4,3},{5,4},{6,5},{7,6},{8,7},{9,8},{10,9},{11,1... | collective-permute-start | bytes 786440 | tf_op jit(solution)/shard_map/ppermute | solution.py:84
  196.8 5.6 %copy-start.1 = (f32[256,256]{0,1:T(8,128)}, f32[256,256]{0,1:T(8,128)S(1)}, u32[]{:S(2)}) copy-start(f32[256,256]{0,1:T(8,128)S(1)} %collective-permute-done.14) | copy-start | bytes 786436

commit v5 on v3

--- a/solution.py
+++ b/solution.py
@@ -33,23 +33,40 @@
     return x
 
 
+def ind_steps(count, place):
+    if count % 2 or (count // 2) & (count // 2 - 1):
+        steps = []
+        mask = 1
+        while mask < count:
+            steps.append(([(j, j ^ mask) for j in range(count)], (place & mask) != 0))
+            mask *= 2
+        return steps
+    rings = count // 2
+    core = place % 2
+    turned = (place // 2 + core) % rings
+    steps = [([(j, j ^ 1) for j in range(count)], core != 0)]
+    mask = 1
+    while mask < rings:
+        pairs = []
+        for j in range(count):
+            c, z = j % 2, j // 2
+            partner = ((((z + c) % rings) ^ mask) - c) % rings
+            pairs.append((j, partner * 2 + c))
+        steps.append((pairs, (turned & mask) != 0))
+        mask *= 2
+    return steps
+
+
 def halving_allreduce(x, axis, count):
-    place = lax.axis_index(axis)
-    masks = []
-    mask = 1
-    while mask < count:
-        masks.append(mask)
-        mask *= 2
-    for mask in masks:
+    steps = ind_steps(count, lax.axis_index(axis))
+    for pairs, high in steps:
         half = x.shape[0] // 2
         lower, upper = x[:half], x[half:]
-        high = (place & mask) != 0
         send = jnp.where(high, lower, upper)
         keep = jnp.where(high, upper, lower)
-        x = keep + lax.ppermute(send, axis, [(j, j ^ mask) for j in range(count)])
-    for mask in reversed(masks):
-        got = lax.ppermute(x, axis, [(j, j ^ mask) for j in range(count)])
-        high = (place & mask) != 0
+        x = keep + lax.ppermute(send, axis, pairs)
+    for pairs, high in reversed(steps):
+        got = lax.ppermute(x, axis, pairs)
         x = jnp.where(high, jnp.concatenate([got, x], 0), jnp.concatenate([x, got], 0))
     return x
 

time: 246 us -> 243 us (0.988)
  waiting for transfers between devices: 76.5 us -> 68.4 us
  starting transfers between devices: 79.4 us -> 84.8 us
    ppermute x8, waiting for transfers between devices: 58.7 us -> 50.7 us  [the longest x4 25.6 us: halving_allreduce(): x = keep + lax.ppermute(send, axis, pairs)]
    ppermute x8, starting transfers between devices: 28.3 us -> 33.6 us  [the longest x4 17.3 us: halving_allreduce(): x = keep + lax.ppermute(send, axis, pairs)]
where the time goes in v5:
time: 243 us; the launch traced here: 242 us
  starting transfers between devices  84.8 us (35%)
  waiting for transfers between devices  68.4 us (28%)
  other arithmetic  58.9 us (24%)
  matrix products  11.9 us (5%)
  between operations  10.9 us (4%)
  local copies, waits for them, and re-layouts  7.48 us (3%)
    ppermute x8, starting transfers between devices, shift(): return lax.ppermute(x, axis, pairs)  29.6 us
    ppermute x4, waiting for transfers between devices, halving_allreduce(): x = keep + lax.ppermute(send, axis, pairs)  25.6 us
    ppermute x4, waiting for transfers between devices, halving_allreduce(): got = lax.ppermute(x, axis, pairs)  25.1 us
    ppermute x4, starting transfers between devices, xor_allreduce(): x = x + lax.ppermute(x, axis, [(j, j ^ mask) for j in range(count)])  21.6 us
    another operation x4, other arithmetic, lower_inverse(): return jax.scipy.linalg.solve_triangular(lower, eye, lower=True)  20.9 us
    ppermute x4, starting transfers between devices, halving_allreduce(): x = keep + lax.ppermute(send, axis, pairs)  17.3 us
    ppermute x4, starting transfers between devices, halving_allreduce(): got = lax.ppermute(x, axis, pairs)  16.3 us
    ppermute x8, waiting for transfers between devices, shift(): return lax.ppermute(x, axis, pairs)  14.5 us
  transfers between devices with their start and end apart: 20, of which 14 were waited for; matrix products, arithmetic and copies ran while one was open for 3% of the time, Pallas kernels for 0%

profile of v5, /device:TPU:6, one launch (start us, length us, event | category | flops | bytes accessed | tf_op | source)
XLA Modules:
  0.0 242.4 jit_solution(2530711761321237557)
XLA Ops:
  0.0 1.1 convert_reduce_fusion
  1.2 1.9 collective-permute-start
  3.1 0.7 multiply_bitcast_fusion
  4.1 0.7 multiply_subtract_fusion
  4.9 0.6 fusion.71
  5.5 0.6 broadcast_compare_fusion.2
  6.3 4.3 %collective-permute-start.1 = (f32[2,2048]{1,0:T(2,128)S(1)}, f32[2,2048]{1,0:T(2,128)S(1)}, u32[]{:S(2)}, u32[]{:S(2)}) collective-permute-start(f32[2,2048]{1,0:T(2,128)S(1)} %fusion.70), channel_id=1, source_target_pairs={{0,64},{32,96},{64,0},{96,32},{128,192},{160,224},{192,128},{224,1... | collective-permute-start | bytes 49160 | tf_op jit(solution)/shard_map/ppermute | solution.py:31
  10.8 1.5 collective-permute-done.1
  12.3 6.1 %collective-permute-start.2 = (f32[2,2048]{1,0:T(2,128)S(1)}, f32[2,2048]{1,0:T(2,128)S(1)}, u32[]{:S(2)}, u32[]{:S(2)}) collective-permute-start(f32[2,2048]{1,0:T(2,128)S(1)} %fusion.83), channel_id=1, source_target_pairs={{0,128},{32,160},{64,192},{96,224},{128,0},{160,32},{192,64},{224,... | collective-permute-start | bytes 49160 | tf_op jit(solution)/shard_map/ppermute | solution.py:31
  18.4 1.7 collective-permute-done.2
  20.1 9.3 %collective-permute-start.3 = (f32[2,2048]{1,0:T(2,128)S(1)}, f32[2,2048]{1,0:T(2,128)S(1)}, u32[]{:S(2)}, u32[]{:S(2)}) collective-permute-start(f32[2,2048]{1,0:T(2,128)S(1)} %add.192), channel_id=1, source_target_pairs={{0,256},{32,288},{64,320},{96,352},{128,384},{160,416},{192,448},{... | collective-permute-start | bytes 49160 | tf_op jit(solution)/shard_map/ppermute | solution.py:31
  31.5 1.1 multiply_convert_fusion
  32.6 1.3 fusion.14
  34.0 4.5 %collective-permute-start.5 = (f32[64,256]{1,0:T(8,128)S(1)}, f32[64,256]{1,0:T(8,128)S(1)}, u32[]{:S(2)}, u32[]{:S(2)}) collective-permute-start(f32[64,256]{1,0:T(8,128)S(1)} %dynamic-slice_bitcast_fusion), channel_id=1, source_target_pairs={{0,2},{1,3},{2,4},{3,5},{4,6},{5,7},{6,8},{7,9},{8,10},{9,11},{10,... | collective-permute-start | bytes 196616 | tf_op jit(solution)/shard_map/ppermute | solution.py:98
  38.5 3.5 %collective-permute-start.4 = (f32[64,256]{1,0:T(8,128)S(1)}, f32[64,256]{1,0:T(8,128)S(1)}, u32[]{:S(2)}, u32[]{:S(2)}) collective-permute-start(f32[64,256]{1,0:T(8,128)S(1)} %dynamic-slice_bitcast_fusion), channel_id=1, source_target_pairs={{0,1},{1,2},{2,3},{3,4},{4,5},{5,6},{6,7},{7,8},{8,9},{9,10},{10,1... | collective-permute-start | bytes 196616 | tf_op jit(solution)/shard_map/ppermute | solution.py:98
  42.0 0.7 constant_dynamic-slice_fusion.1
  47.8 4.4 %collective-permute-start.7 = (f32[64,256]{1,0:T(8,128)S(1)}, f32[64,256]{1,0:T(8,128)S(1)}, u32[]{:S(2)}, u32[]{:S(2)}) collective-permute-start(f32[64,256]{1,0:T(8,128)S(1)} %get-tuple-element.39), channel_id=1, source_target_pairs={{2,0},{3,1},{4,2},{5,3},{6,4},{7,5},{8,6},{9,7},{10,8},{11,9},{12,... | collective-permute-start | bytes 196616 | tf_op jit(solution)/shard_map/ppermute | solution.py:98
  52.1 2.4 collective-permute-start.6
  54.5 0.7 and_reduce_fusion
  55.2 3.1 %collective-permute-done.6 = f32[64,256]{1,0:T(8,128)S(1)} collective-permute-done((f32[64,256]{1,0:T(8,128)S(1)}, f32[64,256]{1,0:T(8,128)S(1)}, u32[]{:S(2)}, u32[]{:S(2)}) %collective-permute-start.6) | collective-permute-done | bytes 65568 | tf_op jit(solution)/shard_map/ppermute | solution.py:98
  58.3 0.7 fusion.47
  58.9 0.8 convolution_bitcast_fusion
  59.9 1.9 collective-permute-start.8
  61.8 2.7 %collective-permute-done.8 = f32[1024,256]{1,0:T(8,128)} collective-permute-done((f32[1024,256]{1,0:T(8,128)S(1)}, f32[1024,256]{1,0:T(8,128)}, u32[]{:S(2)}, u32[]{:S(2)}) %collective-permute-start.8) | collective-permute-done | bytes 1048608 | tf_op jit(solution)/shard_map/ppermute | solution.py:67
  64.5 1.4 select_add_fusion
  66.0 3.4 %collective-permute-start.9 = (f32[512,256]{1,0:T(8,128)S(1)}, f32[512,256]{1,0:T(8,128)S(1)}, u32[]{:S(2)}, u32[]{:S(2)}) collective-permute-start(f32[512,256]{1,0:T(8,128)S(1)} %slice_select_fusion.1), channel_id=1, source_target_pairs={{0,64},{32,480},{64,0},{96,160},{128,192},{160,96},{192,128},{224,... | collective-permute-start | bytes 1572872 | tf_op jit(solution)/shard_map/ppermute | solution.py:67
  69.4 7.7 %collective-permute-done.9 = f32[512,256]{1,0:T(8,128)S(1)} collective-permute-done((f32[512,256]{1,0:T(8,128)S(1)}, f32[512,256]{1,0:T(8,128)S(1)}, u32[]{:S(2)}, u32[]{:S(2)}) %collective-permute-start.9) | collective-permute-done | bytes 524320 | tf_op jit(solution)/shard_map/ppermute | solution.py:67
  77.3 4.3 %collective-permute-start.10 = (f32[256,256]{1,0:T(8,128)S(1)}, f32[256,256]{1,0:T(8,128)S(1)}, u32[]{:S(2)}, u32[]{:S(2)}) collective-permute-start(f32[256,256]{1,0:T(8,128)S(1)} %slice_select_fusion.2), channel_id=1, source_target_pairs={{0,128},{32,160},{64,192},{96,480},{128,0},{160,32},{192,64},{224,... | collective-permute-start | bytes 786440 | tf_op jit(solution)/shard_map/ppermute | solution.py:67
  81.6 9.6 %collective-permute-done.10 = f32[256,256]{1,0:T(8,128)S(1)} collective-permute-done((f32[256,256]{1,0:T(8,128)S(1)}, f32[256,256]{1,0:T(8,128)S(1)}, u32[]{:S(2)}, u32[]{:S(2)}) %collective-permute-start.10) | collective-permute-done | bytes 262176 | tf_op jit(solution)/shard_map/ppermute | solution.py:67
  91.2 7.7 %collective-permute-start.11 = (f32[128,256]{1,0:T(8,128)S(1)}, f32[128,256]{1,0:T(8,128)S(1)}, u32[]{:S(2)}, u32[]{:S(2)}) collective-permute-start(f32[128,256]{1,0:T(8,128)S(1)} %slice_select_fusion.3), channel_id=1, source_target_pairs={{0,256},{32,288},{64,320},{96,352},{128,384},{160,416},{192,448},{... | collective-permute-start | bytes 393224 | tf_op jit(solution)/shard_map/ppermute | solution.py:67
  99.0 5.7 %collective-permute-done.11 = f32[128,256]{1,0:T(8,128)S(1)} collective-permute-done((f32[128,256]{1,0:T(8,128)S(1)}, f32[128,256]{1,0:T(8,128)S(1)}, u32[]{:S(2)}, u32[]{:S(2)}) %collective-permute-start.11) | collective-permute-done | bytes 131104 | tf_op jit(solution)/shard_map/ppermute | solution.py:67
  104.7 5.2 %collective-permute-start.12 = (f32[128,256]{1,0:T(8,128)S(1)}, f32[128,256]{1,0:T(8,128)S(1)}, u32[]{:S(2)}, u32[]{:S(2)}) collective-permute-start(f32[128,256]{1,0:T(8,128)S(1)} %select_add_fusion.3), channel_id=1, source_target_pairs={{0,256},{32,288},{64,320},{96,352},{128,384},{160,416},{192,448},{... | collective-permute-start | bytes 393224 | tf_op jit(solution)/shard_map/ppermute | solution.py:69
  109.8 5.7 %collective-permute-done.12 = f32[128,256]{1,0:T(8,128)S(1)} collective-permute-done((f32[128,256]{1,0:T(8,128)S(1)}, f32[128,256]{1,0:T(8,128)S(1)}, u32[]{:S(2)}, u32[]{:S(2)}) %collective-permute-start.12) | collective-permute-done | bytes 131104 | tf_op jit(solution)/shard_map/ppermute | solution.py:69
  115.5 7.0 %collective-permute-start.13 = (f32[256,256]{1,0:T(8,128)S(1)}, f32[256,256]{1,0:T(8,128)S(1)}, u32[]{:S(2)}, u32[]{:S(2)}) collective-permute-start(f32[256,256]{1,0:T(8,128)S(1)} %maximum_select_fusion.3), channel_id=1, source_target_pairs={{0,128},{32,160},{64,192},{96,480},{128,0},{160,32},{192,64},{224,... | collective-permute-start | bytes 786440 | tf_op jit(solution)/shard_map/ppermute | solution.py:69
  122.5 9.4 %collective-permute-done.13 = f32[256,256]{1,0:T(8,128)S(1)} collective-permute-done((f32[256,256]{1,0:T(8,128)S(1)}, f32[256,256]{1,0:T(8,128)S(1)}, u32[]{:S(2)}, u32[]{:S(2)}) %collective-permute-start.13) | collective-permute-done | bytes 262176 | tf_op jit(solution)/shard_map/ppermute | solution.py:69
  132.0 1.9 collective-permute-start.14
  133.9 9.1 %collective-permute-done.14 = f32[512,256]{1,0:T(8,128)S(1)} collective-permute-done((f32[512,256]{1,0:T(8,128)S(1)}, f32[512,256]{1,0:T(8,128)S(1)}, u32[]{:S(2)}, u32[]{:S(2)}) %collective-permute-start.14) | collective-permute-done | bytes 524320 | tf_op jit(solution)/shard_map/ppermute | solution.py:69
  143.1 2.2 collective-permute-start.15
  145.3 0.6 dynamic_slice.34
  145.9 0.6 broadcast_compare_fusion.1
  146.8 0.8 collective-permute-done.15
  147.7 1.0 copy-done
  148.7 3.0 %fusion.11 = f32[2048,256]{1,0:T(8,128)S(1)} fusion(f32[1024,256]{1,0:T(8,128)S(1)} %maximum_select_fusion.1, f32[1024,256]{1,0:T(8,128)} %copy-done, s32[]{:T(128)} %bitcast.105, s32[2048]{0:T(1024)S(1)} %add_multiply_fusion, pred[]{:T(512)S(6)} %ne.35), kind=kLoop, calls=%fused_computation.15 | loop fusion | flops 9961472 | bytes 4202501 | tf_op jit(solution)/shard_map/add | solution.py:176
  151.7 1.9 copy.19
  153.6 7.5 %fusion.19 = f32[3,256,256]{1,2,0:T(8,128)S(1)} fusion(f32[2048,256]{1,0:T(8,128)S(1)} %fusion.11, f32[2048,3]{0,1:T(4,128)S(1)} %convert_bitcast_fusion, f32[2048,256]{0,1:T(8,128)} %copy.19), kind=kOutput, calls=%fused_computation.23 | convolution fusion | flops 4833411072 | bytes 5005312 | tf_op jit(solution)/shard_map/mc,ck,cl->mkl/dot_general | solution.py:182
  161.1 0.9 slice_bitcast_fusion.1
  161.9 3.5 %collective-permute-start.17 = (f32[256,256]{0,1:T(8,128)}, f32[256,256]{0,1:T(8,128)S(1)}, u32[]{:S(2)}, u32[]{:S(2)}) collective-permute-start(f32[256,256]{0,1:T(8,128)} %get-tuple-element.37), channel_id=1, source_target_pairs={{0,2},{1,3},{2,4},{3,5},{4,6},{5,7},{6,8},{7,9},{8,10},{9,11},{10,... | collective-permute-start | bytes 786440 | tf_op jit(solution)/shard_map/ppermute | solution.py:98
  165.4 4.8 %collective-permute-start.16 = (f32[256,256]{0,1:T(8,128)}, f32[256,256]{0,1:T(8,128)S(1)}, u32[]{:S(2)}, u32[]{:S(2)}) collective-permute-start(f32[256,256]{0,1:T(8,128)} %get-tuple-element.37), channel_id=1, source_target_pairs={{0,1},{1,2},{2,3},{3,4},{4,5},{5,6},{6,7},{7,8},{8,9},{9,10},{10,1... | collective-permute-start | bytes 786440 | tf_op jit(solution)/shard_map/ppermute | solution.py:98
  170.2 4.0 %collective-permute-start.19 = (f32[256,256]{0,1:T(8,128)}, f32[256,256]{0,1:T(8,128)}, u32[]{:S(2)}, u32[]{:S(2)}) collective-permute-start(f32[256,256]{0,1:T(8,128)} %get-tuple-element.38), channel_id=1, source_target_pairs={{2,0},{3,1},{4,2},{5,3},{6,4},{7,5},{8,6},{9,7},{10,8},{11,9},{12,... | collective-permute-start | bytes 786440 | tf_op jit(solution)/shard_map/ppermute | solution.py:98
  174.3 2.6 %collective-permute-start.18 = (f32[256,256]{0,1:T(8,128)}, f32[256,256]{0,1:T(8,128)}, u32[]{:S(2)}, u32[]{:S(2)}) collective-permute-start(f32[256,256]{0,1:T(8,128)} %get-tuple-element.38), channel_id=1, source_target_pairs={{1,0},{2,1},{3,2},{4,3},{5,4},{6,5},{7,6},{8,7},{9,8},{10,9},{11,1... | collective-permute-start | bytes 786440 | tf_op jit(solution)/shard_map/ppermute | solution.py:98
  179.4 0.6 dynamic_slice.35
  180.7 1.1 collective-permute-done.17
  181.7 4.9 %collective-permute-done.16 = f32[256,256]{0,1:T(8,128)S(1)} collective-permute-done((f32[256,256]{0,1:T(8,128)}, f32[256,256]{0,1:T(8,128)S(1)}, u32[]{:S(2)}, u32[]{:S(2)}) %collective-permute-start.16) | collective-permute-done | bytes 262176 | tf_op jit(solution)/shard_map/ppermute | solution.py:98
  186.6 5.5 %collective-permute-done.18 = f32[256,256]{0,1:T(8,128)} collective-permute-done((f32[256,256]{0,1:T(8,128)}, f32[256,256]{0,1:T(8,128)}, u32[]{:S(2)}, u32[]{:S(2)}) %collective-permute-start.18) | collective-permute-done | bytes 262176 | tf_op jit(solution)/shard_map/ppermute | solution.py:98
  192.1 1.1 fusion.39
  193.4 11.7 %cholesky.44 = f32[128,128]{1,0:T(8,128)S(1)} custom-call(f32[128,128]{1,0:T(8,128)S(1)} %fusion.55), custom_call_target="Cholesky" | custom-call | tf_op jit(solution)/shard_map/jit(cholesky)/cholesky | solution.py:85
  205.1 0.6 compare_reduce_fusion.1
  205.8 0.7 fusion.45
  206.4 9.8 %custom-call.6 = f32[1,128,128]{1,2,0:T(8,128)S(1)} custom-call(f32[1,128,128]{2,1,0:T(8,128)S(1)} %fusion.45), custom_call_target="InvertDiagBlocksLowerTriangular" | custom-call | tf_op jit(solution)/shard_map/jit(_solve_triangular)/triangular_solve | solution.py:80
  217.7 11.7 %cholesky.55 = f32[128,128]{1,0:T(8,128)S(1)} custom-call(f32[128,128]{1,0:T(8,128)S(1)} %fusion.53), custom_call_target="Cholesky" | custom-call | tf_op jit(solution)/shard_map/jit(cholesky)/cholesky | solution.py:88
  229.5 0.6 compare_reduce_fusion
  230.1 0.7 fusion.46
  230.8 9.8 %custom-call.7 = f32[1,128,128]{1,2,0:T(8,128)S(1)} custom-call(f32[1,128,128]{2,1,0:T(8,128)S(1)} %fusion.46), custom_call_target="InvertDiagBlocksLowerTriangular" | custom-call | tf_op jit(solution)/shard_map/jit(_solve_triangular)/triangular_solve | solution.py:80
  241.6 0.8 copy.24
  (68 shorter events, 4.4 us)
Async XLA Ops:
  1.2 5.1 %collective-permute-start = (f32[2,2048]{1,0:T(2,128)S(1)}, f32[2,2048]{1,0:T(2,128)S(1)}, u32[]{:S(2)}, u32[]{:S(2)}) collective-permute-start(f32[2,2048]{1,0:T(2,128)S(1)} %pad_maximum_fusion.1), channel_id=1, source_target_pairs={{0,32},{32,0},{64,96},{96,64},{128,160},{160,128},{192,224},{224,1... | collective-permute-start | bytes 49160 | tf_op jit(solution)/shard_map/ppermute | solution.py:31
  6.3 6.0 %collective-permute-start.1 = (f32[2,2048]{1,0:T(2,128)S(1)}, f32[2,2048]{1,0:T(2,128)S(1)}, u32[]{:S(2)}, u32[]{:S(2)}) collective-permute-start(f32[2,2048]{1,0:T(2,128)S(1)} %fusion.70), channel_id=1, source_target_pairs={{0,64},{32,96},{64,0},{96,32},{128,192},{160,224},{192,128},{224,1... | collective-permute-start | bytes 49160 | tf_op jit(solution)/shard_map/ppermute | solution.py:31
  12.3 7.8 %collective-permute-start.2 = (f32[2,2048]{1,0:T(2,128)S(1)}, f32[2,2048]{1,0:T(2,128)S(1)}, u32[]{:S(2)}, u32[]{:S(2)}) collective-permute-start(f32[2,2048]{1,0:T(2,128)S(1)} %fusion.83), channel_id=1, source_target_pairs={{0,128},{32,160},{64,192},{96,224},{128,0},{160,32},{192,64},{224,... | collective-permute-start | bytes 49160 | tf_op jit(solution)/shard_map/ppermute | solution.py:31
  20.1 11.3 %collective-permute-start.3 = (f32[2,2048]{1,0:T(2,128)S(1)}, f32[2,2048]{1,0:T(2,128)S(1)}, u32[]{:S(2)}, u32[]{:S(2)}) collective-permute-start(f32[2,2048]{1,0:T(2,128)S(1)} %add.192), channel_id=1, source_target_pairs={{0,256},{32,288},{64,320},{96,352},{128,384},{160,416},{192,448},{... | collective-permute-start | bytes 49160 | tf_op jit(solution)/shard_map/ppermute | solution.py:31
  32.6 21.9 %copy-start.2 = (s32[3]{0:T(128)S(1)}, s32[3]{0:T(128)}, u32[]{:S(2)}) copy-start(s32[3]{0:T(128)} %constant.188.clone.1) | copy-start | bytes 40
  34.0 13.7 %collective-permute-start.5 = (f32[64,256]{1,0:T(8,128)S(1)}, f32[64,256]{1,0:T(8,128)S(1)}, u32[]{:S(2)}, u32[]{:S(2)}) collective-permute-start(f32[64,256]{1,0:T(8,128)S(1)} %dynamic-slice_bitcast_fusion), channel_id=1, source_target_pairs={{0,2},{1,3},{2,4},{3,5},{4,6},{5,7},{6,8},{7,9},{8,10},{9,11},{10,... | collective-permute-start | bytes 196616 | tf_op jit(solution)/shard_map/ppermute | solution.py:98
  38.5 9.3 %collective-permute-start.4 = (f32[64,256]{1,0:T(8,128)S(1)}, f32[64,256]{1,0:T(8,128)S(1)}, u32[]{:S(2)}, u32[]{:S(2)}) collective-permute-start(f32[64,256]{1,0:T(8,128)S(1)} %dynamic-slice_bitcast_fusion), channel_id=1, source_target_pairs={{0,1},{1,2},{2,3},{3,4},{4,5},{5,6},{6,7},{7,8},{8,9},{9,10},{10,1... | collective-permute-start | bytes 196616 | tf_op jit(solution)/shard_map/ppermute | solution.py:98
  47.8 7.5 %collective-permute-start.7 = (f32[64,256]{1,0:T(8,128)S(1)}, f32[64,256]{1,0:T(8,128)S(1)}, u32[]{:S(2)}, u32[]{:S(2)}) collective-permute-start(f32[64,256]{1,0:T(8,128)S(1)} %get-tuple-element.39), channel_id=1, source_target_pairs={{2,0},{3,1},{4,2},{5,3},{6,4},{7,5},{8,6},{9,7},{10,8},{11,9},{12,... | collective-permute-start | bytes 196616 | tf_op jit(solution)/shard_map/ppermute | solution.py:98
  52.1 6.2 %collective-permute-start.6 = (f32[64,256]{1,0:T(8,128)S(1)}, f32[64,256]{1,0:T(8,128)S(1)}, u32[]{:S(2)}, u32[]{:S(2)}) collective-permute-start(f32[64,256]{1,0:T(8,128)S(1)} %get-tuple-element.39), channel_id=1, source_target_pairs={{1,0},{2,1},{3,2},{4,3},{5,4},{6,5},{7,6},{8,7},{9,8},{10,9},{11,1... | collective-permute-start | bytes 196616 | tf_op jit(solution)/shard_map/ppermute | solution.py:98
  59.9 4.7 %collective-permute-start.8 = (f32[1024,256]{1,0:T(8,128)S(1)}, f32[1024,256]{1,0:T(8,128)}, u32[]{:S(2)}, u32[]{:S(2)}) collective-permute-start(f32[1024,256]{1,0:T(8,128)S(1)} %slice_select_fusion), channel_id=1, source_target_pairs={{0,32},{32,0},{64,96},{96,64},{128,160},{160,128},{192,224},{224,1... | collective-permute-start | bytes 3145736 | tf_op jit(solution)/shard_map/ppermute | solution.py:67
  66.0 11.1 %collective-permute-start.9 = (f32[512,256]{1,0:T(8,128)S(1)}, f32[512,256]{1,0:T(8,128)S(1)}, u32[]{:S(2)}, u32[]{:S(2)}) collective-permute-start(f32[512,256]{1,0:T(8,128)S(1)} %slice_select_fusion.1), channel_id=1, source_target_pairs={{0,64},{32,480},{64,0},{96,160},{128,192},{160,96},{192,128},{224,... | collective-permute-start | bytes 1572872 | tf_op jit(solution)/shard_map/ppermute | solution.py:67
  77.3 13.9 %collective-permute-start.10 = (f32[256,256]{1,0:T(8,128)S(1)}, f32[256,256]{1,0:T(8,128)S(1)}, u32[]{:S(2)}, u32[]{:S(2)}) collective-permute-start(f32[256,256]{1,0:T(8,128)S(1)} %slice_select_fusion.2), channel_id=1, source_target_pairs={{0,128},{32,160},{64,192},{96,480},{128,0},{160,32},{192,64},{224,... | collective-permute-start | bytes 786440 | tf_op jit(solution)/shard_map/ppermute | solution.py:67
  91.2 13.4 %collective-permute-start.11 = (f32[128,256]{1,0:T(8,128)S(1)}, f32[128,256]{1,0:T(8,128)S(1)}, u32[]{:S(2)}, u32[]{:S(2)}) collective-permute-start(f32[128,256]{1,0:T(8,128)S(1)} %slice_select_fusion.3), channel_id=1, source_target_pairs={{0,256},{32,288},{64,320},{96,352},{128,384},{160,416},{192,448},{... | collective-permute-start | bytes 393224 | tf_op jit(solution)/shard_map/ppermute | solution.py:67
  104.7 10.9 %collective-permute-start.12 = (f32[128,256]{1,0:T(8,128)S(1)}, f32[128,256]{1,0:T(8,128)S(1)}, u32[]{:S(2)}, u32[]{:S(2)}) collective-permute-start(f32[128,256]{1,0:T(8,128)S(1)} %select_add_fusion.3), channel_id=1, source_target_pairs={{0,256},{32,288},{64,320},{96,352},{128,384},{160,416},{192,448},{... | collective-permute-start | bytes 393224 | tf_op jit(solution)/shard_map/ppermute | solution.py:69
  115.5 16.4 %collective-permute-start.13 = (f32[256,256]{1,0:T(8,128)S(1)}, f32[256,256]{1,0:T(8,128)S(1)}, u32[]{:S(2)}, u32[]{:S(2)}) collective-permute-start(f32[256,256]{1,0:T(8,128)S(1)} %maximum_select_fusion.3), channel_id=1, source_target_pairs={{0,128},{32,160},{64,192},{96,480},{128,0},{160,32},{192,64},{224,... | collective-permute-start | bytes 786440 | tf_op jit(solution)/shard_map/ppermute | solution.py:69
  132.0 11.1 %collective-permute-start.14 = (f32[512,256]{1,0:T(8,128)S(1)}, f32[512,256]{1,0:T(8,128)S(1)}, u32[]{:S(2)}, u32[]{:S(2)}) collective-permute-start(f32[512,256]{1,0:T(8,128)S(1)} %maximum_select_fusion.2), channel_id=1, source_target_pairs={{0,64},{32,480},{64,0},{96,160},{128,192},{160,96},{192,128},{224,... | collective-permute-start | bytes 1572872 | tf_op jit(solution)/shard_map/ppermute | solution.py:69
  143.1 4.6 %collective-permute-start.15 = (f32[1024,256]{1,0:T(8,128)S(1)}, f32[1024,256]{1,0:T(8,128)S(1)}, u32[]{:S(2)}, u32[]{:S(2)}) collective-permute-start(f32[1024,256]{1,0:T(8,128)S(1)} %maximum_select_fusion.1), channel_id=1, source_target_pairs={{0,32},{32,0},{64,96},{96,64},{128,160},{160,128},{192,224},{224,1... | collective-permute-start | bytes 3145736 | tf_op jit(solution)/shard_map/ppermute | solution.py:69
  147.7 1.0 copy-start
  153.6 25.8 %copy-start.3 = (s32[64]{0:T(128)S(1)}, s32[64]{0:T(128)}, u32[]{:S(2)}) copy-start(s32[64]{0:T(128)} %param.11) | copy-start | bytes 772
  161.9 19.8 %collective-permute-start.17 = (f32[256,256]{0,1:T(8,128)}, f32[256,256]{0,1:T(8,128)S(1)}, u32[]{:S(2)}, u32[]{:S(2)}) collective-permute-start(f32[256,256]{0,1:T(8,128)} %get-tuple-element.37), channel_id=1, source_target_pairs={{0,2},{1,3},{2,4},{3,5},{4,6},{5,7},{6,8},{7,9},{8,10},{9,11},{10,... | collective-permute-start | bytes 786440 | tf_op jit(solution)/shard_map/ppermute | solution.py:98
  165.4 21.2 %collective-permute-start.16 = (f32[256,256]{0,1:T(8,128)}, f32[256,256]{0,1:T(8,128)S(1)}, u32[]{:S(2)}, u32[]{:S(2)}) collective-permute-start(f32[256,256]{0,1:T(8,128)} %get-tuple-element.37), channel_id=1, source_target_pairs={{0,1},{1,2},{2,3},{3,4},{4,5},{5,6},{6,7},{7,8},{8,9},{9,10},{10,1... | collective-permute-start | bytes 786440 | tf_op jit(solution)/shard_map/ppermute | solution.py:98
  170.2 16.4 %collective-permute-start.19 = (f32[256,256]{0,1:T(8,128)}, f32[256,256]{0,1:T(8,128)}, u32[]{:S(2)}, u32[]{:S(2)}) collective-permute-start(f32[256,256]{0,1:T(8,128)} %get-tuple-element.38), channel_id=1, source_target_pairs={{2,0},{3,1},{4,2},{5,3},{6,4},{7,5},{8,6},{9,7},{10,8},{11,9},{12,... | collective-permute-start | bytes 786440 | tf_op jit(solution)/shard_map/ppermute | solution.py:98
  174.3 17.9 %collective-permute-start.18 = (f32[256,256]{0,1:T(8,128)}, f32[256,256]{0,1:T(8,128)}, u32[]{:S(2)}, u32[]{:S(2)}) collective-permute-start(f32[256,256]{0,1:T(8,128)} %get-tuple-element.38), channel_id=1, source_target_pairs={{1,0},{2,1},{3,2},{4,3},{5,4},{6,5},{7,6},{8,7},{9,8},{10,9},{11,1... | collective-permute-start | bytes 786440 | tf_op jit(solution)/shard_map/ppermute | solution.py:98
  186.6 5.5 %copy-start.1 = (f32[256,256]{0,1:T(8,128)}, f32[256,256]{0,1:T(8,128)S(1)}, u32[]{:S(2)}) copy-start(f32[256,256]{0,1:T(8,128)S(1)} %collective-permute-done.16) | copy-start | bytes 786436

commit v6 on v5

--- a/solution.py
+++ b/solution.py
@@ -103,6 +103,7 @@
 
 
 def halo(head_part, tail_part, blk_index, blk_count, reach, edge_blocks, first_block, last_block):
+    head_part, tail_part = lax.optimization_barrier((head_part, tail_part))
     from_lower = []
     from_upper = []
     for step in range(1, reach + 1):
@@ -178,12 +179,18 @@
     row_start = ind_index * row_slice
     my_rows = lax.dynamic_slice_in_dim(projected, row_start, row_slice, 0)
     my_slot = unit_slot[row_start // UNIT]
-    pick = jnp.stack([col_slot == 0, col_slot == last_slot, col_slot == my_slot]).astype(jnp.float32)
+    unit_grams = jnp.einsum(
+        "tgk,tgl->tkl",
+        projected.reshape(unit_count, UNIT, K),
+        projected.reshape(unit_count, UNIT, K),
+        precision=lax.Precision.HIGHEST,
+        preferred_element_type=jnp.float32,
+    )
+    pick = jnp.stack([unit_slot == 0, unit_slot == last_slot, unit_slot == my_slot]).astype(jnp.float32)
     grams = jnp.einsum(
-        "mc,ck,cl->mkl",
+        "mt,tkl->mkl",
         pick,
-        projected,
-        projected,
+        unit_grams,
         precision=lax.Precision.HIGHEST,
         preferred_element_type=jnp.float32,
     )

time: 243 us -> 243 us (level)
  starting transfers between devices: 84.8 us -> 78.6 us
  matrix products: 11.9 us -> 16.6 us
    ppermute x4, starting transfers between devices: 17.3 us -> 11.5 us  [halving_allreduce(): x = keep + lax.ppermute(send, axis, pairs)]
    dot_general x1 -> x2, matrix products: 7.46 us -> 12.1 us  [the longest x1 8.29 us: on_device(): jnp.einsum('tgk,tgl->tkl', projected.reshape(unit_count, UNIT, K), projec...]
    ppermute x4, waiting for transfers between devices: 25.6 us -> 29 us  [halving_allreduce(): x = keep + lax.ppermute(send, axis, pairs)]
    ppermute x4, waiting for transfers between devices: 25.1 us -> 22 us  [halving_allreduce(): got = lax.ppermute(x, axis, pairs)]
  transfers between devices with their start and end apart: 20 -> 20, of which waited for: 14 -> 14; matrix products, arithmetic and copies ran while one was open for 3% -> 4% of each run, Pallas kernels for 0% -> 0%
where the time goes in v6:
time: 243 us; the launch traced here: 242 us
  starting transfers between devices  78.6 us (32%)
  waiting for transfers between devices  66.6 us (27%)
  other arithmetic  60.8 us (25%)
  matrix products  16.6 us (7%)
  between operations  11.1 us (5%)
  local copies, waits for them, and re-layouts  7.84 us (3%)
    ppermute x8, starting transfers between devices, shift(): return lax.ppermute(x, axis, pairs)  29.4 us
    ppermute x4, waiting for transfers between devices, halving_allreduce(): x = keep + lax.ppermute(send, axis, pairs)  29 us
    ppermute x4, waiting for transfers between devices, halving_allreduce(): got = lax.ppermute(x, axis, pairs)  22 us
    ppermute x4, starting transfers between devices, xor_allreduce(): x = x + lax.ppermute(x, axis, [(j, j ^ mask) for j in range(count)])  21.6 us
    another operation x4, other arithmetic, lower_inverse(): return jax.scipy.linalg.solve_triangular(lower, eye, lower=True)  20.9 us
    ppermute x4, starting transfers between devices, halving_allreduce(): got = lax.ppermute(x, axis, pairs)  16.2 us
    another operation x3, other arithmetic, basis_rows(): l11 = jnp.linalg.cholesky(gram[:half, :half])  12.4 us
    another operation x3, other arithmetic, basis_rows(): l22 = jnp.linalg.cholesky(gram[half:, half:] - dot_hi(l21, l21.T))  12.4 us
  transfers between devices with their start and end apart: 20, of which 14 were waited for; matrix products, arithmetic and copies ran while one was open for 4% of the time, Pallas kernels for 0%

profile of v6, /device:TPU:6, one launch (start us, length us, event | category | flops | bytes accessed | tf_op | source)
XLA Modules:
  0.0 241.6 jit_solution(10550750368790003486)
XLA Ops:
  0.0 1.1 convert_reduce_fusion
  1.2 1.9 collective-permute-start
  3.1 0.7 multiply_bitcast_fusion
  4.1 0.7 multiply_subtract_fusion
  5.0 0.6 fusion.86
  5.5 0.7 compare_bitcast_fusion.2
  6.5 4.3 %collective-permute-start.1 = (f32[2,2048]{1,0:T(2,128)S(1)}, f32[2,2048]{1,0:T(2,128)S(1)}, u32[]{:S(2)}, u32[]{:S(2)}) collective-permute-start(f32[2,2048]{1,0:T(2,128)S(1)} %fusion.84), channel_id=1, source_target_pairs={{0,64},{32,96},{64,0},{96,32},{128,192},{160,224},{192,128},{224,1... | collective-permute-start | bytes 49160 | tf_op jit(solution)/shard_map/ppermute | solution.py:31
  10.8 1.7 collective-permute-done.1
  12.6 6.1 %collective-permute-start.2 = (f32[2,2048]{1,0:T(2,128)S(1)}, f32[2,2048]{1,0:T(2,128)S(1)}, u32[]{:S(2)}, u32[]{:S(2)}) collective-permute-start(f32[2,2048]{1,0:T(2,128)S(1)} %fusion.98), channel_id=1, source_target_pairs={{0,128},{32,160},{64,192},{96,224},{128,0},{160,32},{192,64},{224,... | collective-permute-start | bytes 49160 | tf_op jit(solution)/shard_map/ppermute | solution.py:31
  18.7 1.7 collective-permute-done.2
  20.4 9.3 %collective-permute-start.3 = (f32[2,2048]{1,0:T(2,128)S(1)}, f32[2,2048]{1,0:T(2,128)S(1)}, u32[]{:S(2)}, u32[]{:S(2)}) collective-permute-start(f32[2,2048]{1,0:T(2,128)S(1)} %add.224), channel_id=1, source_target_pairs={{0,256},{32,288},{64,320},{96,352},{128,384},{160,416},{192,448},{... | collective-permute-start | bytes 49160 | tf_op jit(solution)/shard_map/ppermute | solution.py:31
  30.4 0.7 constant_dynamic-slice_fusion.1
  37.6 1.1 multiply_convert_fusion
  38.7 1.3 fusion.24
  40.1 4.5 %collective-permute-start.5 = (f32[64,256]{1,0:T(8,128)S(1)}, f32[64,256]{1,0:T(8,128)S(1)}, u32[]{:S(2)}, u32[]{:S(2)}) collective-permute-start(f32[64,256]{1,0:T(8,128)S(1)} %get-tuple-element.35), channel_id=1, source_target_pairs={{0,2},{1,3},{2,4},{3,5},{4,6},{5,7},{6,8},{7,9},{8,10},{9,11},{10,... | collective-permute-start | bytes 196616 | tf_op jit(solution)/shard_map/ppermute | solution.py:98
  44.6 3.5 %collective-permute-start.4 = (f32[64,256]{1,0:T(8,128)S(1)}, f32[64,256]{1,0:T(8,128)S(1)}, u32[]{:S(2)}, u32[]{:S(2)}) collective-permute-start(f32[64,256]{1,0:T(8,128)S(1)} %get-tuple-element.35), channel_id=1, source_target_pairs={{0,1},{1,2},{2,3},{3,4},{4,5},{5,6},{6,7},{7,8},{8,9},{9,10},{10,1... | collective-permute-start | bytes 196616 | tf_op jit(solution)/shard_map/ppermute | solution.py:98
  48.1 0.8 and_reduce_fusion
  48.9 4.3 %collective-permute-start.7 = (f32[64,256]{1,0:T(8,128)S(1)}, f32[64,256]{1,0:T(8,128)S(1)}, u32[]{:S(2)}, u32[]{:S(2)}) collective-permute-start(f32[64,256]{1,0:T(8,128)S(1)} %get-tuple-element.36), channel_id=1, source_target_pairs={{2,0},{3,1},{4,2},{5,3},{6,4},{7,5},{8,6},{9,7},{10,8},{11,9},{12,... | collective-permute-start | bytes 196616 | tf_op jit(solution)/shard_map/ppermute | solution.py:98
  53.3 2.4 collective-permute-start.6
  56.1 3.3 %collective-permute-done.6 = f32[64,256]{1,0:T(8,128)S(1)} collective-permute-done((f32[64,256]{1,0:T(8,128)S(1)}, f32[64,256]{1,0:T(8,128)S(1)}, u32[]{:S(2)}, u32[]{:S(2)}) %collective-permute-start.6) | collective-permute-done | bytes 65568 | tf_op jit(solution)/shard_map/ppermute | solution.py:98
  59.4 0.7 fusion.52
  60.1 0.8 convolution_bitcast_fusion
  61.0 1.9 collective-permute-start.8
  63.0 2.7 %collective-permute-done.8 = f32[1024,256]{1,0:T(8,128)} collective-permute-done((f32[1024,256]{1,0:T(8,128)S(1)}, f32[1024,256]{1,0:T(8,128)}, u32[]{:S(2)}, u32[]{:S(2)}) %collective-permute-start.8) | collective-permute-done | bytes 1048608 | tf_op jit(solution)/shard_map/ppermute | solution.py:67
  65.7 1.4 select_add_fusion
  67.2 3.4 %collective-permute-start.9 = (f32[512,256]{1,0:T(8,128)S(1)}, f32[512,256]{1,0:T(8,128)S(1)}, u32[]{:S(2)}, u32[]{:S(2)}) collective-permute-start(f32[512,256]{1,0:T(8,128)S(1)} %slice_select_fusion.1), channel_id=1, source_target_pairs={{0,64},{32,480},{64,0},{96,160},{128,192},{160,96},{192,128},{224,... | collective-permute-start | bytes 1572872 | tf_op jit(solution)/shard_map/ppermute | solution.py:67
  70.6 7.7 %collective-permute-done.9 = f32[512,256]{1,0:T(8,128)S(1)} collective-permute-done((f32[512,256]{1,0:T(8,128)S(1)}, f32[512,256]{1,0:T(8,128)S(1)}, u32[]{:S(2)}, u32[]{:S(2)}) %collective-permute-start.9) | collective-permute-done | bytes 524320 | tf_op jit(solution)/shard_map/ppermute | solution.py:67
  78.5 4.3 %collective-permute-start.10 = (f32[256,256]{1,0:T(8,128)S(1)}, f32[256,256]{1,0:T(8,128)S(1)}, u32[]{:S(2)}, u32[]{:S(2)}) collective-permute-start(f32[256,256]{1,0:T(8,128)S(1)} %slice_select_fusion.2), channel_id=1, source_target_pairs={{0,128},{32,160},{64,192},{96,480},{128,0},{160,32},{192,64},{224,... | collective-permute-start | bytes 786440 | tf_op jit(solution)/shard_map/ppermute | solution.py:67
  82.8 9.7 %collective-permute-done.10 = f32[256,256]{1,0:T(8,128)S(1)} collective-permute-done((f32[256,256]{1,0:T(8,128)S(1)}, f32[256,256]{1,0:T(8,128)S(1)}, u32[]{:S(2)}, u32[]{:S(2)}) %collective-permute-start.10) | collective-permute-done | bytes 262176 | tf_op jit(solution)/shard_map/ppermute | solution.py:67
  92.6 1.9 collective-permute-start.11
  94.5 8.8 %collective-permute-done.11 = f32[128,256]{1,0:T(8,128)S(1)} collective-permute-done((f32[128,256]{1,0:T(8,128)S(1)}, f32[128,256]{1,0:T(8,128)S(1)}, u32[]{:S(2)}, u32[]{:S(2)}) %collective-permute-start.11) | collective-permute-done | bytes 131104 | tf_op jit(solution)/shard_map/ppermute | solution.py:67
  103.4 4.6 %collective-permute-start.12 = (f32[128,256]{1,0:T(8,128)S(1)}, f32[128,256]{1,0:T(8,128)S(1)}, u32[]{:S(2)}, u32[]{:S(2)}) collective-permute-start(f32[128,256]{1,0:T(8,128)S(1)} %select_add_fusion.3), channel_id=1, source_target_pairs={{0,256},{32,288},{64,320},{96,352},{128,384},{160,416},{192,448},{... | collective-permute-start | bytes 393224 | tf_op jit(solution)/shard_map/ppermute | solution.py:69
  107.9 6.3 %collective-permute-done.12 = f32[128,256]{1,0:T(8,128)S(1)} collective-permute-done((f32[128,256]{1,0:T(8,128)S(1)}, f32[128,256]{1,0:T(8,128)S(1)}, u32[]{:S(2)}, u32[]{:S(2)}) %collective-permute-start.12) | collective-permute-done | bytes 131104 | tf_op jit(solution)/shard_map/ppermute | solution.py:69
  114.3 5.6 %collective-permute-start.13 = (f32[256,256]{1,0:T(8,128)S(1)}, f32[256,256]{1,0:T(8,128)S(1)}, u32[]{:S(2)}, u32[]{:S(2)}) collective-permute-start(f32[256,256]{1,0:T(8,128)S(1)} %maximum_select_fusion.3), channel_id=1, source_target_pairs={{0,128},{32,160},{64,192},{96,480},{128,0},{160,32},{192,64},{224,... | collective-permute-start | bytes 786440 | tf_op jit(solution)/shard_map/ppermute | solution.py:69
  119.9 7.1 %collective-permute-done.13 = f32[256,256]{1,0:T(8,128)S(1)} collective-permute-done((f32[256,256]{1,0:T(8,128)S(1)}, f32[256,256]{1,0:T(8,128)S(1)}, u32[]{:S(2)}, u32[]{:S(2)}) %collective-permute-start.13) | collective-permute-done | bytes 262176 | tf_op jit(solution)/shard_map/ppermute | solution.py:69
  127.1 3.9 %collective-permute-start.14 = (f32[512,256]{1,0:T(8,128)S(1)}, f32[512,256]{1,0:T(8,128)S(1)}, u32[]{:S(2)}, u32[]{:S(2)}) collective-permute-start(f32[512,256]{1,0:T(8,128)S(1)} %maximum_select_fusion.2), channel_id=1, source_target_pairs={{0,64},{32,480},{64,0},{96,160},{128,192},{160,96},{192,128},{224,... | collective-permute-start | bytes 1572872 | tf_op jit(solution)/shard_map/ppermute | solution.py:69
  131.0 7.2 %collective-permute-done.14 = f32[512,256]{1,0:T(8,128)S(1)} collective-permute-done((f32[512,256]{1,0:T(8,128)S(1)}, f32[512,256]{1,0:T(8,128)S(1)}, u32[]{:S(2)}, u32[]{:S(2)}) %collective-permute-start.14) | collective-permute-done | bytes 524320 | tf_op jit(solution)/shard_map/ppermute | solution.py:69
  138.3 2.1 collective-permute-start.15
  141.0 0.6 compare_bitcast_fusion.1
  141.7 1.3 collective-permute-done.15
  143.0 1.8 fusion.18
  144.8 1.9 copy.21
  146.7 8.3 %fusion.16 = f32[16,256,256]{2,1,0:T(8,128)S(1)} fusion(f32[16,128,256]{1,2,0:T(8,128)} %copy.21, s32[]{:T(128)} %bitcast.84, s32[16,128]{1,0:T(8,128)S(1)} %add_multiply_fusion), kind=kOutput, calls=%fused_computation.21 | convolution fusion | flops 1618477056 | bytes 6299652 | tf_op jit(solution)/shard_map/tgk,tgl->tkl/dot_general | solution.py:182
  155.0 3.9 %fusion = f32[3,256,256]{2,0,1:T(4,128)S(1)} fusion(f32[16,256,256]{2,1,0:T(8,128)S(1)} %fusion.16, pred[1,16]{1,0:T(4,128)(4,1)S(1)} %get-tuple-element.57, pred[1,16]{1,0:T(4,128)(4,1)S(1)} %get-tuple-element.56, pred[1,16]{1,0:T(4,128)(4,1)S(1)} %get-tuple-element.43), kind=kOutput, calls=%fused_computation | convolution fusion | flops 37748832 | bytes 4980784 | tf_op jit(solution)/shard_map/mt,tkl->mkl/dot_general | solution.py:190
  159.4 0.8 copy.35
  160.2 0.9 copy.34
  161.1 3.6 %collective-permute-start.17 = (f32[256,256]{0,1:T(8,128)}, f32[256,256]{0,1:T(8,128)S(1)}, u32[]{:S(2)}, u32[]{:S(2)}) collective-permute-start(f32[256,256]{0,1:T(8,128)} %bitcast.30), channel_id=1, source_target_pairs={{0,2},{1,3},{2,4},{3,5},{4,6},{5,7},{6,8},{7,9},{8,10},{9,11},{10,... | collective-permute-start | bytes 786440 | tf_op jit(solution)/shard_map/ppermute | solution.py:98
  164.7 4.7 %collective-permute-start.16 = (f32[256,256]{0,1:T(8,128)}, f32[256,256]{0,1:T(8,128)S(1)}, u32[]{:S(2)}, u32[]{:S(2)}) collective-permute-start(f32[256,256]{0,1:T(8,128)} %bitcast.30), channel_id=1, source_target_pairs={{0,1},{1,2},{2,3},{3,4},{4,5},{5,6},{6,7},{7,8},{8,9},{9,10},{10,1... | collective-permute-start | bytes 786440 | tf_op jit(solution)/shard_map/ppermute | solution.py:98
  169.4 4.0 %collective-permute-start.19 = (f32[256,256]{0,1:T(8,128)}, f32[256,256]{0,1:T(8,128)S(1)}, u32[]{:S(2)}, u32[]{:S(2)}) collective-permute-start(f32[256,256]{0,1:T(8,128)} %bitcast.29), channel_id=1, source_target_pairs={{2,0},{3,1},{4,2},{5,3},{6,4},{7,5},{8,6},{9,7},{10,8},{11,9},{12,... | collective-permute-start | bytes 786440 | tf_op jit(solution)/shard_map/ppermute | solution.py:98
  173.4 2.4 collective-permute-start.18
  175.8 2.1 fusion.7
  181.9 0.9 dynamic-slice_add_fusion
  182.9 2.9 %collective-permute-done.16 = f32[256,256]{0,1:T(8,128)S(1)} collective-permute-done((f32[256,256]{0,1:T(8,128)}, f32[256,256]{0,1:T(8,128)S(1)}, u32[]{:S(2)}, u32[]{:S(2)}) %collective-permute-start.16) | collective-permute-done | bytes 262176 | tf_op jit(solution)/shard_map/ppermute | solution.py:98
  185.8 5.6 %collective-permute-done.18 = f32[256,256]{0,1:T(8,128)} collective-permute-done((f32[256,256]{0,1:T(8,128)}, f32[256,256]{0,1:T(8,128)}, u32[]{:S(2)}, u32[]{:S(2)}) %collective-permute-start.18) | collective-permute-done | bytes 262176 | tf_op jit(solution)/shard_map/ppermute | solution.py:98
  191.4 1.1 fusion.44
  192.6 11.7 %cholesky.44 = f32[128,128]{1,0:T(8,128)S(1)} custom-call(f32[128,128]{1,0:T(8,128)S(1)} %fusion.60), custom_call_target="Cholesky" | custom-call | tf_op jit(solution)/shard_map/jit(cholesky)/cholesky | solution.py:85
  204.4 0.6 compare_reduce_fusion.1
  205.0 0.7 fusion.50
  205.7 9.8 %custom-call.6 = f32[1,128,128]{1,2,0:T(8,128)S(1)} custom-call(f32[1,128,128]{2,1,0:T(8,128)S(1)} %fusion.50), custom_call_target="InvertDiagBlocksLowerTriangular" | custom-call | tf_op jit(solution)/shard_map/jit(_solve_triangular)/triangular_solve | solution.py:80
  216.9 11.7 %cholesky.55 = f32[128,128]{1,0:T(8,128)S(1)} custom-call(f32[128,128]{1,0:T(8,128)S(1)} %fusion.58), custom_call_target="Cholesky" | custom-call | tf_op jit(solution)/shard_map/jit(cholesky)/cholesky | solution.py:88
  228.7 0.6 compare_reduce_fusion
  229.3 0.7 fusion.51
  230.0 9.8 %custom-call.7 = f32[1,128,128]{1,2,0:T(8,128)S(1)} custom-call(f32[1,128,128]{2,1,0:T(8,128)S(1)} %fusion.51), custom_call_target="InvertDiagBlocksLowerTriangular" | custom-call | tf_op jit(solution)/shard_map/jit(_solve_triangular)/triangular_solve | solution.py:80
  240.9 0.8 copy.30
  (65 shorter events, 6.4 us)
Async XLA Ops:
  1.2 5.3 %collective-permute-start = (f32[2,2048]{1,0:T(2,128)S(1)}, f32[2,2048]{1,0:T(2,128)S(1)}, u32[]{:S(2)}, u32[]{:S(2)}) collective-permute-start(f32[2,2048]{1,0:T(2,128)S(1)} %pad_maximum_fusion.1), channel_id=1, source_target_pairs={{0,32},{32,0},{64,96},{96,64},{128,160},{160,128},{192,224},{224,1... | collective-permute-start | bytes 49160 | tf_op jit(solution)/shard_map/ppermute | solution.py:31
  6.5 6.0 %collective-permute-start.1 = (f32[2,2048]{1,0:T(2,128)S(1)}, f32[2,2048]{1,0:T(2,128)S(1)}, u32[]{:S(2)}, u32[]{:S(2)}) collective-permute-start(f32[2,2048]{1,0:T(2,128)S(1)} %fusion.84), channel_id=1, source_target_pairs={{0,64},{32,96},{64,0},{96,32},{128,192},{160,224},{192,128},{224,1... | collective-permute-start | bytes 49160 | tf_op jit(solution)/shard_map/ppermute | solution.py:31
  12.6 7.8 %collective-permute-start.2 = (f32[2,2048]{1,0:T(2,128)S(1)}, f32[2,2048]{1,0:T(2,128)S(1)}, u32[]{:S(2)}, u32[]{:S(2)}) collective-permute-start(f32[2,2048]{1,0:T(2,128)S(1)} %fusion.98), channel_id=1, source_target_pairs={{0,128},{32,160},{64,192},{96,224},{128,0},{160,32},{192,64},{224,... | collective-permute-start | bytes 49160 | tf_op jit(solution)/shard_map/ppermute | solution.py:31
  20.4 17.2 %collective-permute-start.3 = (f32[2,2048]{1,0:T(2,128)S(1)}, f32[2,2048]{1,0:T(2,128)S(1)}, u32[]{:S(2)}, u32[]{:S(2)}) collective-permute-start(f32[2,2048]{1,0:T(2,128)S(1)} %add.224), channel_id=1, source_target_pairs={{0,256},{32,288},{64,320},{96,352},{128,384},{160,416},{192,448},{... | collective-permute-start | bytes 49160 | tf_op jit(solution)/shard_map/ppermute | solution.py:31
  38.7 9.4 %copy-start = (s32[3]{0:T(128)S(1)}, s32[3]{0:T(128)}, u32[]{:S(2)}) copy-start(s32[3]{0:T(128)} %constant.189.clone.1) | copy-start | bytes 40
  40.1 15.5 %collective-permute-start.5 = (f32[64,256]{1,0:T(8,128)S(1)}, f32[64,256]{1,0:T(8,128)S(1)}, u32[]{:S(2)}, u32[]{:S(2)}) collective-permute-start(f32[64,256]{1,0:T(8,128)S(1)} %get-tuple-element.35), channel_id=1, source_target_pairs={{0,2},{1,3},{2,4},{3,5},{4,6},{5,7},{6,8},{7,9},{8,10},{9,11},{10,... | collective-permute-start | bytes 196616 | tf_op jit(solution)/shard_map/ppermute | solution.py:98
  44.6 11.0 %collective-permute-start.4 = (f32[64,256]{1,0:T(8,128)S(1)}, f32[64,256]{1,0:T(8,128)S(1)}, u32[]{:S(2)}, u32[]{:S(2)}) collective-permute-start(f32[64,256]{1,0:T(8,128)S(1)} %get-tuple-element.35), channel_id=1, source_target_pairs={{0,1},{1,2},{2,3},{3,4},{4,5},{5,6},{6,7},{7,8},{8,9},{9,10},{10,1... | collective-permute-start | bytes 196616 | tf_op jit(solution)/shard_map/ppermute | solution.py:98
  48.9 7.2 %collective-permute-start.7 = (f32[64,256]{1,0:T(8,128)S(1)}, f32[64,256]{1,0:T(8,128)S(1)}, u32[]{:S(2)}, u32[]{:S(2)}) collective-permute-start(f32[64,256]{1,0:T(8,128)S(1)} %get-tuple-element.36), channel_id=1, source_target_pairs={{2,0},{3,1},{4,2},{5,3},{6,4},{7,5},{8,6},{9,7},{10,8},{11,9},{12,... | collective-permute-start | bytes 196616 | tf_op jit(solution)/shard_map/ppermute | solution.py:98
  53.3 6.2 %collective-permute-start.6 = (f32[64,256]{1,0:T(8,128)S(1)}, f32[64,256]{1,0:T(8,128)S(1)}, u32[]{:S(2)}, u32[]{:S(2)}) collective-permute-start(f32[64,256]{1,0:T(8,128)S(1)} %get-tuple-element.36), channel_id=1, source_target_pairs={{1,0},{2,1},{3,2},{4,3},{5,4},{6,5},{7,6},{8,7},{9,8},{10,9},{11,1... | collective-permute-start | bytes 196616 | tf_op jit(solution)/shard_map/ppermute | solution.py:98
  61.0 4.7 %collective-permute-start.8 = (f32[1024,256]{1,0:T(8,128)S(1)}, f32[1024,256]{1,0:T(8,128)}, u32[]{:S(2)}, u32[]{:S(2)}) collective-permute-start(f32[1024,256]{1,0:T(8,128)S(1)} %slice_select_fusion), channel_id=1, source_target_pairs={{0,32},{32,0},{64,96},{96,64},{128,160},{160,128},{192,224},{224,1... | collective-permute-start | bytes 3145736 | tf_op jit(solution)/shard_map/ppermute | solution.py:67
  67.2 11.1 %collective-permute-start.9 = (f32[512,256]{1,0:T(8,128)S(1)}, f32[512,256]{1,0:T(8,128)S(1)}, u32[]{:S(2)}, u32[]{:S(2)}) collective-permute-start(f32[512,256]{1,0:T(8,128)S(1)} %slice_select_fusion.1), channel_id=1, source_target_pairs={{0,64},{32,480},{64,0},{96,160},{128,192},{160,96},{192,128},{224,... | collective-permute-start | bytes 1572872 | tf_op jit(solution)/shard_map/ppermute | solution.py:67
  78.5 14.1 %collective-permute-start.10 = (f32[256,256]{1,0:T(8,128)S(1)}, f32[256,256]{1,0:T(8,128)S(1)}, u32[]{:S(2)}, u32[]{:S(2)}) collective-permute-start(f32[256,256]{1,0:T(8,128)S(1)} %slice_select_fusion.2), channel_id=1, source_target_pairs={{0,128},{32,160},{64,192},{96,480},{128,0},{160,32},{192,64},{224,... | collective-permute-start | bytes 786440 | tf_op jit(solution)/shard_map/ppermute | solution.py:67
  92.6 10.8 %collective-permute-start.11 = (f32[128,256]{1,0:T(8,128)S(1)}, f32[128,256]{1,0:T(8,128)S(1)}, u32[]{:S(2)}, u32[]{:S(2)}) collective-permute-start(f32[128,256]{1,0:T(8,128)S(1)} %slice_select_fusion.3), channel_id=1, source_target_pairs={{0,256},{32,288},{64,320},{96,352},{128,384},{160,416},{192,448},{... | collective-permute-start | bytes 393224 | tf_op jit(solution)/shard_map/ppermute | solution.py:67
  103.4 10.9 %collective-permute-start.12 = (f32[128,256]{1,0:T(8,128)S(1)}, f32[128,256]{1,0:T(8,128)S(1)}, u32[]{:S(2)}, u32[]{:S(2)}) collective-permute-start(f32[128,256]{1,0:T(8,128)S(1)} %select_add_fusion.3), channel_id=1, source_target_pairs={{0,256},{32,288},{64,320},{96,352},{128,384},{160,416},{192,448},{... | collective-permute-start | bytes 393224 | tf_op jit(solution)/shard_map/ppermute | solution.py:69
  114.3 12.8 %collective-permute-start.13 = (f32[256,256]{1,0:T(8,128)S(1)}, f32[256,256]{1,0:T(8,128)S(1)}, u32[]{:S(2)}, u32[]{:S(2)}) collective-permute-start(f32[256,256]{1,0:T(8,128)S(1)} %maximum_select_fusion.3), channel_id=1, source_target_pairs={{0,128},{32,160},{64,192},{96,480},{128,0},{160,32},{192,64},{224,... | collective-permute-start | bytes 786440 | tf_op jit(solution)/shard_map/ppermute | solution.py:69
  127.1 11.1 %collective-permute-start.14 = (f32[512,256]{1,0:T(8,128)S(1)}, f32[512,256]{1,0:T(8,128)S(1)}, u32[]{:S(2)}, u32[]{:S(2)}) collective-permute-start(f32[512,256]{1,0:T(8,128)S(1)} %maximum_select_fusion.2), channel_id=1, source_target_pairs={{0,64},{32,480},{64,0},{96,160},{128,192},{160,96},{192,128},{224,... | collective-permute-start | bytes 1572872 | tf_op jit(solution)/shard_map/ppermute | solution.py:69
  138.3 4.7 %collective-permute-start.15 = (f32[1024,256]{1,0:T(8,128)S(1)}, f32[1024,256]{1,0:T(8,128)}, u32[]{:S(2)}, u32[]{:S(2)}) collective-permute-start(f32[1024,256]{1,0:T(8,128)S(1)} %maximum_select_fusion.1), channel_id=1, source_target_pairs={{0,32},{32,0},{64,96},{96,64},{128,160},{160,128},{192,224},{224,1... | collective-permute-start | bytes 3145736 | tf_op jit(solution)/shard_map/ppermute | solution.py:69
  158.8 21.7 %copy-start.1 = (s32[64]{0:T(128)S(1)}, s32[64]{0:T(128)}, u32[]{:S(2)}) copy-start(s32[64]{0:T(128)} %param.11) | copy-start | bytes 772
  161.1 21.8 %collective-permute-start.17 = (f32[256,256]{0,1:T(8,128)}, f32[256,256]{0,1:T(8,128)S(1)}, u32[]{:S(2)}, u32[]{:S(2)}) collective-permute-start(f32[256,256]{0,1:T(8,128)} %bitcast.30), channel_id=1, source_target_pairs={{0,2},{1,3},{2,4},{3,5},{4,6},{5,7},{6,8},{7,9},{8,10},{9,11},{10,... | collective-permute-start | bytes 786440 | tf_op jit(solution)/shard_map/ppermute | solution.py:98
  164.7 21.1 %collective-permute-start.16 = (f32[256,256]{0,1:T(8,128)}, f32[256,256]{0,1:T(8,128)S(1)}, u32[]{:S(2)}, u32[]{:S(2)}) collective-permute-start(f32[256,256]{0,1:T(8,128)} %bitcast.30), channel_id=1, source_target_pairs={{0,1},{1,2},{2,3},{3,4},{4,5},{5,6},{6,7},{7,8},{8,9},{9,10},{10,1... | collective-permute-start | bytes 786440 | tf_op jit(solution)/shard_map/ppermute | solution.py:98
  169.4 16.4 %collective-permute-start.19 = (f32[256,256]{0,1:T(8,128)}, f32[256,256]{0,1:T(8,128)S(1)}, u32[]{:S(2)}, u32[]{:S(2)}) collective-permute-start(f32[256,256]{0,1:T(8,128)} %bitcast.29), channel_id=1, source_target_pairs={{2,0},{3,1},{4,2},{5,3},{6,4},{7,5},{8,6},{9,7},{10,8},{11,9},{12,... | collective-permute-start | bytes 786440 | tf_op jit(solution)/shard_map/ppermute | solution.py:98
  173.4 18.0 %collective-permute-start.18 = (f32[256,256]{0,1:T(8,128)}, f32[256,256]{0,1:T(8,128)}, u32[]{:S(2)}, u32[]{:S(2)}) collective-permute-start(f32[256,256]{0,1:T(8,128)} %bitcast.29), channel_id=1, source_target_pairs={{1,0},{2,1},{3,2},{4,3},{5,4},{6,5},{7,6},{8,7},{9,8},{10,9},{11,1... | collective-permute-start | bytes 786440 | tf_op jit(solution)/shard_map/ppermute | solution.py:98

commit v7 on v5

--- a/solution.py
+++ b/solution.py
@@ -57,15 +57,18 @@
     return steps
 
 
-def halving_allreduce(x, axis, count):
+def halving_allreduce(x, axis, count, doubled_steps=1):
     steps = ind_steps(count, lax.axis_index(axis))
-    for pairs, high in steps:
+    split, doubled = steps[: len(steps) - doubled_steps], steps[len(steps) - doubled_steps :]
+    for pairs, high in split:
         half = x.shape[0] // 2
         lower, upper = x[:half], x[half:]
         send = jnp.where(high, lower, upper)
         keep = jnp.where(high, upper, lower)
         x = keep + lax.ppermute(send, axis, pairs)
-    for pairs, high in reversed(steps):
+    for pairs, high in doubled:
+        x = x + lax.ppermute(x, axis, pairs)
+    for pairs, high in reversed(split):
         got = lax.ppermute(x, axis, pairs)
         x = jnp.where(high, jnp.concatenate([got, x], 0), jnp.concatenate([x, got], 0))
     return x
@@ -103,6 +106,7 @@
 
 
 def halo(head_part, tail_part, blk_index, blk_count, reach, edge_blocks, first_block, last_block):
+    head_part, tail_part = lax.optimization_barrier((head_part, tail_part))
     from_lower = []
     from_upper = []
     for step in range(1, reach + 1):
@@ -178,10 +182,10 @@
     row_start = ind_index * row_slice
     my_rows = lax.dynamic_slice_in_dim(projected, row_start, row_slice, 0)
     my_slot = unit_slot[row_start // UNIT]
-    pick = jnp.stack([col_slot == 0, col_slot == last_slot, col_slot == my_slot]).astype(jnp.float32)
+    edges = jnp.stack([col_slot == 0, col_slot == last_slot]).astype(jnp.float32)
     grams = jnp.einsum(
         "mc,ck,cl->mkl",
-        pick,
+        edges,
         projected,
         projected,
         precision=lax.Precision.HIGHEST,
@@ -190,7 +194,15 @@
     head_in, tail_in = halo(
         grams[0], grams[1], blk_index, blk_count, reach, edge_blocks, first_block, last_block
     )
-    gram = grams[2]
+    own = (col_slot == my_slot).astype(jnp.float32)
+    gram = jnp.einsum(
+        "c,ck,cl->kl",
+        own,
+        projected,
+        projected,
+        precision=lax.Precision.HIGHEST,
+        preferred_element_type=jnp.float32,
+    )
     gram = gram + jnp.where(my_slot == 0, head_in, 0.0)
     gram = gram + jnp.where(my_slot == last_slot, tail_in, 0.0)
     my_block = first_block + my_slot

time: 243 us -> 234 us (0.963)
  starting transfers between devices: 84.8 us -> 74.9 us
    ppermute x0 -> x1, waiting for transfers between devices: none -> 13.2 us  [halving_allreduce(): x = x + lax.ppermute(x, axis, pairs)]
    ppermute x4 -> x3, starting transfers between devices: 17.3 us -> 9.61 us  [halving_allreduce(): x = keep + lax.ppermute(send, axis, pairs)]
    ppermute x4 -> x3, waiting for transfers between devices: 25.1 us -> 17.8 us  [halving_allreduce(): got = lax.ppermute(x, axis, pairs)]
    ppermute x4 -> x3, waiting for transfers between devices: 25.6 us -> 20.1 us  [halving_allreduce(): x = keep + lax.ppermute(send, axis, pairs)]
    ppermute x4 -> x3, starting transfers between devices: 16.3 us -> 12.2 us  [halving_allreduce(): got = lax.ppermute(x, axis, pairs)]
    dot_general x1 -> x2, matrix products: 7.46 us -> 9.36 us  [the longest x1 5.59 us: on_device(): jnp.einsum('mc,ck,cl->mkl', edges, projected, projected, precision=lax.Pr...]
  transfers between devices with their start and end apart: 20 -> 19, of which waited for: 14 -> 14; matrix products, arithmetic and copies ran while one was open for 3% -> 3% of each run, Pallas kernels for 0% -> 0%
where the time goes in v7:
time: 234 us; the launch traced here: 232 us
  starting transfers between devices  74.9 us (32%)
  waiting for transfers between devices  68.7 us (29%)
  other arithmetic  57.2 us (24%)
  matrix products  13.8 us (6%)
  between operations  10.7 us (5%)
  local copies, waits for them, and re-layouts  6.39 us (3%)
    ppermute x8, starting transfers between devices, shift(): return lax.ppermute(x, axis, pairs)  29.5 us
    ppermute x4, starting transfers between devices, xor_allreduce(): x = x + lax.ppermute(x, axis, [(j, j ^ mask) for j in range(count)])  21.6 us
    another operation x4, other arithmetic, lower_inverse(): return jax.scipy.linalg.solve_triangular(lower, eye, lower=True)  20.9 us
    ppermute x3, waiting for transfers between devices, halving_allreduce(): x = keep + lax.ppermute(send, axis, pairs)  20.1 us
    ppermute x3, waiting for transfers between devices, halving_allreduce(): got = lax.ppermute(x, axis, pairs)  17.8 us
    ppermute x8, waiting for transfers between devices, shift(): return lax.ppermute(x, axis, pairs)  14.2 us
    ppermute x1, waiting for transfers between devices, halving_allreduce(): x = x + lax.ppermute(x, axis, pairs)  13.2 us
    another operation x3, other arithmetic, basis_rows(): l22 = jnp.linalg.cholesky(gram[half:, half:] - dot_hi(l21, l21.T))  12.6 us
  transfers between devices with their start and end apart: 19, of which 14 were waited for; matrix products, arithmetic and copies ran while one was open for 3% of the time, Pallas kernels for 0%

profile of v7, /device:TPU:6, one launch (start us, length us, event | category | flops | bytes accessed | tf_op | source)
XLA Modules:
  0.0 231.7 jit_solution(13515145392597163725)
XLA Ops:
  0.0 1.1 convert_reduce_fusion
  1.2 1.9 collective-permute-start
  3.1 0.7 multiply_bitcast_fusion
  4.1 0.7 multiply_subtract_fusion
  5.0 0.6 fusion.81
  5.6 0.6 broadcast_compare_fusion.1
  6.5 4.3 %collective-permute-start.1 = (f32[2,2048]{1,0:T(2,128)S(1)}, f32[2,2048]{1,0:T(2,128)S(1)}, u32[]{:S(2)}, u32[]{:S(2)}) collective-permute-start(f32[2,2048]{1,0:T(2,128)S(1)} %fusion.80), channel_id=1, source_target_pairs={{0,64},{32,96},{64,0},{96,32},{128,192},{160,224},{192,128},{224,1... | collective-permute-start | bytes 49160 | tf_op jit(solution)/shard_map/ppermute | solution.py:31
  10.8 1.7 collective-permute-done.1
  12.5 6.1 %collective-permute-start.2 = (f32[2,2048]{1,0:T(2,128)S(1)}, f32[2,2048]{1,0:T(2,128)S(1)}, u32[]{:S(2)}, u32[]{:S(2)}) collective-permute-start(f32[2,2048]{1,0:T(2,128)S(1)} %fusion.94), channel_id=1, source_target_pairs={{0,128},{32,160},{64,192},{96,224},{128,0},{160,32},{192,64},{224,... | collective-permute-start | bytes 49160 | tf_op jit(solution)/shard_map/ppermute | solution.py:31
  18.6 1.7 collective-permute-done.2
  20.3 9.3 %collective-permute-start.3 = (f32[2,2048]{1,0:T(2,128)S(1)}, f32[2,2048]{1,0:T(2,128)S(1)}, u32[]{:S(2)}, u32[]{:S(2)}) collective-permute-start(f32[2,2048]{1,0:T(2,128)S(1)} %add.192), channel_id=1, source_target_pairs={{0,256},{32,288},{64,320},{96,352},{128,384},{160,416},{192,448},{... | collective-permute-start | bytes 49160 | tf_op jit(solution)/shard_map/ppermute | solution.py:31
  31.6 0.7 constant_dynamic-slice_fusion.1
  37.3 1.1 multiply_convert_fusion
  38.4 1.3 fusion.16
  39.8 3.5 %collective-permute-start.4 = (f32[64,256]{1,0:T(8,128)S(1)}, f32[64,256]{1,0:T(8,128)S(1)}, u32[]{:S(2)}, u32[]{:S(2)}) collective-permute-start(f32[64,256]{1,0:T(8,128)S(1)} %get-tuple-element.35), channel_id=1, source_target_pairs={{0,1},{1,2},{2,3},{3,4},{4,5},{5,6},{6,7},{7,8},{8,9},{9,10},{10,1... | collective-permute-start | bytes 196616 | tf_op jit(solution)/shard_map/ppermute | solution.py:101
  43.2 4.5 %collective-permute-start.5 = (f32[64,256]{1,0:T(8,128)S(1)}, f32[64,256]{1,0:T(8,128)S(1)}, u32[]{:S(2)}, u32[]{:S(2)}) collective-permute-start(f32[64,256]{1,0:T(8,128)S(1)} %get-tuple-element.35), channel_id=1, source_target_pairs={{0,2},{1,3},{2,4},{3,5},{4,6},{5,7},{6,8},{7,9},{8,10},{9,11},{10,... | collective-permute-start | bytes 196616 | tf_op jit(solution)/shard_map/ppermute | solution.py:101
  47.8 0.7 and_reduce_fusion
  48.5 4.5 %collective-permute-start.6 = (f32[64,256]{1,0:T(8,128)S(1)}, f32[64,256]{1,0:T(8,128)S(1)}, u32[]{:S(2)}, u32[]{:S(2)}) collective-permute-start(f32[64,256]{1,0:T(8,128)S(1)} %get-tuple-element.36), channel_id=1, source_target_pairs={{1,0},{2,1},{3,2},{4,3},{5,4},{6,5},{7,6},{8,7},{9,8},{10,9},{11,1... | collective-permute-start | bytes 196616 | tf_op jit(solution)/shard_map/ppermute | solution.py:101
  52.9 2.2 collective-permute-start.7
  55.2 0.6 collective-permute-done.6
  55.8 4.6 %collective-permute-done.7 = f32[64,256]{1,0:T(8,128)S(1)} collective-permute-done((f32[64,256]{1,0:T(8,128)S(1)}, f32[64,256]{1,0:T(8,128)S(1)}, u32[]{:S(2)}, u32[]{:S(2)}) %collective-permute-start.7) | collective-permute-done | bytes 65568 | tf_op jit(solution)/shard_map/ppermute | solution.py:101
  60.4 0.6 fusion.56
  61.0 0.8 convolution_bitcast_fusion
  61.9 1.9 collective-permute-start.8
  63.8 2.7 %collective-permute-done.8 = f32[1024,256]{1,0:T(8,128)} collective-permute-done((f32[1024,256]{1,0:T(8,128)S(1)}, f32[1024,256]{1,0:T(8,128)}, u32[]{:S(2)}, u32[]{:S(2)}) %collective-permute-start.8) | collective-permute-done | bytes 1048608 | tf_op jit(solution)/shard_map/ppermute | solution.py:68
  66.6 1.4 select_add_fusion
  68.1 3.4 %collective-permute-start.9 = (f32[512,256]{1,0:T(8,128)S(1)}, f32[512,256]{1,0:T(8,128)S(1)}, u32[]{:S(2)}, u32[]{:S(2)}) collective-permute-start(f32[512,256]{1,0:T(8,128)S(1)} %slice_select_fusion.1), channel_id=1, source_target_pairs={{0,64},{32,480},{64,0},{96,160},{128,192},{160,96},{192,128},{224,... | collective-permute-start | bytes 1572872 | tf_op jit(solution)/shard_map/ppermute | solution.py:68
  71.5 7.7 %collective-permute-done.9 = f32[512,256]{1,0:T(8,128)S(1)} collective-permute-done((f32[512,256]{1,0:T(8,128)S(1)}, f32[512,256]{1,0:T(8,128)S(1)}, u32[]{:S(2)}, u32[]{:S(2)}) %collective-permute-start.9) | collective-permute-done | bytes 524320 | tf_op jit(solution)/shard_map/ppermute | solution.py:68
  79.3 4.3 %collective-permute-start.10 = (f32[256,256]{1,0:T(8,128)S(1)}, f32[256,256]{1,0:T(8,128)S(1)}, u32[]{:S(2)}, u32[]{:S(2)}) collective-permute-start(f32[256,256]{1,0:T(8,128)S(1)} %slice_select_fusion.2), channel_id=1, source_target_pairs={{0,128},{32,160},{64,192},{96,480},{128,0},{160,32},{192,64},{224,... | collective-permute-start | bytes 786440 | tf_op jit(solution)/shard_map/ppermute | solution.py:68
  83.6 9.7 %collective-permute-done.10 = f32[256,256]{1,0:T(8,128)S(1)} collective-permute-done((f32[256,256]{1,0:T(8,128)S(1)}, f32[256,256]{1,0:T(8,128)S(1)}, u32[]{:S(2)}, u32[]{:S(2)}) %collective-permute-start.10) | collective-permute-done | bytes 262176 | tf_op jit(solution)/shard_map/ppermute | solution.py:68
  93.4 1.9 collective-permute-start.11
  95.3 13.2 %collective-permute-done.11 = f32[256,256]{1,0:T(8,128)S(1)} collective-permute-done((f32[256,256]{1,0:T(8,128)S(1)}, f32[256,256]{1,0:T(8,128)S(1)}, u32[]{:S(2)}, u32[]{:S(2)}) %collective-permute-start.11) | collective-permute-done | bytes 262176 | tf_op jit(solution)/shard_map/ppermute | solution.py:70
  108.6 6.7 %collective-permute-start.12 = (f32[256,256]{1,0:T(8,128)S(1)}, f32[256,256]{1,0:T(8,128)S(1)}, u32[]{:S(2)}, u32[]{:S(2)}) collective-permute-start(f32[256,256]{1,0:T(8,128)S(1)} %add.211), channel_id=1, source_target_pairs={{0,128},{32,160},{64,192},{96,480},{128,0},{160,32},{192,64},{224,... | collective-permute-start | bytes 786440 | tf_op jit(solution)/shard_map/ppermute | solution.py:72
  115.3 7.9 %collective-permute-done.12 = f32[256,256]{1,0:T(8,128)S(1)} collective-permute-done((f32[256,256]{1,0:T(8,128)S(1)}, f32[256,256]{1,0:T(8,128)S(1)}, u32[]{:S(2)}, u32[]{:S(2)}) %collective-permute-start.12) | collective-permute-done | bytes 262176 | tf_op jit(solution)/shard_map/ppermute | solution.py:72
  123.2 3.6 %collective-permute-start.13 = (f32[512,256]{1,0:T(8,128)S(1)}, f32[512,256]{1,0:T(8,128)S(1)}, u32[]{:S(2)}, u32[]{:S(2)}) collective-permute-start(f32[512,256]{1,0:T(8,128)S(1)} %maximum_select_fusion.2), channel_id=1, source_target_pairs={{0,64},{32,480},{64,0},{96,160},{128,192},{160,96},{192,128},{224,... | collective-permute-start | bytes 1572872 | tf_op jit(solution)/shard_map/ppermute | solution.py:72
  126.8 7.5 %collective-permute-done.13 = f32[512,256]{1,0:T(8,128)S(1)} collective-permute-done((f32[512,256]{1,0:T(8,128)S(1)}, f32[512,256]{1,0:T(8,128)S(1)}, u32[]{:S(2)}, u32[]{:S(2)}) %collective-permute-start.13) | collective-permute-done | bytes 524320 | tf_op jit(solution)/shard_map/ppermute | solution.py:72
  134.4 1.9 collective-permute-start.14
  136.5 2.4 %collective-permute-done.14 = f32[1024,256]{1,0:T(8,128)S(1)} collective-permute-done((f32[1024,256]{1,0:T(8,128)S(1)}, f32[1024,256]{1,0:T(8,128)S(1)}, u32[]{:S(2)}, u32[]{:S(2)}) %collective-permute-start.14) | collective-permute-done | bytes 1048608 | tf_op jit(solution)/shard_map/ppermute | solution.py:72
  139.0 2.3 fusion.11
  141.2 1.9 copy.21
  143.1 5.6 %fusion.21 = f32[2,256,256]{1,2,0:T(8,128)S(1)} fusion(f32[2048,256]{1,0:T(8,128)S(1)} %fusion.11, f32[2048,2]{0,1:T(2,128)S(1)} %fusion.69, f32[2048,256]{0,1:T(8,128)} %copy.21), kind=kOutput, calls=%fused_computation.25 | convolution fusion | flops 3222274048 | bytes 4734976 | tf_op jit(solution)/shard_map/mc,ck,cl->mkl/dot_general | solution.py:186
  148.7 0.7 slice_bitcast_fusion
  149.4 2.0 collective-permute-start.15
  151.5 5.6 %collective-permute-start.16 = (f32[256,256]{0,1:T(8,128)}, f32[256,256]{0,1:T(8,128)S(1)}, u32[]{:S(2)}, u32[]{:S(2)}) collective-permute-start(f32[256,256]{0,1:T(8,128)} %get-tuple-element.37), channel_id=1, source_target_pairs={{0,2},{1,3},{2,4},{3,5},{4,6},{5,7},{6,8},{7,9},{8,10},{9,11},{10,... | collective-permute-start | bytes 786440 | tf_op jit(solution)/shard_map/ppermute | solution.py:101
  157.1 4.9 %collective-permute-start.17 = (f32[256,256]{0,1:T(8,128)S(1)}, f32[256,256]{0,1:T(8,128)S(1)}, u32[]{:S(2)}, u32[]{:S(2)}) collective-permute-start(f32[256,256]{0,1:T(8,128)S(1)} %get-tuple-element.38), channel_id=1, source_target_pairs={{1,0},{2,1},{3,2},{4,3},{5,4},{6,5},{7,6},{8,7},{9,8},{10,9},{11,1... | collective-permute-start | bytes 786440 | tf_op jit(solution)/shard_map/ppermute | solution.py:101
  162.0 2.3 collective-permute-start.18
  164.4 0.6 dynamic_slice.34
  167.5 0.6 dynamic_slice.35
  168.8 0.7 compare_convert_fusion
  169.5 3.2 %collective-permute-done.16 = f32[256,256]{0,1:T(8,128)S(1)} collective-permute-done((f32[256,256]{0,1:T(8,128)}, f32[256,256]{0,1:T(8,128)S(1)}, u32[]{:S(2)}, u32[]{:S(2)}) %collective-permute-start.16) | collective-permute-done | bytes 262176 | tf_op jit(solution)/shard_map/ppermute | solution.py:101
  172.7 1.4 collective-permute-done.17
  174.1 4.4 %collective-permute-done.18 = f32[256,256]{0,1:T(8,128)S(1)} collective-permute-done((f32[256,256]{0,1:T(8,128)S(1)}, f32[256,256]{0,1:T(8,128)S(1)}, u32[]{:S(2)}, u32[]{:S(2)}) %collective-permute-start.18) | collective-permute-done | bytes 262176 | tf_op jit(solution)/shard_map/ppermute | solution.py:101
  178.6 3.8 %fusion.35 = f32[256,256]{0,1:T(8,128)S(1)} fusion(f32[2048,256]{1,0:T(8,128)S(1)} %fusion.11, f32[2048]{0:T(1024)S(1)} %compare_convert_fusion, f32[256,256]{0,1:T(8,128)S(1)} %collective-permute-done.18, f32[256,256]{0,1:T(8,128)S(1)} %collective-permute-done.17, f32[256,256]{0,1:T(8,128)S(1)} %collective-permute-done.16, ...), kind=kOutput, calls=%fused_computation.34 | convolution fusion | flops 1611857920 | bytes 3416074 | tf_op jit(solution)/shard_map/c,ck,cl->kl/dot_general | solution.py:198
  182.5 11.7 %cholesky.44 = f32[128,128]{1,0:T(8,128)S(1)} custom-call(f32[128,128]{1,0:T(8,128)S(1)} %fusion.64), custom_call_target="Cholesky" | custom-call | tf_op jit(solution)/shard_map/jit(cholesky)/cholesky | solution.py:88
  194.2 0.6 compare_reduce_fusion.1
  194.9 0.7 fusion.54
  195.5 9.8 %custom-call.6 = f32[1,128,128]{1,2,0:T(8,128)S(1)} custom-call(f32[1,128,128]{2,1,0:T(8,128)S(1)} %fusion.54), custom_call_target="InvertDiagBlocksLowerTriangular" | custom-call | tf_op jit(solution)/shard_map/jit(_solve_triangular)/triangular_solve | solution.py:83
  205.6 0.3 fusion.59
  206.8 11.9 %cholesky.55 = f32[128,128]{1,0:T(8,128)S(1)} custom-call(f32[128,128]{1,0:T(8,128)S(1)} %fusion.62), custom_call_target="Cholesky" | custom-call | tf_op jit(solution)/shard_map/jit(cholesky)/cholesky | solution.py:91
  218.7 0.6 compare_reduce_fusion
  219.4 0.7 fusion.55
  220.0 9.8 %custom-call.7 = f32[1,128,128]{1,2,0:T(8,128)S(1)} custom-call(f32[1,128,128]{2,1,0:T(8,128)S(1)} %fusion.55), custom_call_target="InvertDiagBlocksLowerTriangular" | custom-call | tf_op jit(solution)/shard_map/jit(_solve_triangular)/triangular_solve | solution.py:83
  229.9 0.3 fusion.50
  230.9 0.8 copy.27
  (59 shorter events, 3.8 us)
Async XLA Ops:
  1.2 5.3 %collective-permute-start = (f32[2,2048]{1,0:T(2,128)S(1)}, f32[2,2048]{1,0:T(2,128)S(1)}, u32[]{:S(2)}, u32[]{:S(2)}) collective-permute-start(f32[2,2048]{1,0:T(2,128)S(1)} %pad_maximum_fusion.1), channel_id=1, source_target_pairs={{0,32},{32,0},{64,96},{96,64},{128,160},{160,128},{192,224},{224,1... | collective-permute-start | bytes 49160 | tf_op jit(solution)/shard_map/ppermute | solution.py:31
  6.5 6.0 %collective-permute-start.1 = (f32[2,2048]{1,0:T(2,128)S(1)}, f32[2,2048]{1,0:T(2,128)S(1)}, u32[]{:S(2)}, u32[]{:S(2)}) collective-permute-start(f32[2,2048]{1,0:T(2,128)S(1)} %fusion.80), channel_id=1, source_target_pairs={{0,64},{32,96},{64,0},{96,32},{128,192},{160,224},{192,128},{224,1... | collective-permute-start | bytes 49160 | tf_op jit(solution)/shard_map/ppermute | solution.py:31
  12.5 7.8 %collective-permute-start.2 = (f32[2,2048]{1,0:T(2,128)S(1)}, f32[2,2048]{1,0:T(2,128)S(1)}, u32[]{:S(2)}, u32[]{:S(2)}) collective-permute-start(f32[2,2048]{1,0:T(2,128)S(1)} %fusion.94), channel_id=1, source_target_pairs={{0,128},{32,160},{64,192},{96,224},{128,0},{160,32},{192,64},{224,... | collective-permute-start | bytes 49160 | tf_op jit(solution)/shard_map/ppermute | solution.py:31
  20.3 16.9 %collective-permute-start.3 = (f32[2,2048]{1,0:T(2,128)S(1)}, f32[2,2048]{1,0:T(2,128)S(1)}, u32[]{:S(2)}, u32[]{:S(2)}) collective-permute-start(f32[2,2048]{1,0:T(2,128)S(1)} %add.192), channel_id=1, source_target_pairs={{0,256},{32,288},{64,320},{96,352},{128,384},{160,416},{192,448},{... | collective-permute-start | bytes 49160 | tf_op jit(solution)/shard_map/ppermute | solution.py:31
  38.4 9.4 %copy-start = (s32[3]{0:T(128)S(1)}, s32[3]{0:T(128)}, u32[]{:S(2)}) copy-start(s32[3]{0:T(128)} %constant.186.clone.1) | copy-start | bytes 40
  39.8 15.4 %collective-permute-start.4 = (f32[64,256]{1,0:T(8,128)S(1)}, f32[64,256]{1,0:T(8,128)S(1)}, u32[]{:S(2)}, u32[]{:S(2)}) collective-permute-start(f32[64,256]{1,0:T(8,128)S(1)} %get-tuple-element.35), channel_id=1, source_target_pairs={{0,1},{1,2},{2,3},{3,4},{4,5},{5,6},{6,7},{7,8},{8,9},{9,10},{10,1... | collective-permute-start | bytes 196616 | tf_op jit(solution)/shard_map/ppermute | solution.py:101
  43.2 12.0 %collective-permute-start.5 = (f32[64,256]{1,0:T(8,128)S(1)}, f32[64,256]{1,0:T(8,128)S(1)}, u32[]{:S(2)}, u32[]{:S(2)}) collective-permute-start(f32[64,256]{1,0:T(8,128)S(1)} %get-tuple-element.35), channel_id=1, source_target_pairs={{0,2},{1,3},{2,4},{3,5},{4,6},{5,7},{6,8},{7,9},{8,10},{9,11},{10,... | collective-permute-start | bytes 196616 | tf_op jit(solution)/shard_map/ppermute | solution.py:101
  48.5 7.4 %collective-permute-start.6 = (f32[64,256]{1,0:T(8,128)S(1)}, f32[64,256]{1,0:T(8,128)S(1)}, u32[]{:S(2)}, u32[]{:S(2)}) collective-permute-start(f32[64,256]{1,0:T(8,128)S(1)} %get-tuple-element.36), channel_id=1, source_target_pairs={{1,0},{2,1},{3,2},{4,3},{5,4},{6,5},{7,6},{8,7},{9,8},{10,9},{11,1... | collective-permute-start | bytes 196616 | tf_op jit(solution)/shard_map/ppermute | solution.py:101
  52.9 7.5 %collective-permute-start.7 = (f32[64,256]{1,0:T(8,128)S(1)}, f32[64,256]{1,0:T(8,128)S(1)}, u32[]{:S(2)}, u32[]{:S(2)}) collective-permute-start(f32[64,256]{1,0:T(8,128)S(1)} %get-tuple-element.36), channel_id=1, source_target_pairs={{2,0},{3,1},{4,2},{5,3},{6,4},{7,5},{8,6},{9,7},{10,8},{11,9},{12,... | collective-permute-start | bytes 196616 | tf_op jit(solution)/shard_map/ppermute | solution.py:101
  61.9 4.7 %collective-permute-start.8 = (f32[1024,256]{1,0:T(8,128)S(1)}, f32[1024,256]{1,0:T(8,128)}, u32[]{:S(2)}, u32[]{:S(2)}) collective-permute-start(f32[1024,256]{1,0:T(8,128)S(1)} %slice_select_fusion), channel_id=1, source_target_pairs={{0,32},{32,0},{64,96},{96,64},{128,160},{160,128},{192,224},{224,1... | collective-permute-start | bytes 3145736 | tf_op jit(solution)/shard_map/ppermute | solution.py:68
  68.1 11.1 %collective-permute-start.9 = (f32[512,256]{1,0:T(8,128)S(1)}, f32[512,256]{1,0:T(8,128)S(1)}, u32[]{:S(2)}, u32[]{:S(2)}) collective-permute-start(f32[512,256]{1,0:T(8,128)S(1)} %slice_select_fusion.1), channel_id=1, source_target_pairs={{0,64},{32,480},{64,0},{96,160},{128,192},{160,96},{192,128},{224,... | collective-permute-start | bytes 1572872 | tf_op jit(solution)/shard_map/ppermute | solution.py:68
  79.3 14.1 %collective-permute-start.10 = (f32[256,256]{1,0:T(8,128)S(1)}, f32[256,256]{1,0:T(8,128)S(1)}, u32[]{:S(2)}, u32[]{:S(2)}) collective-permute-start(f32[256,256]{1,0:T(8,128)S(1)} %slice_select_fusion.2), channel_id=1, source_target_pairs={{0,128},{32,160},{64,192},{96,480},{128,0},{160,32},{192,64},{224,... | collective-permute-start | bytes 786440 | tf_op jit(solution)/shard_map/ppermute | solution.py:68
  93.4 15.1 %collective-permute-start.11 = (f32[256,256]{1,0:T(8,128)S(1)}, f32[256,256]{1,0:T(8,128)S(1)}, u32[]{:S(2)}, u32[]{:S(2)}) collective-permute-start(f32[256,256]{1,0:T(8,128)S(1)} %select_add_fusion.2), channel_id=1, source_target_pairs={{0,256},{32,288},{64,320},{96,352},{128,384},{160,416},{192,448},{... | collective-permute-start | bytes 786440 | tf_op jit(solution)/shard_map/ppermute | solution.py:70
  108.6 14.6 %collective-permute-start.12 = (f32[256,256]{1,0:T(8,128)S(1)}, f32[256,256]{1,0:T(8,128)S(1)}, u32[]{:S(2)}, u32[]{:S(2)}) collective-permute-start(f32[256,256]{1,0:T(8,128)S(1)} %add.211), channel_id=1, source_target_pairs={{0,128},{32,160},{64,192},{96,480},{128,0},{160,32},{192,64},{224,... | collective-permute-start | bytes 786440 | tf_op jit(solution)/shard_map/ppermute | solution.py:72
  123.2 11.1 %collective-permute-start.13 = (f32[512,256]{1,0:T(8,128)S(1)}, f32[512,256]{1,0:T(8,128)S(1)}, u32[]{:S(2)}, u32[]{:S(2)}) collective-permute-start(f32[512,256]{1,0:T(8,128)S(1)} %maximum_select_fusion.2), channel_id=1, source_target_pairs={{0,64},{32,480},{64,0},{96,160},{128,192},{160,96},{192,128},{224,... | collective-permute-start | bytes 1572872 | tf_op jit(solution)/shard_map/ppermute | solution.py:72
  134.4 4.6 %collective-permute-start.14 = (f32[1024,256]{1,0:T(8,128)S(1)}, f32[1024,256]{1,0:T(8,128)S(1)}, u32[]{:S(2)}, u32[]{:S(2)}) collective-permute-start(f32[1024,256]{1,0:T(8,128)S(1)} %maximum_select_fusion.1), channel_id=1, source_target_pairs={{0,32},{32,0},{64,96},{96,64},{128,160},{160,128},{192,224},{224,1... | collective-permute-start | bytes 3145736 | tf_op jit(solution)/shard_map/ppermute | solution.py:72
  143.1 24.4 %copy-start.1 = (s32[64]{0:T(128)S(1)}, s32[64]{0:T(128)}, u32[]{:S(2)}) copy-start(s32[64]{0:T(128)} %param.11) | copy-start | bytes 772
  149.4 20.1 %collective-permute-start.15 = (f32[256,256]{0,1:T(8,128)}, f32[256,256]{0,1:T(8,128)S(1)}, u32[]{:S(2)}, u32[]{:S(2)}) collective-permute-start(f32[256,256]{0,1:T(8,128)} %get-tuple-element.37), channel_id=1, source_target_pairs={{0,1},{1,2},{2,3},{3,4},{4,5},{5,6},{6,7},{7,8},{8,9},{9,10},{10,1... | collective-permute-start | bytes 786440 | tf_op jit(solution)/shard_map/ppermute | solution.py:101
  151.5 21.2 %collective-permute-start.16 = (f32[256,256]{0,1:T(8,128)}, f32[256,256]{0,1:T(8,128)S(1)}, u32[]{:S(2)}, u32[]{:S(2)}) collective-permute-start(f32[256,256]{0,1:T(8,128)} %get-tuple-element.37), channel_id=1, source_target_pairs={{0,2},{1,3},{2,4},{3,5},{4,6},{5,7},{6,8},{7,9},{8,10},{9,11},{10,... | collective-permute-start | bytes 786440 | tf_op jit(solution)/shard_map/ppermute | solution.py:101
  157.1 17.0 %collective-permute-start.17 = (f32[256,256]{0,1:T(8,128)S(1)}, f32[256,256]{0,1:T(8,128)S(1)}, u32[]{:S(2)}, u32[]{:S(2)}) collective-permute-start(f32[256,256]{0,1:T(8,128)S(1)} %get-tuple-element.38), channel_id=1, source_target_pairs={{1,0},{2,1},{3,2},{4,3},{5,4},{6,5},{7,6},{8,7},{9,8},{10,9},{11,1... | collective-permute-start | bytes 786440 | tf_op jit(solution)/shard_map/ppermute | solution.py:101
  162.0 16.5 %collective-permute-start.18 = (f32[256,256]{0,1:T(8,128)S(1)}, f32[256,256]{0,1:T(8,128)S(1)}, u32[]{:S(2)}, u32[]{:S(2)}) collective-permute-start(f32[256,256]{0,1:T(8,128)S(1)} %get-tuple-element.38), channel_id=1, source_target_pairs={{2,0},{3,1},{4,2},{5,3},{6,4},{7,5},{8,6},{9,7},{10,8},{11,9},{12,... | collective-permute-start | bytes 786440 | tf_op jit(solution)/shard_map/ppermute | solution.py:101

commit v8 on v7

--- a/solution.py
+++ b/solution.py
@@ -1,9 +1,8 @@
-import math
-
 import jax
 import jax.numpy as jnp
 from jax import lax
 from jax.sharding import PartitionSpec as P
+
 
 K = 256
 UNIT = 128
@@ -85,15 +84,29 @@
 
 def basis_rows(gram, rows):
     half = gram.shape[0] // 2
-    l11 = jnp.linalg.cholesky(gram[:half, :half])
+    l11 = lax.linalg.cholesky(gram[:half, :half], symmetrize_input=False)
     m11 = lower_inverse(l11)
     l21 = dot_hi(gram[half:, :half], m11.T)
-    l22 = jnp.linalg.cholesky(gram[half:, half:] - dot_hi(l21, l21.T))
+    l22 = lax.linalg.cholesky(gram[half:, half:] - dot_hi(l21, l21.T), symmetrize_input=False)
     m22 = lower_inverse(l22)
     m21 = -dot_hi(m22, dot_hi(l21, m11))
     left = dot_hi(rows[:, :half], m11.T)
     right = dot_hi(rows[:, :half], m21.T) + dot_hi(rows[:, half:], m22.T)
     return jnp.concatenate([left, right], 1)
+
+
+def pack_symmetric(gram):
+    half = gram.shape[0] // 2
+    corner = gram[half:, half:].reshape(half // 2, gram.shape[1])
+    return jnp.concatenate([gram[:half], corner], 0)
+
+
+def unpack_symmetric(packed):
+    half = packed.shape[1] // 2
+    top = packed[:half]
+    corner = packed[half:].reshape(half, half)
+    bottom = jnp.concatenate([top[:, half:].T, corner], 1)
+    return jnp.concatenate([top, bottom], 0)
 
 
 def shift(x, axis, count, step):
@@ -192,8 +205,17 @@
         preferred_element_type=jnp.float32,
     )
     head_in, tail_in = halo(
-        grams[0], grams[1], blk_index, blk_count, reach, edge_blocks, first_block, last_block
-    )
+        pack_symmetric(grams[0]),
+        pack_symmetric(grams[1]),
+        blk_index,
+        blk_count,
+        reach,
+        edge_blocks,
+        first_block,
+        last_block,
+    )
+    head_in = unpack_symmetric(head_in)
+    tail_in = unpack_symmetric(tail_in)
     own = (col_slot == my_slot).astype(jnp.float32)
     gram = jnp.einsum(
         "c,ck,cl->kl",
@@ -203,6 +225,7 @@
         precision=lax.Precision.HIGHEST,
         preferred_element_type=jnp.float32,
     )
+    gram = lax.optimization_barrier(gram)
     gram = gram + jnp.where(my_slot == 0, head_in, 0.0)
     gram = gram + jnp.where(my_slot == last_slot, tail_in, 0.0)
     my_block = first_block + my_slot

time: 234 us -> 229 us (0.979)
  the two profiles are of different devices: /device:TPU:6 before, /device:TPU:14 now
where the time goes in v8:
time: 229 us; the launch traced here: 228 us
  starting transfers between devices  75.2 us (33%)
  waiting for transfers between devices  64.5 us (28%)
  other arithmetic  57.5 us (25%)
  matrix products  13.8 us (6%)
  between operations  10.9 us (5%)
  local copies, waits for them, and re-layouts  6.41 us (3%)
    ppermute x8, starting transfers between devices, shift(): return lax.ppermute(x, axis, pairs)  29.8 us
    ppermute x4, starting transfers between devices, xor_allreduce(): x = x + lax.ppermute(x, axis, [(j, j ^ mask) for j in range(count)])  21.6 us
    another operation x4, other arithmetic, lower_inverse(): return jax.scipy.linalg.solve_triangular(lower, eye, lower=True)  20.9 us
    ppermute x3, waiting for transfers between devices, halving_allreduce(): x = keep + lax.ppermute(send, axis, pairs)  20.1 us
    ppermute x8, waiting for transfers between devices, shift(): return lax.ppermute(x, axis, pairs)  15.3 us
    ppermute x1, waiting for transfers between devices, halving_allreduce(): x = x + lax.ppermute(x, axis, pairs)  13.2 us
    another operation x3, other arithmetic, basis_rows(): lax.linalg.cholesky(gram[half:, half:] - dot_hi(l21, l21.T), symmetrize_i...  12.6 us
    ppermute x3, waiting for transfers between devices, halving_allreduce(): got = lax.ppermute(x, axis, pairs)  12.5 us
  transfers between devices with their start and end apart: 19, of which 13 were waited for; matrix products, arithmetic and copies ran while one was open for 5% of the time, Pallas kernels for 0%

profile of v8, /device:TPU:14, one launch (start us, length us, event | category | flops | bytes accessed | tf_op | source)
XLA Modules:
  0.0 228.3 jit_solution(1088370979651359180)
XLA Ops:
  0.0 1.1 convert_reduce_fusion
  1.2 1.9 collective-permute-start
  3.1 0.7 multiply_bitcast_fusion
  4.1 0.7 multiply_subtract_fusion
  5.0 0.6 fusion.73
  5.6 0.6 broadcast_compare_fusion.1
  6.4 4.3 %collective-permute-start.1 = (f32[2,2048]{1,0:T(2,128)S(1)}, f32[2,2048]{1,0:T(2,128)S(1)}, u32[]{:S(2)}, u32[]{:S(2)}) collective-permute-start(f32[2,2048]{1,0:T(2,128)S(1)} %fusion.72), channel_id=1, source_target_pairs={{0,64},{32,96},{64,0},{96,32},{128,192},{160,224},{192,128},{224,1... | collective-permute-start | bytes 49160 | tf_op jit(solution)/shard_map/ppermute | solution.py:30
  10.7 1.7 collective-permute-done.1
  12.5 6.1 %collective-permute-start.2 = (f32[2,2048]{1,0:T(2,128)S(1)}, f32[2,2048]{1,0:T(2,128)S(1)}, u32[]{:S(2)}, u32[]{:S(2)}) collective-permute-start(f32[2,2048]{1,0:T(2,128)S(1)} %fusion.86), channel_id=1, source_target_pairs={{0,128},{32,160},{64,192},{96,224},{128,0},{160,32},{192,64},{224,... | collective-permute-start | bytes 49160 | tf_op jit(solution)/shard_map/ppermute | solution.py:30
  18.6 1.7 collective-permute-done.2
  20.3 9.3 %collective-permute-start.3 = (f32[2,2048]{1,0:T(2,128)S(1)}, f32[2,2048]{1,0:T(2,128)S(1)}, u32[]{:S(2)}, u32[]{:S(2)}) collective-permute-start(f32[2,2048]{1,0:T(2,128)S(1)} %add.188), channel_id=1, source_target_pairs={{0,256},{32,288},{64,320},{96,352},{128,384},{160,416},{192,448},{... | collective-permute-start | bytes 49160 | tf_op jit(solution)/shard_map/ppermute | solution.py:30
  31.5 0.7 constant_dynamic-slice_fusion.1
  37.2 1.1 multiply_convert_fusion
  38.3 1.3 fusion.16
  39.7 3.5 %collective-permute-start.4 = (f32[64,256]{1,0:T(8,128)S(1)}, f32[64,256]{1,0:T(8,128)S(1)}, u32[]{:S(2)}, u32[]{:S(2)}) collective-permute-start(f32[64,256]{1,0:T(8,128)S(1)} %get-tuple-element.35), channel_id=1, source_target_pairs={{0,1},{1,2},{2,3},{3,4},{4,5},{5,6},{6,7},{7,8},{8,9},{9,10},{10,1... | collective-permute-start | bytes 196616 | tf_op jit(solution)/shard_map/ppermute | solution.py:114
  43.2 5.7 %collective-permute-start.5 = (f32[64,256]{1,0:T(8,128)S(1)}, f32[64,256]{1,0:T(8,128)S(1)}, u32[]{:S(2)}, u32[]{:S(2)}) collective-permute-start(f32[64,256]{1,0:T(8,128)S(1)} %get-tuple-element.35), channel_id=1, source_target_pairs={{0,2},{1,3},{2,4},{3,5},{4,6},{5,7},{6,8},{7,9},{8,10},{9,11},{10,... | collective-permute-start | bytes 196616 | tf_op jit(solution)/shard_map/ppermute | solution.py:114
  48.9 0.8 and_reduce_fusion
  49.7 1.9 collective-permute-start.6
  51.6 3.6 %collective-permute-start.7 = (f32[64,256]{1,0:T(8,128)S(1)}, f32[64,256]{1,0:T(8,128)S(1)}, u32[]{:S(2)}, u32[]{:S(2)}) collective-permute-start(f32[64,256]{1,0:T(8,128)S(1)} %get-tuple-element.36), channel_id=1, source_target_pairs={{2,0},{3,1},{4,2},{5,3},{6,4},{7,5},{8,6},{9,7},{10,8},{11,9},{12,... | collective-permute-start | bytes 196616 | tf_op jit(solution)/shard_map/ppermute | solution.py:114
  55.2 1.2 collective-permute-done.6
  56.5 2.5 %collective-permute-done.7 = f32[64,256]{1,0:T(8,128)S(1)} collective-permute-done((f32[64,256]{1,0:T(8,128)S(1)}, f32[64,256]{1,0:T(8,128)S(1)}, u32[]{:S(2)}, u32[]{:S(2)}) %collective-permute-start.7) | collective-permute-done | bytes 65568 | tf_op jit(solution)/shard_map/ppermute | solution.py:114
  59.0 0.7 fusion.50
  59.7 0.8 convolution_bitcast_fusion
  60.6 1.9 collective-permute-start.8
  62.5 2.7 %collective-permute-done.8 = f32[1024,256]{1,0:T(8,128)} collective-permute-done((f32[1024,256]{1,0:T(8,128)S(1)}, f32[1024,256]{1,0:T(8,128)}, u32[]{:S(2)}, u32[]{:S(2)}) %collective-permute-start.8) | collective-permute-done | bytes 1048608 | tf_op jit(solution)/shard_map/ppermute | solution.py:67
  65.3 1.4 select_add_fusion
  66.8 3.4 %collective-permute-start.9 = (f32[512,256]{1,0:T(8,128)S(1)}, f32[512,256]{1,0:T(8,128)S(1)}, u32[]{:S(2)}, u32[]{:S(2)}) collective-permute-start(f32[512,256]{1,0:T(8,128)S(1)} %slice_select_fusion.1), channel_id=1, source_target_pairs={{0,64},{32,480},{64,0},{96,160},{128,192},{160,96},{192,128},{224,... | collective-permute-start | bytes 1572872 | tf_op jit(solution)/shard_map/ppermute | solution.py:67
  70.2 7.7 %collective-permute-done.9 = f32[512,256]{1,0:T(8,128)S(1)} collective-permute-done((f32[512,256]{1,0:T(8,128)S(1)}, f32[512,256]{1,0:T(8,128)S(1)}, u32[]{:S(2)}, u32[]{:S(2)}) %collective-permute-start.9) | collective-permute-done | bytes 524320 | tf_op jit(solution)/shard_map/ppermute | solution.py:67
  78.0 4.3 %collective-permute-start.10 = (f32[256,256]{1,0:T(8,128)S(1)}, f32[256,256]{1,0:T(8,128)S(1)}, u32[]{:S(2)}, u32[]{:S(2)}) collective-permute-start(f32[256,256]{1,0:T(8,128)S(1)} %slice_select_fusion.2), channel_id=1, source_target_pairs={{0,128},{32,160},{64,192},{96,480},{128,0},{160,32},{192,64},{224,... | collective-permute-start | bytes 786440 | tf_op jit(solution)/shard_map/ppermute | solution.py:67
  82.3 9.7 %collective-permute-done.10 = f32[256,256]{1,0:T(8,128)S(1)} collective-permute-done((f32[256,256]{1,0:T(8,128)S(1)}, f32[256,256]{1,0:T(8,128)S(1)}, u32[]{:S(2)}, u32[]{:S(2)}) %collective-permute-start.10) | collective-permute-done | bytes 262176 | tf_op jit(solution)/shard_map/ppermute | solution.py:67
  92.1 1.9 collective-permute-start.11
  94.0 13.2 %collective-permute-done.11 = f32[256,256]{1,0:T(8,128)S(1)} collective-permute-done((f32[256,256]{1,0:T(8,128)S(1)}, f32[256,256]{1,0:T(8,128)S(1)}, u32[]{:S(2)}, u32[]{:S(2)}) %collective-permute-start.11) | collective-permute-done | bytes 262176 | tf_op jit(solution)/shard_map/ppermute | solution.py:69
  107.3 6.7 %collective-permute-start.12 = (f32[256,256]{1,0:T(8,128)S(1)}, f32[256,256]{1,0:T(8,128)S(1)}, u32[]{:S(2)}, u32[]{:S(2)}) collective-permute-start(f32[256,256]{1,0:T(8,128)S(1)} %add.207), channel_id=1, source_target_pairs={{0,128},{32,160},{64,192},{96,480},{128,0},{160,32},{192,64},{224,... | collective-permute-start | bytes 786440 | tf_op jit(solution)/shard_map/ppermute | solution.py:71
  114.0 7.9 %collective-permute-done.12 = f32[256,256]{1,0:T(8,128)S(1)} collective-permute-done((f32[256,256]{1,0:T(8,128)S(1)}, f32[256,256]{1,0:T(8,128)S(1)}, u32[]{:S(2)}, u32[]{:S(2)}) %collective-permute-start.12) | collective-permute-done | bytes 262176 | tf_op jit(solution)/shard_map/ppermute | solution.py:71
  121.9 3.7 %collective-permute-start.13 = (f32[512,256]{1,0:T(8,128)S(1)}, f32[512,256]{1,0:T(8,128)S(1)}, u32[]{:S(2)}, u32[]{:S(2)}) collective-permute-start(f32[512,256]{1,0:T(8,128)S(1)} %maximum_select_fusion.2), channel_id=1, source_target_pairs={{0,64},{32,480},{64,0},{96,160},{128,192},{160,96},{192,128},{224,... | collective-permute-start | bytes 1572872 | tf_op jit(solution)/shard_map/ppermute | solution.py:71
  125.6 0.6 dynamic_slice.34
  128.7 0.7 dynamic_slice.35
  130.2 2.8 %collective-permute-done.13 = f32[512,256]{1,0:T(8,128)S(1)} collective-permute-done((f32[512,256]{1,0:T(8,128)S(1)}, f32[512,256]{1,0:T(8,128)S(1)}, u32[]{:S(2)}, u32[]{:S(2)}) %collective-permute-start.13) | collective-permute-done | bytes 524320 | tf_op jit(solution)/shard_map/ppermute | solution.py:71
  133.1 1.9 collective-permute-start.14
  135.1 0.7 compare_convert_fusion
  135.9 1.8 collective-permute-done.14
  137.7 2.3 fusion.11
  140.0 1.9 copy.24
  141.8 5.6 %fusion.21 = f32[2,256,256]{1,2,0:T(8,128)S(1)} fusion(f32[2048,256]{1,0:T(8,128)S(1)} %fusion.11, f32[2048,2]{0,1:T(2,128)S(1)} %fusion.61, f32[2048,256]{0,1:T(8,128)} %copy.24), kind=kOutput, calls=%fused_computation.25 | convolution fusion | flops 3222274048 | bytes 4734976 | tf_op jit(solution)/shard_map/mc,ck,cl->mkl/dot_general | solution.py:199
  148.0 3.8 %collective-permute-start.17 = (f32[192,256]{0,1:T(8,128)S(1)}, f32[192,256]{0,1:T(8,128)S(1)}, u32[]{:S(2)}, u32[]{:S(2)}) collective-permute-start(f32[192,256]{0,1:T(8,128)S(1)} %pad_maximum_fusion), channel_id=1, source_target_pairs={{1,0},{2,1},{3,2},{4,3},{5,4},{6,5},{7,6},{8,7},{9,8},{10,9},{11,1... | collective-permute-start | bytes 589832 | tf_op jit(solution)/shard_map/ppermute | solution.py:114
  151.8 4.0 %collective-permute-start.18 = (f32[192,256]{0,1:T(8,128)S(1)}, f32[192,256]{0,1:T(8,128)S(1)}, u32[]{:S(2)}, u32[]{:S(2)}) collective-permute-start(f32[192,256]{0,1:T(8,128)S(1)} %pad_maximum_fusion), channel_id=1, source_target_pairs={{2,0},{3,1},{4,2},{5,3},{6,4},{7,5},{8,6},{9,7},{10,8},{11,9},{12,... | collective-permute-start | bytes 589832 | tf_op jit(solution)/shard_map/ppermute | solution.py:114
  155.8 3.5 %collective-permute-start.15 = (f32[192,256]{0,1:T(8,128)S(1)}, f32[192,256]{0,1:T(8,128)S(1)}, u32[]{:S(2)}, u32[]{:S(2)}) collective-permute-start(f32[192,256]{0,1:T(8,128)S(1)} %pad_maximum_fusion.1), channel_id=1, source_target_pairs={{0,1},{1,2},{2,3},{3,4},{4,5},{5,6},{6,7},{7,8},{8,9},{9,10},{10,1... | collective-permute-start | bytes 589832 | tf_op jit(solution)/shard_map/ppermute | solution.py:114
  159.3 3.9 %collective-permute-start.16 = (f32[192,256]{0,1:T(8,128)S(1)}, f32[192,256]{0,1:T(8,128)S(1)}, u32[]{:S(2)}, u32[]{:S(2)}) collective-permute-start(f32[192,256]{0,1:T(8,128)S(1)} %pad_maximum_fusion.1), channel_id=1, source_target_pairs={{0,2},{1,3},{2,4},{3,5},{4,6},{5,7},{6,8},{7,9},{8,10},{9,11},{10,... | collective-permute-start | bytes 589832 | tf_op jit(solution)/shard_map/ppermute | solution.py:114
  163.1 3.8 %fusion.2 = f32[256,256]{1,0:T(8,128)S(1)} fusion(f32[2048,256]{1,0:T(8,128)S(1)} %fusion.11, f32[2048]{0:T(1024)S(1)} %compare_convert_fusion), kind=kOutput, calls=%fused_computation.2 | convolution fusion | flops 1611137024 | bytes 2367488 | tf_op jit(solution)/shard_map/c,ck,cl->kl/dot_general | solution.py:220
  167.1 4.5 %collective-permute-done.15 = f32[192,256]{0,1:T(8,128)S(1)} collective-permute-done((f32[192,256]{0,1:T(8,128)S(1)}, f32[192,256]{0,1:T(8,128)S(1)}, u32[]{:S(2)}, u32[]{:S(2)}) %collective-permute-start.15) | collective-permute-done | bytes 196640 | tf_op jit(solution)/shard_map/ppermute | solution.py:114
  171.6 7.1 %collective-permute-done.16 = f32[192,256]{0,1:T(8,128)S(1)} collective-permute-done((f32[192,256]{0,1:T(8,128)S(1)}, f32[192,256]{0,1:T(8,128)S(1)}, u32[]{:S(2)}, u32[]{:S(2)}) %collective-permute-start.16) | collective-permute-done | bytes 196640 | tf_op jit(solution)/shard_map/ppermute | solution.py:114
  179.2 11.7 %custom-call.8 = f32[128,128]{1,0:T(8,128)S(1)} custom-call(f32[128,128]{1,0:T(8,128)S(1)} %slice.191), custom_call_target="Cholesky" | custom-call | tf_op jit(solution)/shard_map/cholesky/custom-call.1 | solution.py:87
  191.0 0.6 compare_reduce_fusion.1
  191.6 0.7 fusion.48
  192.3 9.8 %custom-call.9 = f32[1,128,128]{1,2,0:T(8,128)S(1)} custom-call(f32[1,128,128]{2,1,0:T(8,128)S(1)} %fusion.48), custom_call_target="InvertDiagBlocksLowerTriangular" | custom-call | tf_op jit(solution)/shard_map/jit(_solve_triangular)/triangular_solve | solution.py:82
  202.1 0.3 fusion.46
  203.4 11.9 %custom-call.10 = f32[128,128]{1,0:T(8,128)S(1)} custom-call(f32[128,128]{1,0:T(8,128)S(1)} %convolution_subtract_fusion), custom_call_target="Cholesky" | custom-call | tf_op jit(solution)/shard_map/cholesky/custom-call.1 | solution.py:90
  215.4 0.6 compare_reduce_fusion
  216.0 0.7 fusion.49
  216.7 9.8 %custom-call.11 = f32[1,128,128]{1,2,0:T(8,128)S(1)} custom-call(f32[1,128,128]{2,1,0:T(8,128)S(1)} %fusion.49), custom_call_target="InvertDiagBlocksLowerTriangular" | custom-call | tf_op jit(solution)/shard_map/jit(_solve_triangular)/triangular_solve | solution.py:82
  226.5 0.3 fusion.44
  227.0 0.3 fusion.51
  227.3 0.3 convolution_add_fusion
  227.6 0.8 copy.34
  (81 shorter events, 4.1 us)
Async XLA Ops:
  1.2 5.2 %collective-permute-start = (f32[2,2048]{1,0:T(2,128)S(1)}, f32[2,2048]{1,0:T(2,128)S(1)}, u32[]{:S(2)}, u32[]{:S(2)}) collective-permute-start(f32[2,2048]{1,0:T(2,128)S(1)} %pad_maximum_fusion.3), channel_id=1, source_target_pairs={{0,32},{32,0},{64,96},{96,64},{128,160},{160,128},{192,224},{224,1... | collective-permute-start | bytes 49160 | tf_op jit(solution)/shard_map/ppermute | solution.py:30
  6.4 6.0 %collective-permute-start.1 = (f32[2,2048]{1,0:T(2,128)S(1)}, f32[2,2048]{1,0:T(2,128)S(1)}, u32[]{:S(2)}, u32[]{:S(2)}) collective-permute-start(f32[2,2048]{1,0:T(2,128)S(1)} %fusion.72), channel_id=1, source_target_pairs={{0,64},{32,96},{64,0},{96,32},{128,192},{160,224},{192,128},{224,1... | collective-permute-start | bytes 49160 | tf_op jit(solution)/shard_map/ppermute | solution.py:30
  12.5 7.8 %collective-permute-start.2 = (f32[2,2048]{1,0:T(2,128)S(1)}, f32[2,2048]{1,0:T(2,128)S(1)}, u32[]{:S(2)}, u32[]{:S(2)}) collective-permute-start(f32[2,2048]{1,0:T(2,128)S(1)} %fusion.86), channel_id=1, source_target_pairs={{0,128},{32,160},{64,192},{96,224},{128,0},{160,32},{192,64},{224,... | collective-permute-start | bytes 49160 | tf_op jit(solution)/shard_map/ppermute | solution.py:30
  20.3 16.8 %collective-permute-start.3 = (f32[2,2048]{1,0:T(2,128)S(1)}, f32[2,2048]{1,0:T(2,128)S(1)}, u32[]{:S(2)}, u32[]{:S(2)}) collective-permute-start(f32[2,2048]{1,0:T(2,128)S(1)} %add.188), channel_id=1, source_target_pairs={{0,256},{32,288},{64,320},{96,352},{128,384},{160,416},{192,448},{... | collective-permute-start | bytes 49160 | tf_op jit(solution)/shard_map/ppermute | solution.py:30
  38.3 10.6 %copy-start = (s32[3]{0:T(128)S(1)}, s32[3]{0:T(128)}, u32[]{:S(2)}) copy-start(s32[3]{0:T(128)} %constant.174.clone.1) | copy-start | bytes 40
  39.7 15.5 %collective-permute-start.4 = (f32[64,256]{1,0:T(8,128)S(1)}, f32[64,256]{1,0:T(8,128)S(1)}, u32[]{:S(2)}, u32[]{:S(2)}) collective-permute-start(f32[64,256]{1,0:T(8,128)S(1)} %get-tuple-element.35), channel_id=1, source_target_pairs={{0,1},{1,2},{2,3},{3,4},{4,5},{5,6},{6,7},{7,8},{8,9},{9,10},{10,1... | collective-permute-start | bytes 196616 | tf_op jit(solution)/shard_map/ppermute | solution.py:114
  43.2 12.0 %collective-permute-start.5 = (f32[64,256]{1,0:T(8,128)S(1)}, f32[64,256]{1,0:T(8,128)S(1)}, u32[]{:S(2)}, u32[]{:S(2)}) collective-permute-start(f32[64,256]{1,0:T(8,128)S(1)} %get-tuple-element.35), channel_id=1, source_target_pairs={{0,2},{1,3},{2,4},{3,5},{4,6},{5,7},{6,8},{7,9},{8,10},{9,11},{10,... | collective-permute-start | bytes 196616 | tf_op jit(solution)/shard_map/ppermute | solution.py:114
  49.7 6.8 %collective-permute-start.6 = (f32[64,256]{1,0:T(8,128)S(1)}, f32[64,256]{1,0:T(8,128)S(1)}, u32[]{:S(2)}, u32[]{:S(2)}) collective-permute-start(f32[64,256]{1,0:T(8,128)S(1)} %get-tuple-element.36), channel_id=1, source_target_pairs={{1,0},{2,1},{3,2},{4,3},{5,4},{6,5},{7,6},{8,7},{9,8},{10,9},{11,1... | collective-permute-start | bytes 196616 | tf_op jit(solution)/shard_map/ppermute | solution.py:114
  51.6 7.3 %collective-permute-start.7 = (f32[64,256]{1,0:T(8,128)S(1)}, f32[64,256]{1,0:T(8,128)S(1)}, u32[]{:S(2)}, u32[]{:S(2)}) collective-permute-start(f32[64,256]{1,0:T(8,128)S(1)} %get-tuple-element.36), channel_id=1, source_target_pairs={{2,0},{3,1},{4,2},{5,3},{6,4},{7,5},{8,6},{9,7},{10,8},{11,9},{12,... | collective-permute-start | bytes 196616 | tf_op jit(solution)/shard_map/ppermute | solution.py:114
  60.6 4.7 %collective-permute-start.8 = (f32[1024,256]{1,0:T(8,128)S(1)}, f32[1024,256]{1,0:T(8,128)}, u32[]{:S(2)}, u32[]{:S(2)}) collective-permute-start(f32[1024,256]{1,0:T(8,128)S(1)} %slice_select_fusion), channel_id=1, source_target_pairs={{0,32},{32,0},{64,96},{96,64},{128,160},{160,128},{192,224},{224,1... | collective-permute-start | bytes 3145736 | tf_op jit(solution)/shard_map/ppermute | solution.py:67
  66.8 11.1 %collective-permute-start.9 = (f32[512,256]{1,0:T(8,128)S(1)}, f32[512,256]{1,0:T(8,128)S(1)}, u32[]{:S(2)}, u32[]{:S(2)}) collective-permute-start(f32[512,256]{1,0:T(8,128)S(1)} %slice_select_fusion.1), channel_id=1, source_target_pairs={{0,64},{32,480},{64,0},{96,160},{128,192},{160,96},{192,128},{224,... | collective-permute-start | bytes 1572872 | tf_op jit(solution)/shard_map/ppermute | solution.py:67
  77.9 50.8 %copy-start.1 = (s32[64]{0:T(128)S(1)}, s32[64]{0:T(128)}, u32[]{:S(2)}) copy-start(s32[64]{0:T(128)} %param.11) | copy-start | bytes 772
  78.0 14.1 %collective-permute-start.10 = (f32[256,256]{1,0:T(8,128)S(1)}, f32[256,256]{1,0:T(8,128)S(1)}, u32[]{:S(2)}, u32[]{:S(2)}) collective-permute-start(f32[256,256]{1,0:T(8,128)S(1)} %slice_select_fusion.2), channel_id=1, source_target_pairs={{0,128},{32,160},{64,192},{96,480},{128,0},{160,32},{192,64},{224,... | collective-permute-start | bytes 786440 | tf_op jit(solution)/shard_map/ppermute | solution.py:67
  92.1 15.1 %collective-permute-start.11 = (f32[256,256]{1,0:T(8,128)S(1)}, f32[256,256]{1,0:T(8,128)S(1)}, u32[]{:S(2)}, u32[]{:S(2)}) collective-permute-start(f32[256,256]{1,0:T(8,128)S(1)} %select_add_fusion.4), channel_id=1, source_target_pairs={{0,256},{32,288},{64,320},{96,352},{128,384},{160,416},{192,448},{... | collective-permute-start | bytes 786440 | tf_op jit(solution)/shard_map/ppermute | solution.py:69
  107.3 14.6 %collective-permute-start.12 = (f32[256,256]{1,0:T(8,128)S(1)}, f32[256,256]{1,0:T(8,128)S(1)}, u32[]{:S(2)}, u32[]{:S(2)}) collective-permute-start(f32[256,256]{1,0:T(8,128)S(1)} %add.207), channel_id=1, source_target_pairs={{0,128},{32,160},{64,192},{96,480},{128,0},{160,32},{192,64},{224,... | collective-permute-start | bytes 786440 | tf_op jit(solution)/shard_map/ppermute | solution.py:71
  121.9 11.1 %collective-permute-start.13 = (f32[512,256]{1,0:T(8,128)S(1)}, f32[512,256]{1,0:T(8,128)S(1)}, u32[]{:S(2)}, u32[]{:S(2)}) collective-permute-start(f32[512,256]{1,0:T(8,128)S(1)} %maximum_select_fusion.2), channel_id=1, source_target_pairs={{0,64},{32,480},{64,0},{96,160},{128,192},{160,96},{192,128},{224,... | collective-permute-start | bytes 1572872 | tf_op jit(solution)/shard_map/ppermute | solution.py:71
  133.1 4.6 %collective-permute-start.14 = (f32[1024,256]{1,0:T(8,128)S(1)}, f32[1024,256]{1,0:T(8,128)S(1)}, u32[]{:S(2)}, u32[]{:S(2)}) collective-permute-start(f32[1024,256]{1,0:T(8,128)S(1)} %maximum_select_fusion.1), channel_id=1, source_target_pairs={{0,32},{32,0},{64,96},{96,64},{128,160},{160,128},{192,224},{224,1... | collective-permute-start | bytes 3145736 | tf_op jit(solution)/shard_map/ppermute | solution.py:71
  148.0 19.0 %collective-permute-start.17 = (f32[192,256]{0,1:T(8,128)S(1)}, f32[192,256]{0,1:T(8,128)S(1)}, u32[]{:S(2)}, u32[]{:S(2)}) collective-permute-start(f32[192,256]{0,1:T(8,128)S(1)} %pad_maximum_fusion), channel_id=1, source_target_pairs={{1,0},{2,1},{3,2},{4,3},{5,4},{6,5},{7,6},{8,7},{9,8},{10,9},{11,1... | collective-permute-start | bytes 589832 | tf_op jit(solution)/shard_map/ppermute | solution.py:114
  151.8 15.2 %collective-permute-start.18 = (f32[192,256]{0,1:T(8,128)S(1)}, f32[192,256]{0,1:T(8,128)S(1)}, u32[]{:S(2)}, u32[]{:S(2)}) collective-permute-start(f32[192,256]{0,1:T(8,128)S(1)} %pad_maximum_fusion), channel_id=1, source_target_pairs={{2,0},{3,1},{4,2},{5,3},{6,4},{7,5},{8,6},{9,7},{10,8},{11,9},{12,... | collective-permute-start | bytes 589832 | tf_op jit(solution)/shard_map/ppermute | solution.py:114
  155.8 15.8 %collective-permute-start.15 = (f32[192,256]{0,1:T(8,128)S(1)}, f32[192,256]{0,1:T(8,128)S(1)}, u32[]{:S(2)}, u32[]{:S(2)}) collective-permute-start(f32[192,256]{0,1:T(8,128)S(1)} %pad_maximum_fusion.1), channel_id=1, source_target_pairs={{0,1},{1,2},{2,3},{3,4},{4,5},{5,6},{6,7},{7,8},{8,9},{9,10},{10,1... | collective-permute-start | bytes 589832 | tf_op jit(solution)/shard_map/ppermute | solution.py:114
  159.3 19.4 %collective-permute-start.16 = (f32[192,256]{0,1:T(8,128)S(1)}, f32[192,256]{0,1:T(8,128)S(1)}, u32[]{:S(2)}, u32[]{:S(2)}) collective-permute-start(f32[192,256]{0,1:T(8,128)S(1)} %pad_maximum_fusion.1), channel_id=1, source_target_pairs={{0,2},{1,3},{2,4},{3,5},{4,6},{5,7},{6,8},{7,9},{8,10},{9,11},{10,... | collective-permute-start | bytes 589832 | tf_op jit(solution)/shard_map/ppermute | solution.py:114

commit v9 on v8

--- a/solution.py
+++ b/solution.py
@@ -84,10 +84,10 @@
 
 def basis_rows(gram, rows):
     half = gram.shape[0] // 2
-    l11 = lax.linalg.cholesky(gram[:half, :half], symmetrize_input=False)
+    l11 = jnp.linalg.cholesky(gram[:half, :half])
     m11 = lower_inverse(l11)
     l21 = dot_hi(gram[half:, :half], m11.T)
-    l22 = lax.linalg.cholesky(gram[half:, half:] - dot_hi(l21, l21.T), symmetrize_input=False)
+    l22 = jnp.linalg.cholesky(gram[half:, half:] - dot_hi(l21, l21.T))
     m22 = lower_inverse(l22)
     m21 = -dot_hi(m22, dot_hi(l21, m11))
     left = dot_hi(rows[:, :half], m11.T)
@@ -173,13 +173,15 @@
 
     columns = col_base + jnp.arange(col_span, dtype=jnp.int32)
     signs = sketch_signs(columns, sketch_seed[0], K)
+    signs_b = signs.astype(jnp.bfloat16)
+    signs, signs_b = lax.optimization_barrier((signs, signs_b))
     slot_ids = jnp.arange(slot_total, dtype=jnp.int32)
     col_slot = jnp.repeat(unit_slot, UNIT)
     col_mask = col_slot[None, :] == slot_ids[:, None]
     masked_std = jnp.where(col_mask[:, None, :], standard[None], jnp.zeros((), jnp.bfloat16))
 
     parts = jnp.einsum(
-        "snc,ck->snk", masked_std, signs.astype(jnp.bfloat16), preferred_element_type=jnp.float32
+        "snc,ck->snk", masked_std, signs_b, preferred_element_type=jnp.float32
     )
     head_in, tail_in = halo(
         parts[0], parts[last_slot], blk_index, blk_count, reach, edge_blocks, first_block, last_block

time: 229 us -> 226 us (0.987)
  the two profiles are of different devices: /device:TPU:14 before, /device:TPU:6 now
where the time goes in v9:
time: 226 us; the launch traced here: 223 us
  starting transfers between devices  67.5 us (30%)
  waiting for transfers between devices  66.9 us (30%)
  other arithmetic  59.1 us (26%)
  matrix products  12.5 us (6%)
  between operations  10.6 us (5%)
  local copies, waits for them, and re-layouts  6.23 us (3%)
    ppermute x8, starting transfers between devices, shift(): return lax.ppermute(x, axis, pairs)  27.6 us
    ppermute x4, starting transfers between devices, xor_allreduce(): x = x + lax.ppermute(x, axis, [(j, j ^ mask) for j in range(count)])  21.6 us
    another operation x4, other arithmetic, lower_inverse(): return jax.scipy.linalg.solve_triangular(lower, eye, lower=True)  20.9 us
    ppermute x3, waiting for transfers between devices, halving_allreduce(): x = keep + lax.ppermute(send, axis, pairs)  20.1 us
    ppermute x3, waiting for transfers between devices, halving_allreduce(): got = lax.ppermute(x, axis, pairs)  17.3 us
    ppermute x1, waiting for transfers between devices, halving_allreduce(): x = x + lax.ppermute(x, axis, pairs)  16.4 us
    another operation x3, other arithmetic, basis_rows(): l22 = jnp.linalg.cholesky(gram[half:, half:] - dot_hi(l21, l21.T))  12.6 us
    another operation x3, other arithmetic, basis_rows(): l11 = jnp.linalg.cholesky(gram[:half, :half])  12.4 us
  transfers between devices with their start and end apart: 19, of which 13 were waited for; matrix products, arithmetic and copies ran while one was open for 6% of the time, Pallas kernels for 0%

profile of v9, /device:TPU:6, one launch (start us, length us, event | category | flops | bytes accessed | tf_op | source)
XLA Modules:
  0.0 222.8 jit_solution(12637021387050234659)
XLA Ops:
  0.0 1.2 convert_reduce_fusion
  1.2 1.9 collective-permute-start
  3.2 0.7 multiply_bitcast_fusion
  4.2 0.7 multiply_subtract_fusion
  5.0 0.6 fusion.62
  5.6 0.5 broadcast_compare_fusion.1
  6.9 2.1 fusion.27
  9.1 4.3 %collective-permute-start.1 = (f32[2,2048]{1,0:T(2,128)S(1)}, f32[2,2048]{1,0:T(2,128)S(1)}, u32[]{:S(2)}, u32[]{:S(2)}) collective-permute-start(f32[2,2048]{1,0:T(2,128)S(1)} %fusion.61), channel_id=1, source_target_pairs={{0,64},{32,96},{64,0},{96,32},{128,192},{160,224},{192,128},{224,1... | collective-permute-start | bytes 49160 | tf_op jit(solution)/shard_map/ppermute | solution.py:30
  13.5 1.5 collective-permute-done.1
  15.1 6.1 %collective-permute-start.2 = (f32[2,2048]{1,0:T(2,128)S(1)}, f32[2,2048]{1,0:T(2,128)S(1)}, u32[]{:S(2)}, u32[]{:S(2)}) collective-permute-start(f32[2,2048]{1,0:T(2,128)S(1)} %fusion.75), channel_id=1, source_target_pairs={{0,128},{32,160},{64,192},{96,224},{128,0},{160,32},{192,64},{224,... | collective-permute-start | bytes 49160 | tf_op jit(solution)/shard_map/ppermute | solution.py:30
  21.2 1.7 collective-permute-done.2
  22.9 9.3 %collective-permute-start.3 = (f32[2,2048]{1,0:T(2,128)S(1)}, f32[2,2048]{1,0:T(2,128)S(1)}, u32[]{:S(2)}, u32[]{:S(2)}) collective-permute-start(f32[2,2048]{1,0:T(2,128)S(1)} %add.192), channel_id=1, source_target_pairs={{0,256},{32,288},{64,320},{96,352},{128,384},{160,416},{192,448},{... | collective-permute-start | bytes 49160 | tf_op jit(solution)/shard_map/ppermute | solution.py:30
  33.4 0.6 constant_dynamic-slice_fusion.1
  39.0 0.5 fusion.16
  39.6 3.5 %collective-permute-start.4 = (f32[64,256]{1,0:T(8,128)S(1)}, f32[64,256]{1,0:T(8,128)S(1)}, u32[]{:S(2)}, u32[]{:S(2)}) collective-permute-start(f32[64,256]{1,0:T(8,128)S(1)} %get-tuple-element.38), channel_id=1, source_target_pairs={{0,1},{1,2},{2,3},{3,4},{4,5},{5,6},{6,7},{7,8},{8,9},{9,10},{10,1... | collective-permute-start | bytes 196616 | tf_op jit(solution)/shard_map/ppermute | solution.py:114
  43.1 4.5 %collective-permute-start.5 = (f32[64,256]{1,0:T(8,128)S(1)}, f32[64,256]{1,0:T(8,128)S(1)}, u32[]{:S(2)}, u32[]{:S(2)}) collective-permute-start(f32[64,256]{1,0:T(8,128)S(1)} %get-tuple-element.38), channel_id=1, source_target_pairs={{0,2},{1,3},{2,4},{3,5},{4,6},{5,7},{6,8},{7,9},{8,10},{9,11},{10,... | collective-permute-start | bytes 196616 | tf_op jit(solution)/shard_map/ppermute | solution.py:114
  47.6 0.7 and_reduce_fusion
  48.3 4.5 %collective-permute-start.6 = (f32[64,256]{1,0:T(8,128)S(1)}, f32[64,256]{1,0:T(8,128)S(1)}, u32[]{:S(2)}, u32[]{:S(2)}) collective-permute-start(f32[64,256]{1,0:T(8,128)S(1)} %get-tuple-element.39), channel_id=1, source_target_pairs={{1,0},{2,1},{3,2},{4,3},{5,4},{6,5},{7,6},{8,7},{9,8},{10,9},{11,1... | collective-permute-start | bytes 196616 | tf_op jit(solution)/shard_map/ppermute | solution.py:114
  52.8 2.2 %collective-permute-start.7 = (f32[64,256]{1,0:T(8,128)S(1)}, f32[64,256]{1,0:T(8,128)S(1)}, u32[]{:S(2)}, u32[]{:S(2)}) collective-permute-start(f32[64,256]{1,0:T(8,128)S(1)} %get-tuple-element.39), channel_id=1, source_target_pairs={{2,0},{3,1},{4,2},{5,3},{6,4},{7,5},{8,6},{9,7},{10,8},{11,9},{12,... | collective-permute-start | bytes 196616 | tf_op jit(solution)/shard_map/ppermute | solution.py:114
  55.1 0.6 collective-permute-done.6
  55.7 4.6 %collective-permute-done.7 = f32[64,256]{1,0:T(8,128)S(1)} collective-permute-done((f32[64,256]{1,0:T(8,128)S(1)}, f32[64,256]{1,0:T(8,128)S(1)}, u32[]{:S(2)}, u32[]{:S(2)}) %collective-permute-start.7) | collective-permute-done | bytes 65568 | tf_op jit(solution)/shard_map/ppermute | solution.py:114
  60.2 0.6 fusion.42
  60.9 0.8 convolution_bitcast_fusion
  61.8 1.9 collective-permute-start.8
  63.7 2.7 %collective-permute-done.8 = f32[1024,256]{1,0:T(8,128)} collective-permute-done((f32[1024,256]{1,0:T(8,128)S(1)}, f32[1024,256]{1,0:T(8,128)}, u32[]{:S(2)}, u32[]{:S(2)}) %collective-permute-start.8) | collective-permute-done | bytes 1048608 | tf_op jit(solution)/shard_map/ppermute | solution.py:67
  66.4 1.4 select_add_fusion
  68.0 3.4 %collective-permute-start.9 = (f32[512,256]{1,0:T(8,128)S(1)}, f32[512,256]{1,0:T(8,128)S(1)}, u32[]{:S(2)}, u32[]{:S(2)}) collective-permute-start(f32[512,256]{1,0:T(8,128)S(1)} %slice_select_fusion.1), channel_id=1, source_target_pairs={{0,64},{32,480},{64,0},{96,160},{128,192},{160,96},{192,128},{224,... | collective-permute-start | bytes 1572872 | tf_op jit(solution)/shard_map/ppermute | solution.py:67
  71.4 7.7 %collective-permute-done.9 = f32[512,256]{1,0:T(8,128)S(1)} collective-permute-done((f32[512,256]{1,0:T(8,128)S(1)}, f32[512,256]{1,0:T(8,128)S(1)}, u32[]{:S(2)}, u32[]{:S(2)}) %collective-permute-start.9) | collective-permute-done | bytes 524320 | tf_op jit(solution)/shard_map/ppermute | solution.py:67
  79.2 4.3 %collective-permute-start.10 = (f32[256,256]{1,0:T(8,128)S(1)}, f32[256,256]{1,0:T(8,128)S(1)}, u32[]{:S(2)}, u32[]{:S(2)}) collective-permute-start(f32[256,256]{1,0:T(8,128)S(1)} %slice_select_fusion.2), channel_id=1, source_target_pairs={{0,128},{32,160},{64,192},{96,480},{128,0},{160,32},{192,64},{224,... | collective-permute-start | bytes 786440 | tf_op jit(solution)/shard_map/ppermute | solution.py:67
  83.5 9.7 %collective-permute-done.10 = f32[256,256]{1,0:T(8,128)S(1)} collective-permute-done((f32[256,256]{1,0:T(8,128)S(1)}, f32[256,256]{1,0:T(8,128)S(1)}, u32[]{:S(2)}, u32[]{:S(2)}) %collective-permute-start.10) | collective-permute-done | bytes 262176 | tf_op jit(solution)/shard_map/ppermute | solution.py:67
  93.3 2.7 %collective-permute-start.11 = (f32[256,256]{1,0:T(8,128)S(1)}, f32[256,256]{1,0:T(8,128)S(1)}, u32[]{:S(2)}, u32[]{:S(2)}) collective-permute-start(f32[256,256]{1,0:T(8,128)S(1)} %select_add_fusion.2), channel_id=1, source_target_pairs={{0,256},{32,288},{64,320},{96,352},{128,384},{160,416},{192,448},{... | collective-permute-start | bytes 786440 | tf_op jit(solution)/shard_map/ppermute | solution.py:69
  96.0 16.4 %collective-permute-done.11 = f32[256,256]{1,0:T(8,128)S(1)} collective-permute-done((f32[256,256]{1,0:T(8,128)S(1)}, f32[256,256]{1,0:T(8,128)S(1)}, u32[]{:S(2)}, u32[]{:S(2)}) %collective-permute-start.11) | collective-permute-done | bytes 262176 | tf_op jit(solution)/shard_map/ppermute | solution.py:69
  112.4 2.1 collective-permute-start.12
  114.5 10.9 %collective-permute-done.12 = f32[256,256]{1,0:T(8,128)S(1)} collective-permute-done((f32[256,256]{1,0:T(8,128)S(1)}, f32[256,256]{1,0:T(8,128)S(1)}, u32[]{:S(2)}, u32[]{:S(2)}) %collective-permute-start.12) | collective-permute-done | bytes 262176 | tf_op jit(solution)/shard_map/ppermute | solution.py:71
  125.4 1.9 collective-permute-start.13
  127.4 0.6 dynamic_slice.34
  130.5 0.6 dynamic_slice.35
  131.8 4.7 %collective-permute-done.13 = f32[512,256]{1,0:T(8,128)S(1)} collective-permute-done((f32[512,256]{1,0:T(8,128)S(1)}, f32[512,256]{1,0:T(8,128)S(1)}, u32[]{:S(2)}, u32[]{:S(2)}) %collective-permute-start.13) | collective-permute-done | bytes 524320 | tf_op jit(solution)/shard_map/ppermute | solution.py:71
  136.6 2.0 collective-permute-start.14
  138.7 0.7 compare_convert_fusion
  139.4 1.7 collective-permute-done.14
  141.2 2.0 fusion.11
  143.2 1.9 copy.26
  145.0 5.1 %fusion.20 = f32[2,256,256]{2,1,0:T(8,128)S(1)} fusion(f32[2048,256]{1,0:T(8,128)S(1)} %fusion.11, f32[2048,2]{0,1:T(2,128)S(1)} %fusion.55, f32[2048,256]{0,1:T(8,128)} %copy.26), kind=kOutput, calls=%fused_computation.24 | convolution fusion | flops 3222274048 | bytes 4734976 | tf_op jit(solution)/shard_map/mc,ck,cl->mkl/dot_general | solution.py:201
  150.3 4.1 %collective-permute-start.17 = (f32[192,256]{1,0:T(8,128)S(1)}, f32[192,256]{1,0:T(8,128)}, u32[]{:S(2)}, u32[]{:S(2)}) collective-permute-start(f32[192,256]{1,0:T(8,128)S(1)} %pad_maximum_fusion), channel_id=1, source_target_pairs={{1,0},{2,1},{3,2},{4,3},{5,4},{6,5},{7,6},{8,7},{9,8},{10,9},{11,1... | collective-permute-start | bytes 589832 | tf_op jit(solution)/shard_map/ppermute | solution.py:114
  154.4 2.0 collective-permute-start.18
  156.4 3.7 %collective-permute-start.15 = (f32[192,256]{1,0:T(8,128)S(1)}, f32[192,256]{1,0:T(8,128)S(1)}, u32[]{:S(2)}, u32[]{:S(2)}) collective-permute-start(f32[192,256]{1,0:T(8,128)S(1)} %pad_maximum_fusion.1), channel_id=1, source_target_pairs={{0,1},{1,2},{2,3},{3,4},{4,5},{5,6},{6,7},{7,8},{8,9},{9,10},{10,1... | collective-permute-start | bytes 589832 | tf_op jit(solution)/shard_map/ppermute | solution.py:114
  160.1 3.1 %collective-permute-start.16 = (f32[192,256]{1,0:T(8,128)S(1)}, f32[192,256]{1,0:T(8,128)S(1)}, u32[]{:S(2)}, u32[]{:S(2)}) collective-permute-start(f32[192,256]{1,0:T(8,128)S(1)} %pad_maximum_fusion.1), channel_id=1, source_target_pairs={{0,2},{1,3},{2,4},{3,5},{4,6},{5,7},{6,8},{7,9},{8,10},{9,11},{10,... | collective-permute-start | bytes 589832 | tf_op jit(solution)/shard_map/ppermute | solution.py:114
  163.3 3.8 %fusion.2 = f32[256,256]{1,0:T(8,128)S(1)} fusion(f32[2048,256]{1,0:T(8,128)S(1)} %fusion.11, f32[2048]{0:T(1024)S(1)} %compare_convert_fusion), kind=kOutput, calls=%fused_computation.2 | convolution fusion | flops 1611137024 | bytes 2367488 | tf_op jit(solution)/shard_map/c,ck,cl->kl/dot_general | solution.py:222
  167.2 1.4 collective-permute-done.18
  168.7 1.0 select_add_fusion.3
  169.7 3.3 %collective-permute-done.16 = f32[192,256]{1,0:T(8,128)S(1)} collective-permute-done((f32[192,256]{1,0:T(8,128)S(1)}, f32[192,256]{1,0:T(8,128)S(1)}, u32[]{:S(2)}, u32[]{:S(2)}) %collective-permute-start.16) | collective-permute-done | bytes 196640 | tf_op jit(solution)/shard_map/ppermute | solution.py:114
  173.6 11.7 %cholesky.44 = f32[128,128]{1,0:T(8,128)S(1)} custom-call(f32[128,128]{1,0:T(8,128)S(1)} %fusion.50), custom_call_target="Cholesky" | custom-call | tf_op jit(solution)/shard_map/jit(cholesky)/cholesky | solution.py:87
  185.4 0.6 compare_reduce_fusion.1
  186.0 0.7 fusion.40
  186.7 9.8 %custom-call.6 = f32[1,128,128]{1,2,0:T(8,128)S(1)} custom-call(f32[1,128,128]{2,1,0:T(8,128)S(1)} %fusion.40), custom_call_target="InvertDiagBlocksLowerTriangular" | custom-call | tf_op jit(solution)/shard_map/jit(_solve_triangular)/triangular_solve | solution.py:82
  196.5 0.3 fusion.38
  196.8 0.3 fusion.45
  197.9 11.9 %cholesky.55 = f32[128,128]{1,0:T(8,128)S(1)} custom-call(f32[128,128]{1,0:T(8,128)S(1)} %fusion.48), custom_call_target="Cholesky" | custom-call | tf_op jit(solution)/shard_map/jit(cholesky)/cholesky | solution.py:90
  209.9 0.6 compare_reduce_fusion
  210.5 0.7 fusion.41
  211.2 9.8 %custom-call.7 = f32[1,128,128]{1,2,0:T(8,128)S(1)} custom-call(f32[1,128,128]{2,1,0:T(8,128)S(1)} %fusion.41), custom_call_target="InvertDiagBlocksLowerTriangular" | custom-call | tf_op jit(solution)/shard_map/jit(_solve_triangular)/triangular_solve | solution.py:82
  221.0 0.3 fusion.36
  222.1 0.8 copy.35
  (85 shorter events, 4.3 us)
Async XLA Ops:
  0.0 38.9 %copy-start = (s32[64,2048]{1,0:T(8,128)S(1)}, s32[64,2048]{1,0:T(8,128)}, u32[]{:S(2)}) copy-start(s32[64,2048]{1,0:T(8,128)} %param.10) | copy-start | bytes 1572868
  1.2 7.8 %collective-permute-start = (f32[2,2048]{1,0:T(2,128)S(1)}, f32[2,2048]{1,0:T(2,128)S(1)}, u32[]{:S(2)}, u32[]{:S(2)}) collective-permute-start(f32[2,2048]{1,0:T(2,128)S(1)} %pad_maximum_fusion.3), channel_id=1, source_target_pairs={{0,32},{32,0},{64,96},{96,64},{128,160},{160,128},{192,224},{224,1... | collective-permute-start | bytes 49160 | tf_op jit(solution)/shard_map/ppermute | solution.py:30
  9.1 6.0 %collective-permute-start.1 = (f32[2,2048]{1,0:T(2,128)S(1)}, f32[2,2048]{1,0:T(2,128)S(1)}, u32[]{:S(2)}, u32[]{:S(2)}) collective-permute-start(f32[2,2048]{1,0:T(2,128)S(1)} %fusion.61), channel_id=1, source_target_pairs={{0,64},{32,96},{64,0},{96,32},{128,192},{160,224},{192,128},{224,1... | collective-permute-start | bytes 49160 | tf_op jit(solution)/shard_map/ppermute | solution.py:30
  15.1 7.8 %collective-permute-start.2 = (f32[2,2048]{1,0:T(2,128)S(1)}, f32[2,2048]{1,0:T(2,128)S(1)}, u32[]{:S(2)}, u32[]{:S(2)}) collective-permute-start(f32[2,2048]{1,0:T(2,128)S(1)} %fusion.75), channel_id=1, source_target_pairs={{0,128},{32,160},{64,192},{96,224},{128,0},{160,32},{192,64},{224,... | collective-permute-start | bytes 49160 | tf_op jit(solution)/shard_map/ppermute | solution.py:30
  22.9 16.0 %collective-permute-start.3 = (f32[2,2048]{1,0:T(2,128)S(1)}, f32[2,2048]{1,0:T(2,128)S(1)}, u32[]{:S(2)}, u32[]{:S(2)}) collective-permute-start(f32[2,2048]{1,0:T(2,128)S(1)} %add.192), channel_id=1, source_target_pairs={{0,256},{32,288},{64,320},{96,352},{128,384},{160,416},{192,448},{... | collective-permute-start | bytes 49160 | tf_op jit(solution)/shard_map/ppermute | solution.py:30
  39.0 8.6 %copy-start.1 = (s32[3]{0:T(128)S(1)}, s32[3]{0:T(128)}, u32[]{:S(2)}) copy-start(s32[3]{0:T(128)} %constant.186.clone.1) | copy-start | bytes 40
  39.6 15.4 %collective-permute-start.4 = (f32[64,256]{1,0:T(8,128)S(1)}, f32[64,256]{1,0:T(8,128)S(1)}, u32[]{:S(2)}, u32[]{:S(2)}) collective-permute-start(f32[64,256]{1,0:T(8,128)S(1)} %get-tuple-element.38), channel_id=1, source_target_pairs={{0,1},{1,2},{2,3},{3,4},{4,5},{5,6},{6,7},{7,8},{8,9},{9,10},{10,1... | collective-permute-start | bytes 196616 | tf_op jit(solution)/shard_map/ppermute | solution.py:114
  43.1 12.0 %collective-permute-start.5 = (f32[64,256]{1,0:T(8,128)S(1)}, f32[64,256]{1,0:T(8,128)S(1)}, u32[]{:S(2)}, u32[]{:S(2)}) collective-permute-start(f32[64,256]{1,0:T(8,128)S(1)} %get-tuple-element.38), channel_id=1, source_target_pairs={{0,2},{1,3},{2,4},{3,5},{4,6},{5,7},{6,8},{7,9},{8,10},{9,11},{10,... | collective-permute-start | bytes 196616 | tf_op jit(solution)/shard_map/ppermute | solution.py:114
  48.3 7.4 %collective-permute-start.6 = (f32[64,256]{1,0:T(8,128)S(1)}, f32[64,256]{1,0:T(8,128)S(1)}, u32[]{:S(2)}, u32[]{:S(2)}) collective-permute-start(f32[64,256]{1,0:T(8,128)S(1)} %get-tuple-element.39), channel_id=1, source_target_pairs={{1,0},{2,1},{3,2},{4,3},{5,4},{6,5},{7,6},{8,7},{9,8},{10,9},{11,1... | collective-permute-start | bytes 196616 | tf_op jit(solution)/shard_map/ppermute | solution.py:114
  52.8 7.4 %collective-permute-start.7 = (f32[64,256]{1,0:T(8,128)S(1)}, f32[64,256]{1,0:T(8,128)S(1)}, u32[]{:S(2)}, u32[]{:S(2)}) collective-permute-start(f32[64,256]{1,0:T(8,128)S(1)} %get-tuple-element.39), channel_id=1, source_target_pairs={{2,0},{3,1},{4,2},{5,3},{6,4},{7,5},{8,6},{9,7},{10,8},{11,9},{12,... | collective-permute-start | bytes 196616 | tf_op jit(solution)/shard_map/ppermute | solution.py:114
  61.8 4.7 %collective-permute-start.8 = (f32[1024,256]{1,0:T(8,128)S(1)}, f32[1024,256]{1,0:T(8,128)}, u32[]{:S(2)}, u32[]{:S(2)}) collective-permute-start(f32[1024,256]{1,0:T(8,128)S(1)} %slice_select_fusion), channel_id=1, source_target_pairs={{0,32},{32,0},{64,96},{96,64},{128,160},{160,128},{192,224},{224,1... | collective-permute-start | bytes 3145736 | tf_op jit(solution)/shard_map/ppermute | solution.py:67
  68.0 11.1 %collective-permute-start.9 = (f32[512,256]{1,0:T(8,128)S(1)}, f32[512,256]{1,0:T(8,128)S(1)}, u32[]{:S(2)}, u32[]{:S(2)}) collective-permute-start(f32[512,256]{1,0:T(8,128)S(1)} %slice_select_fusion.1), channel_id=1, source_target_pairs={{0,64},{32,480},{64,0},{96,160},{128,192},{160,96},{192,128},{224,... | collective-permute-start | bytes 1572872 | tf_op jit(solution)/shard_map/ppermute | solution.py:67
  79.1 51.3 %copy-start.2 = (s32[64]{0:T(128)S(1)}, s32[64]{0:T(128)}, u32[]{:S(2)}) copy-start(s32[64]{0:T(128)} %param.11) | copy-start | bytes 772
  79.2 14.1 %collective-permute-start.10 = (f32[256,256]{1,0:T(8,128)S(1)}, f32[256,256]{1,0:T(8,128)S(1)}, u32[]{:S(2)}, u32[]{:S(2)}) collective-permute-start(f32[256,256]{1,0:T(8,128)S(1)} %slice_select_fusion.2), channel_id=1, source_target_pairs={{0,128},{32,160},{64,192},{96,480},{128,0},{160,32},{192,64},{224,... | collective-permute-start | bytes 786440 | tf_op jit(solution)/shard_map/ppermute | solution.py:67
  93.3 19.1 %collective-permute-start.11 = (f32[256,256]{1,0:T(8,128)S(1)}, f32[256,256]{1,0:T(8,128)S(1)}, u32[]{:S(2)}, u32[]{:S(2)}) collective-permute-start(f32[256,256]{1,0:T(8,128)S(1)} %select_add_fusion.2), channel_id=1, source_target_pairs={{0,256},{32,288},{64,320},{96,352},{128,384},{160,416},{192,448},{... | collective-permute-start | bytes 786440 | tf_op jit(solution)/shard_map/ppermute | solution.py:69
  112.4 13.0 %collective-permute-start.12 = (f32[256,256]{1,0:T(8,128)S(1)}, f32[256,256]{1,0:T(8,128)S(1)}, u32[]{:S(2)}, u32[]{:S(2)}) collective-permute-start(f32[256,256]{1,0:T(8,128)S(1)} %add.211), channel_id=1, source_target_pairs={{0,128},{32,160},{64,192},{96,480},{128,0},{160,32},{192,64},{224,... | collective-permute-start | bytes 786440 | tf_op jit(solution)/shard_map/ppermute | solution.py:71
  125.4 11.1 %collective-permute-start.13 = (f32[512,256]{1,0:T(8,128)S(1)}, f32[512,256]{1,0:T(8,128)S(1)}, u32[]{:S(2)}, u32[]{:S(2)}) collective-permute-start(f32[512,256]{1,0:T(8,128)S(1)} %maximum_select_fusion.2), channel_id=1, source_target_pairs={{0,64},{32,480},{64,0},{96,160},{128,192},{160,96},{192,128},{224,... | collective-permute-start | bytes 1572872 | tf_op jit(solution)/shard_map/ppermute | solution.py:71
  136.6 4.6 %collective-permute-start.14 = (f32[1024,256]{1,0:T(8,128)S(1)}, f32[1024,256]{1,0:T(8,128)S(1)}, u32[]{:S(2)}, u32[]{:S(2)}) collective-permute-start(f32[1024,256]{1,0:T(8,128)S(1)} %maximum_select_fusion.1), channel_id=1, source_target_pairs={{0,32},{32,0},{64,96},{96,64},{128,160},{160,128},{192,224},{224,1... | collective-permute-start | bytes 3145736 | tf_op jit(solution)/shard_map/ppermute | solution.py:71
  150.3 16.9 %collective-permute-start.17 = (f32[192,256]{1,0:T(8,128)S(1)}, f32[192,256]{1,0:T(8,128)}, u32[]{:S(2)}, u32[]{:S(2)}) collective-permute-start(f32[192,256]{1,0:T(8,128)S(1)} %pad_maximum_fusion), channel_id=1, source_target_pairs={{1,0},{2,1},{3,2},{4,3},{5,4},{6,5},{7,6},{8,7},{9,8},{10,9},{11,1... | collective-permute-start | bytes 589832 | tf_op jit(solution)/shard_map/ppermute | solution.py:114
  154.4 14.3 %collective-permute-start.18 = (f32[192,256]{1,0:T(8,128)S(1)}, f32[192,256]{1,0:T(8,128)}, u32[]{:S(2)}, u32[]{:S(2)}) collective-permute-start(f32[192,256]{1,0:T(8,128)S(1)} %pad_maximum_fusion), channel_id=1, source_target_pairs={{2,0},{3,1},{4,2},{5,3},{6,4},{7,5},{8,6},{9,7},{10,8},{11,9},{12,... | collective-permute-start | bytes 589832 | tf_op jit(solution)/shard_map/ppermute | solution.py:114
  156.4 13.3 %collective-permute-start.15 = (f32[192,256]{1,0:T(8,128)S(1)}, f32[192,256]{1,0:T(8,128)S(1)}, u32[]{:S(2)}, u32[]{:S(2)}) collective-permute-start(f32[192,256]{1,0:T(8,128)S(1)} %pad_maximum_fusion.1), channel_id=1, source_target_pairs={{0,1},{1,2},{2,3},{3,4},{4,5},{5,6},{6,7},{7,8},{8,9},{9,10},{10,1... | collective-permute-start | bytes 589832 | tf_op jit(solution)/shard_map/ppermute | solution.py:114
  160.1 12.8 %collective-permute-start.16 = (f32[192,256]{1,0:T(8,128)S(1)}, f32[192,256]{1,0:T(8,128)S(1)}, u32[]{:S(2)}, u32[]{:S(2)}) collective-permute-start(f32[192,256]{1,0:T(8,128)S(1)} %pad_maximum_fusion.1), channel_id=1, source_target_pairs={{0,2},{1,3},{2,4},{3,5},{4,6},{5,7},{6,8},{7,9},{8,10},{9,11},{10,... | collective-permute-start | bytes 589832 | tf_op jit(solution)/shard_map/ppermute | solution.py:114

commit v10 on v9

--- a/solution.py
+++ b/solution.py
@@ -74,7 +74,7 @@
 
 
 def dot_hi(a, b):
-    return jnp.dot(a, b, precision=lax.Precision.HIGHEST, preferred_element_type=jnp.float32)
+    return jnp.dot(a, b, precision=lax.Precision.HIGH, preferred_element_type=jnp.float32)
 
 
 def lower_inverse(lower):
@@ -203,7 +203,7 @@
         edges,
         projected,
         projected,
-        precision=lax.Precision.HIGHEST,
+        precision=lax.Precision.HIGH,
         preferred_element_type=jnp.float32,
     )
     head_in, tail_in = halo(
@@ -224,7 +224,7 @@
         own,
         projected,
         projected,
-        precision=lax.Precision.HIGHEST,
+        precision=lax.Precision.HIGH,
         preferred_element_type=jnp.float32,
     )
     gram = lax.optimization_barrier(gram)

time: 226 us -> 224 us (level)
  matrix products: 12.5 us -> 8.84 us
  transfers between devices with their start and end apart: 19 -> 19, of which waited for: 13 -> 13; matrix products, arithmetic and copies ran while one was open for 6% -> 5% of each run, Pallas kernels for 0% -> 0%
where the time goes in v10:
time: 224 us; the launch traced here: 221 us
  waiting for transfers between devices  68.6 us (31%)
  starting transfers between devices  67.5 us (30%)
  other arithmetic  59.1 us (26%)
  between operations  10.6 us (5%)
  matrix products  8.84 us (4%)
  local copies, waits for them, and re-layouts  6.23 us (3%)
    ppermute x8, starting transfers between devices, shift(): return lax.ppermute(x, axis, pairs)  27.6 us
    ppermute x4, starting transfers between devices, xor_allreduce(): x = x + lax.ppermute(x, axis, [(j, j ^ mask) for j in range(count)])  21.6 us
    another operation x4, other arithmetic, lower_inverse(): return jax.scipy.linalg.solve_triangular(lower, eye, lower=True)  20.9 us
    ppermute x3, waiting for transfers between devices, halving_allreduce(): x = keep + lax.ppermute(send, axis, pairs)  20.1 us
    ppermute x3, waiting for transfers between devices, halving_allreduce(): got = lax.ppermute(x, axis, pairs)  17.3 us
    ppermute x1, waiting for transfers between devices, halving_allreduce(): x = x + lax.ppermute(x, axis, pairs)  16.4 us
    another operation x3, other arithmetic, basis_rows(): l22 = jnp.linalg.cholesky(gram[half:, half:] - dot_hi(l21, l21.T))  12.6 us
    another operation x3, other arithmetic, basis_rows(): l11 = jnp.linalg.cholesky(gram[:half, :half])  12.4 us
  transfers between devices with their start and end apart: 19, of which 13 were waited for; matrix products, arithmetic and copies ran while one was open for 5% of the time, Pallas kernels for 0%

profile of v10, /device:TPU:6, one launch (start us, length us, event | category | flops | bytes accessed | tf_op | source)
XLA Modules:
  0.0 220.9 jit_solution(17473188683204920354)
XLA Ops:
  0.0 1.2 convert_reduce_fusion
  1.2 1.9 collective-permute-start
  3.2 0.7 multiply_bitcast_fusion
  4.2 0.7 multiply_subtract_fusion
  5.0 0.6 fusion.62
  5.6 0.5 broadcast_compare_fusion.1
  6.9 2.1 fusion.27
  9.1 4.3 %collective-permute-start.1 = (f32[2,2048]{1,0:T(2,128)S(1)}, f32[2,2048]{1,0:T(2,128)S(1)}, u32[]{:S(2)}, u32[]{:S(2)}) collective-permute-start(f32[2,2048]{1,0:T(2,128)S(1)} %fusion.61), channel_id=1, source_target_pairs={{0,64},{32,96},{64,0},{96,32},{128,192},{160,224},{192,128},{224,1... | collective-permute-start | bytes 49160 | tf_op jit(solution)/shard_map/ppermute | solution.py:30
  13.5 1.5 collective-permute-done.1
  15.1 6.1 %collective-permute-start.2 = (f32[2,2048]{1,0:T(2,128)S(1)}, f32[2,2048]{1,0:T(2,128)S(1)}, u32[]{:S(2)}, u32[]{:S(2)}) collective-permute-start(f32[2,2048]{1,0:T(2,128)S(1)} %fusion.75), channel_id=1, source_target_pairs={{0,128},{32,160},{64,192},{96,224},{128,0},{160,32},{192,64},{224,... | collective-permute-start | bytes 49160 | tf_op jit(solution)/shard_map/ppermute | solution.py:30
  21.2 1.7 collective-permute-done.2
  22.9 9.3 %collective-permute-start.3 = (f32[2,2048]{1,0:T(2,128)S(1)}, f32[2,2048]{1,0:T(2,128)S(1)}, u32[]{:S(2)}, u32[]{:S(2)}) collective-permute-start(f32[2,2048]{1,0:T(2,128)S(1)} %add.192), channel_id=1, source_target_pairs={{0,256},{32,288},{64,320},{96,352},{128,384},{160,416},{192,448},{... | collective-permute-start | bytes 49160 | tf_op jit(solution)/shard_map/ppermute | solution.py:30
  33.4 0.6 constant_dynamic-slice_fusion.1
  39.0 0.5 fusion.16
  39.6 3.5 %collective-permute-start.4 = (f32[64,256]{1,0:T(8,128)S(1)}, f32[64,256]{1,0:T(8,128)S(1)}, u32[]{:S(2)}, u32[]{:S(2)}) collective-permute-start(f32[64,256]{1,0:T(8,128)S(1)} %get-tuple-element.38), channel_id=1, source_target_pairs={{0,1},{1,2},{2,3},{3,4},{4,5},{5,6},{6,7},{7,8},{8,9},{9,10},{10,1... | collective-permute-start | bytes 196616 | tf_op jit(solution)/shard_map/ppermute | solution.py:114
  43.1 4.5 %collective-permute-start.5 = (f32[64,256]{1,0:T(8,128)S(1)}, f32[64,256]{1,0:T(8,128)S(1)}, u32[]{:S(2)}, u32[]{:S(2)}) collective-permute-start(f32[64,256]{1,0:T(8,128)S(1)} %get-tuple-element.38), channel_id=1, source_target_pairs={{0,2},{1,3},{2,4},{3,5},{4,6},{5,7},{6,8},{7,9},{8,10},{9,11},{10,... | collective-permute-start | bytes 196616 | tf_op jit(solution)/shard_map/ppermute | solution.py:114
  47.6 0.7 and_reduce_fusion
  48.3 4.5 %collective-permute-start.6 = (f32[64,256]{1,0:T(8,128)S(1)}, f32[64,256]{1,0:T(8,128)S(1)}, u32[]{:S(2)}, u32[]{:S(2)}) collective-permute-start(f32[64,256]{1,0:T(8,128)S(1)} %get-tuple-element.39), channel_id=1, source_target_pairs={{1,0},{2,1},{3,2},{4,3},{5,4},{6,5},{7,6},{8,7},{9,8},{10,9},{11,1... | collective-permute-start | bytes 196616 | tf_op jit(solution)/shard_map/ppermute | solution.py:114
  52.8 2.2 %collective-permute-start.7 = (f32[64,256]{1,0:T(8,128)S(1)}, f32[64,256]{1,0:T(8,128)S(1)}, u32[]{:S(2)}, u32[]{:S(2)}) collective-permute-start(f32[64,256]{1,0:T(8,128)S(1)} %get-tuple-element.39), channel_id=1, source_target_pairs={{2,0},{3,1},{4,2},{5,3},{6,4},{7,5},{8,6},{9,7},{10,8},{11,9},{12,... | collective-permute-start | bytes 196616 | tf_op jit(solution)/shard_map/ppermute | solution.py:114
  55.1 0.6 collective-permute-done.6
  55.7 4.6 %collective-permute-done.7 = f32[64,256]{1,0:T(8,128)S(1)} collective-permute-done((f32[64,256]{1,0:T(8,128)S(1)}, f32[64,256]{1,0:T(8,128)S(1)}, u32[]{:S(2)}, u32[]{:S(2)}) %collective-permute-start.7) | collective-permute-done | bytes 65568 | tf_op jit(solution)/shard_map/ppermute | solution.py:114
  60.2 0.6 fusion.42
  60.9 0.8 convolution_bitcast_fusion
  61.8 1.9 collective-permute-start.8
  63.7 2.7 %collective-permute-done.8 = f32[1024,256]{1,0:T(8,128)} collective-permute-done((f32[1024,256]{1,0:T(8,128)S(1)}, f32[1024,256]{1,0:T(8,128)}, u32[]{:S(2)}, u32[]{:S(2)}) %collective-permute-start.8) | collective-permute-done | bytes 1048608 | tf_op jit(solution)/shard_map/ppermute | solution.py:67
  66.4 1.4 select_add_fusion
  68.0 3.4 %collective-permute-start.9 = (f32[512,256]{1,0:T(8,128)S(1)}, f32[512,256]{1,0:T(8,128)S(1)}, u32[]{:S(2)}, u32[]{:S(2)}) collective-permute-start(f32[512,256]{1,0:T(8,128)S(1)} %slice_select_fusion.1), channel_id=1, source_target_pairs={{0,64},{32,480},{64,0},{96,160},{128,192},{160,96},{192,128},{224,... | collective-permute-start | bytes 1572872 | tf_op jit(solution)/shard_map/ppermute | solution.py:67
  71.4 7.7 %collective-permute-done.9 = f32[512,256]{1,0:T(8,128)S(1)} collective-permute-done((f32[512,256]{1,0:T(8,128)S(1)}, f32[512,256]{1,0:T(8,128)S(1)}, u32[]{:S(2)}, u32[]{:S(2)}) %collective-permute-start.9) | collective-permute-done | bytes 524320 | tf_op jit(solution)/shard_map/ppermute | solution.py:67
  79.2 4.3 %collective-permute-start.10 = (f32[256,256]{1,0:T(8,128)S(1)}, f32[256,256]{1,0:T(8,128)S(1)}, u32[]{:S(2)}, u32[]{:S(2)}) collective-permute-start(f32[256,256]{1,0:T(8,128)S(1)} %slice_select_fusion.2), channel_id=1, source_target_pairs={{0,128},{32,160},{64,192},{96,480},{128,0},{160,32},{192,64},{224,... | collective-permute-start | bytes 786440 | tf_op jit(solution)/shard_map/ppermute | solution.py:67
  83.5 9.7 %collective-permute-done.10 = f32[256,256]{1,0:T(8,128)S(1)} collective-permute-done((f32[256,256]{1,0:T(8,128)S(1)}, f32[256,256]{1,0:T(8,128)S(1)}, u32[]{:S(2)}, u32[]{:S(2)}) %collective-permute-start.10) | collective-permute-done | bytes 262176 | tf_op jit(solution)/shard_map/ppermute | solution.py:67
  93.3 2.7 %collective-permute-start.11 = (f32[256,256]{1,0:T(8,128)S(1)}, f32[256,256]{1,0:T(8,128)S(1)}, u32[]{:S(2)}, u32[]{:S(2)}) collective-permute-start(f32[256,256]{1,0:T(8,128)S(1)} %select_add_fusion.2), channel_id=1, source_target_pairs={{0,256},{32,288},{64,320},{96,352},{128,384},{160,416},{192,448},{... | collective-permute-start | bytes 786440 | tf_op jit(solution)/shard_map/ppermute | solution.py:69
  96.0 16.4 %collective-permute-done.11 = f32[256,256]{1,0:T(8,128)S(1)} collective-permute-done((f32[256,256]{1,0:T(8,128)S(1)}, f32[256,256]{1,0:T(8,128)S(1)}, u32[]{:S(2)}, u32[]{:S(2)}) %collective-permute-start.11) | collective-permute-done | bytes 262176 | tf_op jit(solution)/shard_map/ppermute | solution.py:69
  112.4 2.1 collective-permute-start.12
  114.5 10.9 %collective-permute-done.12 = f32[256,256]{1,0:T(8,128)S(1)} collective-permute-done((f32[256,256]{1,0:T(8,128)S(1)}, f32[256,256]{1,0:T(8,128)S(1)}, u32[]{:S(2)}, u32[]{:S(2)}) %collective-permute-start.12) | collective-permute-done | bytes 262176 | tf_op jit(solution)/shard_map/ppermute | solution.py:71
  125.4 1.9 collective-permute-start.13
  127.4 0.6 dynamic_slice.34
  130.5 0.6 dynamic_slice.35
  131.8 4.7 %collective-permute-done.13 = f32[512,256]{1,0:T(8,128)S(1)} collective-permute-done((f32[512,256]{1,0:T(8,128)S(1)}, f32[512,256]{1,0:T(8,128)S(1)}, u32[]{:S(2)}, u32[]{:S(2)}) %collective-permute-start.13) | collective-permute-done | bytes 524320 | tf_op jit(solution)/shard_map/ppermute | solution.py:71
  136.6 2.0 collective-permute-start.14
  138.7 0.7 compare_convert_fusion
  139.4 1.7 collective-permute-done.14
  141.2 2.0 fusion.11
  143.2 1.9 copy.26
  145.0 3.4 %fusion.20 = f32[2,256,256]{2,1,0:T(8,128)S(1)} fusion(f32[2048,256]{1,0:T(8,128)S(1)} %fusion.11, f32[2048,2]{0,1:T(2,128)S(1)} %fusion.55, f32[2048,256]{0,1:T(8,128)} %copy.26), kind=kOutput, calls=%fused_computation.24 | convolution fusion | flops 1611661312 | bytes 4734976 | tf_op jit(solution)/shard_map/mc,ck,cl->mkl/dot_general | solution.py:201
  148.7 4.1 %collective-permute-start.17 = (f32[192,256]{1,0:T(8,128)S(1)}, f32[192,256]{1,0:T(8,128)}, u32[]{:S(2)}, u32[]{:S(2)}) collective-permute-start(f32[192,256]{1,0:T(8,128)S(1)} %pad_maximum_fusion), channel_id=1, source_target_pairs={{1,0},{2,1},{3,2},{4,3},{5,4},{6,5},{7,6},{8,7},{9,8},{10,9},{11,1... | collective-permute-start | bytes 589832 | tf_op jit(solution)/shard_map/ppermute | solution.py:114
  152.8 2.0 collective-permute-start.18
  154.8 3.7 %collective-permute-start.15 = (f32[192,256]{1,0:T(8,128)S(1)}, f32[192,256]{1,0:T(8,128)S(1)}, u32[]{:S(2)}, u32[]{:S(2)}) collective-permute-start(f32[192,256]{1,0:T(8,128)S(1)} %pad_maximum_fusion.1), channel_id=1, source_target_pairs={{0,1},{1,2},{2,3},{3,4},{4,5},{5,6},{6,7},{7,8},{8,9},{9,10},{10,1... | collective-permute-start | bytes 589832 | tf_op jit(solution)/shard_map/ppermute | solution.py:114
  158.5 3.1 %collective-permute-start.16 = (f32[192,256]{1,0:T(8,128)S(1)}, f32[192,256]{1,0:T(8,128)S(1)}, u32[]{:S(2)}, u32[]{:S(2)}) collective-permute-start(f32[192,256]{1,0:T(8,128)S(1)} %pad_maximum_fusion.1), channel_id=1, source_target_pairs={{0,2},{1,3},{2,4},{3,5},{4,6},{5,7},{6,8},{7,9},{8,10},{9,11},{10,... | collective-permute-start | bytes 589832 | tf_op jit(solution)/shard_map/ppermute | solution.py:114
  161.6 2.1 fusion.2
  163.9 3.1 %collective-permute-done.18 = f32[192,256]{1,0:T(8,128)} collective-permute-done((f32[192,256]{1,0:T(8,128)S(1)}, f32[192,256]{1,0:T(8,128)}, u32[]{:S(2)}, u32[]{:S(2)}) %collective-permute-start.18) | collective-permute-done | bytes 196640 | tf_op jit(solution)/shard_map/ppermute | solution.py:114
  167.0 1.0 select_add_fusion.3
  168.1 3.3 %collective-permute-done.16 = f32[192,256]{1,0:T(8,128)S(1)} collective-permute-done((f32[192,256]{1,0:T(8,128)S(1)}, f32[192,256]{1,0:T(8,128)S(1)}, u32[]{:S(2)}, u32[]{:S(2)}) %collective-permute-start.16) | collective-permute-done | bytes 196640 | tf_op jit(solution)/shard_map/ppermute | solution.py:114
  172.0 11.7 %cholesky.44 = f32[128,128]{1,0:T(8,128)S(1)} custom-call(f32[128,128]{1,0:T(8,128)S(1)} %fusion.50), custom_call_target="Cholesky" | custom-call | tf_op jit(solution)/shard_map/jit(cholesky)/cholesky | solution.py:87
  183.7 0.6 compare_reduce_fusion.1
  184.4 0.7 fusion.40
  185.0 9.8 %custom-call.6 = f32[1,128,128]{1,2,0:T(8,128)S(1)} custom-call(f32[1,128,128]{2,1,0:T(8,128)S(1)} %fusion.40), custom_call_target="InvertDiagBlocksLowerTriangular" | custom-call | tf_op jit(solution)/shard_map/jit(_solve_triangular)/triangular_solve | solution.py:82
  194.9 0.3 fusion.38
  195.2 0.2 fusion.45
  196.2 11.9 %cholesky.55 = f32[128,128]{1,0:T(8,128)S(1)} custom-call(f32[128,128]{1,0:T(8,128)S(1)} %fusion.48), custom_call_target="Cholesky" | custom-call | tf_op jit(solution)/shard_map/jit(cholesky)/cholesky | solution.py:90
  208.1 0.6 compare_reduce_fusion
  208.7 0.7 fusion.41
  209.4 9.8 %custom-call.7 = f32[1,128,128]{1,2,0:T(8,128)S(1)} custom-call(f32[1,128,128]{2,1,0:T(8,128)S(1)} %fusion.41), custom_call_target="InvertDiagBlocksLowerTriangular" | custom-call | tf_op jit(solution)/shard_map/jit(_solve_triangular)/triangular_solve | solution.py:82
  219.2 0.3 fusion.36
  220.2 0.8 copy.35
  (85 shorter events, 4.1 us)
Async XLA Ops:
  0.0 38.9 %copy-start = (s32[64,2048]{1,0:T(8,128)S(1)}, s32[64,2048]{1,0:T(8,128)}, u32[]{:S(2)}) copy-start(s32[64,2048]{1,0:T(8,128)} %param.10) | copy-start | bytes 1572868
  1.2 7.8 %collective-permute-start = (f32[2,2048]{1,0:T(2,128)S(1)}, f32[2,2048]{1,0:T(2,128)S(1)}, u32[]{:S(2)}, u32[]{:S(2)}) collective-permute-start(f32[2,2048]{1,0:T(2,128)S(1)} %pad_maximum_fusion.3), channel_id=1, source_target_pairs={{0,32},{32,0},{64,96},{96,64},{128,160},{160,128},{192,224},{224,1... | collective-permute-start | bytes 49160 | tf_op jit(solution)/shard_map/ppermute | solution.py:30
  9.1 6.0 %collective-permute-start.1 = (f32[2,2048]{1,0:T(2,128)S(1)}, f32[2,2048]{1,0:T(2,128)S(1)}, u32[]{:S(2)}, u32[]{:S(2)}) collective-permute-start(f32[2,2048]{1,0:T(2,128)S(1)} %fusion.61), channel_id=1, source_target_pairs={{0,64},{32,96},{64,0},{96,32},{128,192},{160,224},{192,128},{224,1... | collective-permute-start | bytes 49160 | tf_op jit(solution)/shard_map/ppermute | solution.py:30
  15.1 7.8 %collective-permute-start.2 = (f32[2,2048]{1,0:T(2,128)S(1)}, f32[2,2048]{1,0:T(2,128)S(1)}, u32[]{:S(2)}, u32[]{:S(2)}) collective-permute-start(f32[2,2048]{1,0:T(2,128)S(1)} %fusion.75), channel_id=1, source_target_pairs={{0,128},{32,160},{64,192},{96,224},{128,0},{160,32},{192,64},{224,... | collective-permute-start | bytes 49160 | tf_op jit(solution)/shard_map/ppermute | solution.py:30
  22.9 16.0 %collective-permute-start.3 = (f32[2,2048]{1,0:T(2,128)S(1)}, f32[2,2048]{1,0:T(2,128)S(1)}, u32[]{:S(2)}, u32[]{:S(2)}) collective-permute-start(f32[2,2048]{1,0:T(2,128)S(1)} %add.192), channel_id=1, source_target_pairs={{0,256},{32,288},{64,320},{96,352},{128,384},{160,416},{192,448},{... | collective-permute-start | bytes 49160 | tf_op jit(solution)/shard_map/ppermute | solution.py:30
  39.0 8.6 %copy-start.1 = (s32[3]{0:T(128)S(1)}, s32[3]{0:T(128)}, u32[]{:S(2)}) copy-start(s32[3]{0:T(128)} %constant.186.clone.1) | copy-start | bytes 40
  39.6 15.4 %collective-permute-start.4 = (f32[64,256]{1,0:T(8,128)S(1)}, f32[64,256]{1,0:T(8,128)S(1)}, u32[]{:S(2)}, u32[]{:S(2)}) collective-permute-start(f32[64,256]{1,0:T(8,128)S(1)} %get-tuple-element.38), channel_id=1, source_target_pairs={{0,1},{1,2},{2,3},{3,4},{4,5},{5,6},{6,7},{7,8},{8,9},{9,10},{10,1... | collective-permute-start | bytes 196616 | tf_op jit(solution)/shard_map/ppermute | solution.py:114
  43.1 12.0 %collective-permute-start.5 = (f32[64,256]{1,0:T(8,128)S(1)}, f32[64,256]{1,0:T(8,128)S(1)}, u32[]{:S(2)}, u32[]{:S(2)}) collective-permute-start(f32[64,256]{1,0:T(8,128)S(1)} %get-tuple-element.38), channel_id=1, source_target_pairs={{0,2},{1,3},{2,4},{3,5},{4,6},{5,7},{6,8},{7,9},{8,10},{9,11},{10,... | collective-permute-start | bytes 196616 | tf_op jit(solution)/shard_map/ppermute | solution.py:114
  48.3 7.4 %collective-permute-start.6 = (f32[64,256]{1,0:T(8,128)S(1)}, f32[64,256]{1,0:T(8,128)S(1)}, u32[]{:S(2)}, u32[]{:S(2)}) collective-permute-start(f32[64,256]{1,0:T(8,128)S(1)} %get-tuple-element.39), channel_id=1, source_target_pairs={{1,0},{2,1},{3,2},{4,3},{5,4},{6,5},{7,6},{8,7},{9,8},{10,9},{11,1... | collective-permute-start | bytes 196616 | tf_op jit(solution)/shard_map/ppermute | solution.py:114
  52.8 7.4 %collective-permute-start.7 = (f32[64,256]{1,0:T(8,128)S(1)}, f32[64,256]{1,0:T(8,128)S(1)}, u32[]{:S(2)}, u32[]{:S(2)}) collective-permute-start(f32[64,256]{1,0:T(8,128)S(1)} %get-tuple-element.39), channel_id=1, source_target_pairs={{2,0},{3,1},{4,2},{5,3},{6,4},{7,5},{8,6},{9,7},{10,8},{11,9},{12,... | collective-permute-start | bytes 196616 | tf_op jit(solution)/shard_map/ppermute | solution.py:114
  61.8 4.7 %collective-permute-start.8 = (f32[1024,256]{1,0:T(8,128)S(1)}, f32[1024,256]{1,0:T(8,128)}, u32[]{:S(2)}, u32[]{:S(2)}) collective-permute-start(f32[1024,256]{1,0:T(8,128)S(1)} %slice_select_fusion), channel_id=1, source_target_pairs={{0,32},{32,0},{64,96},{96,64},{128,160},{160,128},{192,224},{224,1... | collective-permute-start | bytes 3145736 | tf_op jit(solution)/shard_map/ppermute | solution.py:67
  68.0 11.1 %collective-permute-start.9 = (f32[512,256]{1,0:T(8,128)S(1)}, f32[512,256]{1,0:T(8,128)S(1)}, u32[]{:S(2)}, u32[]{:S(2)}) collective-permute-start(f32[512,256]{1,0:T(8,128)S(1)} %slice_select_fusion.1), channel_id=1, source_target_pairs={{0,64},{32,480},{64,0},{96,160},{128,192},{160,96},{192,128},{224,... | collective-permute-start | bytes 1572872 | tf_op jit(solution)/shard_map/ppermute | solution.py:67
  79.1 51.3 %copy-start.2 = (s32[64]{0:T(128)S(1)}, s32[64]{0:T(128)}, u32[]{:S(2)}) copy-start(s32[64]{0:T(128)} %param.11) | copy-start | bytes 772
  79.2 14.1 %collective-permute-start.10 = (f32[256,256]{1,0:T(8,128)S(1)}, f32[256,256]{1,0:T(8,128)S(1)}, u32[]{:S(2)}, u32[]{:S(2)}) collective-permute-start(f32[256,256]{1,0:T(8,128)S(1)} %slice_select_fusion.2), channel_id=1, source_target_pairs={{0,128},{32,160},{64,192},{96,480},{128,0},{160,32},{192,64},{224,... | collective-permute-start | bytes 786440 | tf_op jit(solution)/shard_map/ppermute | solution.py:67
  93.3 19.1 %collective-permute-start.11 = (f32[256,256]{1,0:T(8,128)S(1)}, f32[256,256]{1,0:T(8,128)S(1)}, u32[]{:S(2)}, u32[]{:S(2)}) collective-permute-start(f32[256,256]{1,0:T(8,128)S(1)} %select_add_fusion.2), channel_id=1, source_target_pairs={{0,256},{32,288},{64,320},{96,352},{128,384},{160,416},{192,448},{... | collective-permute-start | bytes 786440 | tf_op jit(solution)/shard_map/ppermute | solution.py:69
  112.4 13.0 %collective-permute-start.12 = (f32[256,256]{1,0:T(8,128)S(1)}, f32[256,256]{1,0:T(8,128)S(1)}, u32[]{:S(2)}, u32[]{:S(2)}) collective-permute-start(f32[256,256]{1,0:T(8,128)S(1)} %add.211), channel_id=1, source_target_pairs={{0,128},{32,160},{64,192},{96,480},{128,0},{160,32},{192,64},{224,... | collective-permute-start | bytes 786440 | tf_op jit(solution)/shard_map/ppermute | solution.py:71
  125.4 11.1 %collective-permute-start.13 = (f32[512,256]{1,0:T(8,128)S(1)}, f32[512,256]{1,0:T(8,128)S(1)}, u32[]{:S(2)}, u32[]{:S(2)}) collective-permute-start(f32[512,256]{1,0:T(8,128)S(1)} %maximum_select_fusion.2), channel_id=1, source_target_pairs={{0,64},{32,480},{64,0},{96,160},{128,192},{160,96},{192,128},{224,... | collective-permute-start | bytes 1572872 | tf_op jit(solution)/shard_map/ppermute | solution.py:71
  136.6 4.6 %collective-permute-start.14 = (f32[1024,256]{1,0:T(8,128)S(1)}, f32[1024,256]{1,0:T(8,128)S(1)}, u32[]{:S(2)}, u32[]{:S(2)}) collective-permute-start(f32[1024,256]{1,0:T(8,128)S(1)} %maximum_select_fusion.1), channel_id=1, source_target_pairs={{0,32},{32,0},{64,96},{96,64},{128,160},{160,128},{192,224},{224,1... | collective-permute-start | bytes 3145736 | tf_op jit(solution)/shard_map/ppermute | solution.py:71
  148.7 15.2 %collective-permute-start.17 = (f32[192,256]{1,0:T(8,128)S(1)}, f32[192,256]{1,0:T(8,128)}, u32[]{:S(2)}, u32[]{:S(2)}) collective-permute-start(f32[192,256]{1,0:T(8,128)S(1)} %pad_maximum_fusion), channel_id=1, source_target_pairs={{1,0},{2,1},{3,2},{4,3},{5,4},{6,5},{7,6},{8,7},{9,8},{10,9},{11,1... | collective-permute-start | bytes 589832 | tf_op jit(solution)/shard_map/ppermute | solution.py:114
  152.8 14.3 %collective-permute-start.18 = (f32[192,256]{1,0:T(8,128)S(1)}, f32[192,256]{1,0:T(8,128)}, u32[]{:S(2)}, u32[]{:S(2)}) collective-permute-start(f32[192,256]{1,0:T(8,128)S(1)} %pad_maximum_fusion), channel_id=1, source_target_pairs={{2,0},{3,1},{4,2},{5,3},{6,4},{7,5},{8,6},{9,7},{10,8},{11,9},{12,... | collective-permute-start | bytes 589832 | tf_op jit(solution)/shard_map/ppermute | solution.py:114
  154.8 13.3 %collective-permute-start.15 = (f32[192,256]{1,0:T(8,128)S(1)}, f32[192,256]{1,0:T(8,128)S(1)}, u32[]{:S(2)}, u32[]{:S(2)}) collective-permute-start(f32[192,256]{1,0:T(8,128)S(1)} %pad_maximum_fusion.1), channel_id=1, source_target_pairs={{0,1},{1,2},{2,3},{3,4},{4,5},{5,6},{6,7},{7,8},{8,9},{9,10},{10,1... | collective-permute-start | bytes 589832 | tf_op jit(solution)/shard_map/ppermute | solution.py:114
  158.5 12.8 %collective-permute-start.16 = (f32[192,256]{1,0:T(8,128)S(1)}, f32[192,256]{1,0:T(8,128)S(1)}, u32[]{:S(2)}, u32[]{:S(2)}) collective-permute-start(f32[192,256]{1,0:T(8,128)S(1)} %pad_maximum_fusion.1), channel_id=1, source_target_pairs={{0,2},{1,3},{2,4},{3,5},{4,6},{5,7},{6,8},{7,9},{8,10},{9,11},{10,... | collective-permute-start | bytes 589832 | tf_op jit(solution)/shard_map/ppermute | solution.py:114
